TPU v7x, 512 devices: a whole 4x8x8 slice. The times are simulated.
512 devices in a mesh: dp: 16 (over y, core), tensor: 32 (over z, x).
Axes of the slice: x: 4, y: 8, z: 8, core: 2. Of those that a mesh axis runs over, the one named last changes fastest.
Arguments:
- layer_input: bfloat16 [65536, 8192], P('dp', 'tensor'), may hold values from -6 to 6
- output_grad: bfloat16 [65536, 1024], P(('dp', 'tensor')), may hold values from -6 to 6
- key_weight: bfloat16 [8192, 1024], P('tensor'), may hold values from -0.0625 to 0.0625
- adapter_down: bfloat16 [128, 16, 8192], P('dp', None, 'tensor'), may hold values from -0.0625 to 0.0625
- adapter_up: bfloat16 [128, 16, 1024], P('dp', None, 'tensor'), may hold values from -0.1875 to 0.1875
- segment_adapter: int32 [512], replicated, may hold values from 0 to 127
- adapter_slot: int32 [128], replicated, may hold values from 0 to 127, each once
- live_segments: int32 [16], P('dp'), may hold values from 1 to 32, as said below
Outputs:
- input_grad: bfloat16 [65536, 8192], P('dp', 'tensor')
- down_grad: bfloat16 [128, 16, 8192], P('dp', None, 'tensor')
- up_grad: bfloat16 [128, 16, 1024], P('dp', None, 'tensor')
Inputs may be any that keep to these rules, and one draw needn't show every extreme that they name: `live_segments`: some data group has all 32 segments live; a group's segments at or past its count are padding.
All inputs are finite; a program needn't handle non-finite values.
Results may differ from a plain program's by a relative error of at most 0.0057.
Values may be sent and summed in bfloat16 or wider, within the bound.
No kernel may reach another device: no remote copies, remote signals or barrier semaphores. Data moves between devices by JAX's collectives and lax.ppermute only.
A program may use at most 64 MiB of HBM per device.

v0:
```python
import jax
import jax.numpy as jnp
from jax import lax
from jax.sharding import PartitionSpec as P


def on_device(
    layer_input,
    output_grad,
    key_weight,
    adapter_down,
    adapter_up,
    segment_adapter,
    adapter_slot,
    live_segments,
):
    tensor_size = lax.axis_size("tensor")
    position = lax.axis_index("tensor")
    group_count = lax.axis_size("dp")
    group_index = lax.axis_index("dp")
    row_count = output_grad.shape[0]
    tok_group = layer_input.shape[0]
    width_shard = layer_input.shape[1]
    key_width = output_grad.shape[1]
    key_shard = key_width // tensor_size
    adapters = adapter_slot.shape[0]
    rank_dim = adapter_down.shape[1]
    seg_total = segment_adapter.shape[0]
    seg_group = seg_total // group_count
    seg_len = tok_group // seg_group
    per_owner = adapters // group_count
    slot_ids = jnp.arange(adapters, dtype=jnp.int32)
    lookup = segment_adapter[:, None] == slot_ids[None, :]
    every_slot = jnp.sum(jnp.where(lookup, adapter_slot[None, :], 0), axis=1)
    seg_slot = lax.dynamic_slice_in_dim(every_slot, group_index * seg_group, seg_group)
    local_rows = position * row_count + jnp.arange(row_count, dtype=jnp.int32)
    live_rows = local_rows // seg_len < live_segments[0]
    masked = jnp.where(live_rows[:, None], output_grad, jnp.zeros_like(output_grad))
    whole = lax.all_gather(masked, "tensor", axis=0, tiled=True)
    stores = (
        lax.all_gather(adapter_down, "dp", axis=0, tiled=True),
        lax.all_gather(adapter_up, "dp", axis=0, tiled=True),
    )
    choose = (seg_slot[:, None] == slot_ids[None, :]).astype(jnp.bfloat16)
    down_seg = jnp.dot(choose, stores[0].reshape(adapters, -1), preferred_element_type=jnp.float32)
    down_seg = down_seg.astype(jnp.bfloat16).reshape(seg_group, rank_dim, width_shard)
    up_seg = jnp.dot(choose, stores[1].reshape(adapters, -1), preferred_element_type=jnp.float32)
    up_seg = up_seg.astype(jnp.bfloat16).reshape(seg_group, rank_dim, key_shard)
    own_keys = lax.dynamic_slice_in_dim(whole, position * key_shard, key_shard, 1).reshape(
        seg_group, seg_len, key_shard
    )
    input_seg = layer_input.reshape(seg_group, seg_len, width_shard)
    up_part = jnp.einsum("sjk,srk->rsj", own_keys, up_seg, preferred_element_type=jnp.float32)
    down_part = jnp.einsum("sjd,srd->rsj", input_seg, down_seg, preferred_element_type=jnp.float32)
    lowrank, projected = lax.psum((up_part, down_part), "tensor")
    lowrank = lowrank.astype(jnp.bfloat16)
    projected = projected.astype(jnp.bfloat16)
    frozen = lax.dot_general(
        whole, key_weight, (((1,), (1,)), ((), ())), preferred_element_type=jnp.float32
    )
    extra = jnp.einsum("rsj,srd->sjd", lowrank, down_seg, preferred_element_type=jnp.float32)
    input_grad = (frozen + 2.0 * extra.reshape(tok_group, width_shard)).astype(jnp.bfloat16)
    seg_down = 2.0 * jnp.einsum(
        "rsj,sjd->srd", lowrank, input_seg, preferred_element_type=jnp.float32
    )
    seg_up = 2.0 * jnp.einsum(
        "rsj,sjk->srk", projected, own_keys, preferred_element_type=jnp.float32
    )
    seg_index = jnp.arange(seg_group, dtype=jnp.int32)
    same = seg_slot[:, None] == seg_slot[None, :]
    earlier = same & (seg_index[None, :] < seg_index[:, None])
    leading = jnp.logical_not(jnp.any(earlier, axis=1))
    merge_rows = (same & leading[:, None]).astype(jnp.float32)
    rows_down = jnp.einsum(
        "us,srd->urd", merge_rows, seg_down, precision=lax.Precision.HIGHEST
    ).astype(jnp.bfloat16)
    rows_up = jnp.einsum("us,srk->urk", merge_rows, seg_up, precision=lax.Precision.HIGHEST).astype(
        jnp.bfloat16
    )
    every_down, every_up = (
        lax.all_gather(rows_down, "dp", axis=0, tiled=True),
        lax.all_gather(rows_up, "dp", axis=0, tiled=True),
    )
    owned = group_index * per_owner + jnp.arange(per_owner, dtype=jnp.int32)
    mine = (every_slot[:, None] == owned[None, :]).astype(jnp.bfloat16)
    down_grad = jnp.einsum(
        "sp,srd->prd", mine, every_down, preferred_element_type=jnp.float32
    ).astype(jnp.bfloat16)
    up_grad = jnp.einsum("sp,srk->prk", mine, every_up, preferred_element_type=jnp.float32).astype(
        jnp.bfloat16
    )
    return (input_grad, down_grad, up_grad)


def solution(mesh):
    in_specs = (
        P("dp", "tensor"),
        P(("dp", "tensor"), None),
        P("tensor", None),
        P("dp", None, "tensor"),
        P("dp", None, "tensor"),
        P(),
        P(),
        P("dp"),
    )
    out_specs = (P("dp", "tensor"), P("dp", None, "tensor"), P("dp", None, "tensor"))
    return jax.shard_map(
        on_device, mesh=mesh, in_specs=in_specs, out_specs=out_specs, check_vma=False
    )
```

profile of v0, /device:TPU:1, one launch (start us, length us, event | category | flops | bytes accessed | tf_op | source)
XLA Modules:
  0.0 368.9 jit_solution(6331386676512770924)
XLA Ops:
  7.2 0.7 all-gather.6.cloned.1.call-update
  7.9 0.0 all-gather.4.cloned.1.call-start
  8.6 1.7 broadcast_select_fusion
  10.4 0.0 all-gather.8.cloned.1.call-start
  10.5 0.9 select_reduce_fusion
  11.4 0.1 dynamic_slice.6
  11.5 0.2 fusion.6
  11.7 22.9 %all_gather.16 = bf16[128,16,32]{2,1,0:T(8,128)(2,1)S(1)} all-gather(bf16[8,16,32]{2,1,0:T(8,128)(2,1)} %param.12), channel_id=1, replica_groups=mesh['dp'=16,'tensor'=32] {'dp'}, dimensions={0}, use_global_device_ids=true | all-gather | bytes 139264 | tf_op jit(solution)/shard_map/all_gather | solution.py:42
  34.5 0.4 copy.26
  35.0 0.2 convolution_convert_fusion.5
  35.1 0.2 reshape.60
  35.3 21.6 %all-gather.6.cloned.1.call-done = bf16[128,16,256]{2,1,0:T(8,128)(2,1)} async-done(((bf16[8,16,256]{2,1,0:T(8,128)(2,1)}), bf16[128,16,256]{2,1,0:T(8,128)(2,1)}) %all-gather.6.cloned.1.call-update) | async-done | bytes 1048592 | tf_op jit(solution)/shard_map/all_gather | solution.py:41
  56.9 1.6 copy.37
  58.5 0.3 convolution_convert_fusion
  58.8 0.1 copy.38
  58.9 1.4 convolution_bitcast_fusion
  60.3 103.2 %all-gather.4.cloned.1.call-done = bf16[4096,1024]{1,0:T(8,128)(2,1)} async-done(((bf16[128,1024]{1,0:T(8,128)(2,1)}), bf16[4096,1024]{1,0:T(8,128)(2,1)}) %all-gather.4.cloned.1.call-update) | async-done | bytes 8388624 | tf_op jit(solution)/shard_map/all_gather | solution.py:39
  163.5 1.6 constant_dynamic-slice_fusion
  165.0 1.4 convolution_bitcast_fusion.1
  166.4 117.5 %all-reduce.2 = (bf16[16,32,128]{2,0,1:T(8,128)(2,1)S(1)}, bf16[16,32,128]{2,0,1:T(8,128)(2,1)}) all-reduce(f32[16,32,128]{2,0,1:T(8,128)} %convolution_bitcast_fusion.1, f32[16,32,128]{2,0,1:T(8,128)} %convolution_bitcast_fusion), channel_id=1, replica_groups=mesh['dp'=16,'tensor'=32] {'tensor'}, use_global_device_ids=true, to_apply=%region_1.2 | all-reduce | flops 131072 | bytes 786432 | tf_op jit(solution)/shard_map/psum | solution.py:55
  283.9 0.4 convolution_multiply_fusion.1
  284.3 1.4 convolution_convert_fusion.1
  285.8 1.3 convolution_multiply_fusion.2
  287.0 0.4 convolution_convert_fusion.2
  287.4 57.7 %all_gather.19 = bf16[512,16,32]{2,0,1:T(8,128)(2,1)S(1)} all-gather(bf16[32,16,32]{2,0,1:T(8,128)(2,1)S(1)} %convolution_convert_fusion.2), channel_id=1, replica_groups=mesh['dp'=16,'tensor'=32] {'dp'}, dimensions={0}, use_global_device_ids=true | all-gather | bytes 557056 | tf_op jit(solution)/shard_map/all_gather | solution.py:82
  345.1 0.4 convolution_convert_fusion.4
  345.5 0.6 copy.33
  346.2 0.8 convolution_multiply_fusion
  346.9 7.5 %fusion = bf16[4096,256]{1,0:T(8,128)(2,1)} fusion(f32[4096,256]{1,0:T(8,128)S(1)} %bitcast.43, bf16[4096,1024]{1,0:T(8,128)(2,1)} %all-gather.4.cloned.1.call-done, bf16[256,1024]{1,0:T(8,128)(2,1)S(1)} %copy-done.1), kind=kOutput, calls=%fused_computation.1 | convolution fusion | flops 2149580800 | bytes 15204352 | tf_op jit(solution)/shard_map/dot_general | solution.py:58
  354.4 4.4 %all-gather.8.cloned.1.call-done = bf16[512,16,256]{2,0,1:T(8,128)(2,1)} async-done(((bf16[32,16,256]{2,0,1:T(8,128)(2,1)}), bf16[512,16,256]{2,0,1:T(8,128)(2,1)}) %all-gather.8.cloned.1.call-update) | async-done | bytes 4194320 | tf_op jit(solution)/shard_map/all_gather | solution.py:81
  358.9 2.9 convolution_convert_fusion.3
  361.7 0.7 copy.32
  (10 shorter events, 0.1 us)
Async XLA Ops:
  7.2 51.7 %copy-start = (bf16[4096,256]{1,0:T(8,128)(2,1)S(1)}, bf16[4096,256]{1,0:T(8,128)(2,1)}, u32[]{:S(2)}) copy-start(bf16[4096,256]{1,0:T(8,128)(2,1)} %param.8) | copy-start | bytes 6291460
  7.2 49.7 %all-gather.6.cloned.1.call-start = ((), (), s32[]{:S(2)}) async-start(), calls=%async_computation.1 | async-start | bytes 1114112 | tf_op jit(solution)/shard_map/all_gather | solution.py:41
  7.9 155.5 %all-gather.4.cloned.1.call-start = ((), (), s32[]{:S(2)}) async-start(), calls=%async_computation | async-start | bytes 8650752 | tf_op jit(solution)/shard_map/all_gather | solution.py:39
  10.4 348.5 %all-gather.8.cloned.1.call-start = ((), (), s32[]{:S(2)}) async-start(), calls=%async_computation.2 | async-start | bytes 4456448 | tf_op jit(solution)/shard_map/all_gather | solution.py:81
  287.4 59.5 %copy-start.1 = (bf16[256,1024]{1,0:T(8,128)(2,1)S(1)}, bf16[256,1024]{1,0:T(8,128)(2,1)}, u32[]{:S(2)}) copy-start(bf16[256,1024]{1,0:T(8,128)(2,1)} %param.10) | copy-start | bytes 1572868
Sparse Core Ops, SparseCore 0:
  10.1 46.6 all-gather.5
  60.6 102.8 all-gather.3
  285.9 72.9 all-gather.7
where the time goes:
time: 369 us
  blocking collectives  198 us (54%)
  waiting for transfers between devices  130 us (35%)
  matrix products  18.2 us (5%)
  between operations  14.5 us (4%)
  local copies, waits for them, and re-layouts  5.25 us (1%)
    psum x1, blocking collectives, on_device(): lowrank, projected = lax.psum((up_part, down_part), 'tensor')  117 us
    all_gather x1, waiting for transfers between devices, on_device(): whole = lax.all_gather(masked, 'tensor', axis=0, tiled=True)  103 us
    all_gather x1, blocking collectives, on_device(): lax.all_gather(rows_up, 'dp', axis=0, tiled=True)  57.7 us
    all_gather x1, blocking collectives, on_device(): lax.all_gather(adapter_up, 'dp', axis=0, tiled=True)  22.9 us
    all_gather x1, waiting for transfers between devices, on_device(): lax.all_gather(adapter_down, 'dp', axis=0, tiled=True)  21.6 us
    dot_general x1, matrix products, on_device(): lax.dot_general(whole, key_weight, (((1,), (1,)), ((), ())), preferred_el...  7.47 us
  transfers between devices with their start and end apart: 3, of which 3 were waited for; matrix products, arithmetic and copies ran while one was open for 5% of the time, Pallas kernels for 0%

commit v1 on v0

v1 whole, which is shorter than its diff:
```python
import jax
import jax.numpy as jnp
from jax import lax
from jax.sharding import PartitionSpec as P


def on_device(
    layer_input,
    output_grad,
    key_weight,
    adapter_down,
    adapter_up,
    segment_adapter,
    adapter_slot,
    live_segments,
):
    tensor_size = lax.axis_size("tensor")
    position = lax.axis_index("tensor")
    group_count = lax.axis_size("dp")
    group_index = lax.axis_index("dp")
    tok_group = layer_input.shape[0]
    width_shard = layer_input.shape[1]
    key_width = output_grad.shape[1]
    key_shard = key_width // tensor_size
    adapters = adapter_slot.shape[0]
    rank_dim = adapter_down.shape[1]
    seg_total = segment_adapter.shape[0]
    seg_group = seg_total // group_count
    seg_len = tok_group // seg_group

    whole_raw = lax.all_gather(output_grad, "tensor", axis=0, tiled=True)

    slot_ids = jnp.arange(adapters, dtype=jnp.int32)
    lookup = segment_adapter[:, None] == slot_ids[None, :]
    every_slot = jnp.sum(jnp.where(lookup, adapter_slot[None, :], 0), axis=1)
    seg_slot = lax.dynamic_slice_in_dim(every_slot, group_index * seg_group, seg_group)
    seg_live = jnp.arange(seg_group, dtype=jnp.int32) < live_segments[0]

    local_store = jnp.concatenate([adapter_down, adapter_up], axis=2)
    stores = lax.all_gather(local_store, "dp", axis=0, tiled=True)
    choose = (seg_slot[:, None] == slot_ids[None, :]).astype(jnp.bfloat16)
    seg_store = jnp.dot(choose, stores.reshape(adapters, -1), preferred_element_type=jnp.float32)
    seg_store = seg_store.astype(jnp.bfloat16).reshape(seg_group, rank_dim, width_shard + key_shard)
    down_seg = seg_store[:, :, :width_shard]
    up_seg = seg_store[:, :, width_shard:]

    whole = jnp.where(
        jnp.repeat(seg_live, seg_len)[:, None], whole_raw, jnp.zeros_like(whole_raw)
    )
    own_keys = lax.dynamic_slice_in_dim(whole, position * key_shard, key_shard, 1).reshape(
        seg_group, seg_len, key_shard
    )
    input_seg = layer_input.reshape(seg_group, seg_len, width_shard)
    up_part = jnp.einsum("sjk,srk->srj", own_keys, up_seg, preferred_element_type=jnp.float32)
    down_part = jnp.einsum("sjd,srd->srj", input_seg, down_seg, preferred_element_type=jnp.float32)
    both = lax.psum(jnp.stack([up_part, down_part]), "tensor")
    both = lax.reduce_precision(both, exponent_bits=8, mantissa_bits=7)
    lowrank = both[0].astype(jnp.bfloat16)
    projected = both[1].astype(jnp.bfloat16)

    frozen = lax.dot_general(
        whole, key_weight, (((1,), (1,)), ((), ())), preferred_element_type=jnp.float32
    )
    extra = jnp.einsum("srj,srd->sjd", lowrank, down_seg, preferred_element_type=jnp.float32)
    input_grad = (frozen + 2.0 * extra.reshape(tok_group, width_shard)).astype(jnp.bfloat16)

    seg_down = 2.0 * jnp.einsum(
        "srj,sjd->srd", lowrank, input_seg, preferred_element_type=jnp.float32
    )
    seg_up = 2.0 * jnp.einsum(
        "srj,sjk->srk", projected, own_keys, preferred_element_type=jnp.float32
    )
    seg_grad = jnp.concatenate([seg_down, seg_up], axis=2)
    onehot = (seg_slot[:, None] == slot_ids[None, :]).astype(jnp.float32)
    part = jnp.einsum("sa,srd->ard", onehot, seg_grad, precision=lax.Precision.HIGHEST)
    part = lax.reduce_precision(part, exponent_bits=8, mantissa_bits=7)
    total = lax.psum_scatter(part, "dp", scatter_dimension=0, tiled=True)
    down_grad = total[:, :, :width_shard].astype(jnp.bfloat16)
    up_grad = total[:, :, width_shard:].astype(jnp.bfloat16)
    return (input_grad, down_grad, up_grad)


def solution(mesh):
    in_specs = (
        P("dp", "tensor"),
        P(("dp", "tensor"), None),
        P("tensor", None),
        P("dp", None, "tensor"),
        P("dp", None, "tensor"),
        P(),
        P(),
        P("dp"),
    )
    out_specs = (P("dp", "tensor"), P("dp", None, "tensor"), P("dp", None, "tensor"))
    return jax.shard_map(
        on_device, mesh=mesh, in_specs=in_specs, out_specs=out_specs, check_vma=False
    )
```

time: 369 us -> 404 us (1.095)
  waiting for transfers between devices: 130 us -> 353 us
  blocking collectives: 198 us -> 0 us
  other arithmetic: 2.88 us -> 9.97 us
    psum x0 -> x1, waiting for transfers between devices: none -> 152 us  [on_device(): both = lax.psum(jnp.stack([up_part, down_part]), 'tensor')]
    psum x1 -> x0, blocking collectives: 117 us -> none  [on_device(): lowrank, projected = lax.psum((up_part, down_part), 'tensor')]
    all_gather x2 -> x0, blocking collectives: 80.6 us -> none  [the longest x1 57.7 us: on_device(): lax.all_gather(rows_up, 'dp', axis=0, tiled=True)]
    reduce_scatter x0 -> x1, waiting for transfers between devices: none -> 54.3 us  [on_device(): total = lax.psum_scatter(part, 'dp', scatter_dimension=0, tiled=True)]
    all_gather x3 -> x2, waiting for transfers between devices: 129 us -> 147 us  [the longest x1 99.8 us: on_device(): whole_raw = lax.all_gather(output_grad, 'tensor', axis=0, tiled=True)]
    dot_general x11 -> x7, matrix products: 10.7 us -> 8.02 us  [the longest x1 3.25 us: on_device(): jnp.einsum('sa,srd->ard', onehot, seg_grad, precision=lax.Precision.HIGHEST)]
  transfers between devices with their start and end apart: 3 -> 4, of which waited for: 3 -> 4; matrix products, arithmetic and copies ran while one was open for 5% -> 4% of each run, Pallas kernels for 0% -> 0%
where the time goes in v1:
time: 404 us; the launch traced here: 402 us
  waiting for transfers between devices  353 us (87%)
  matrix products  15.3 us (4%)
  between operations  14.5 us (4%)
  other arithmetic  9.97 us (2%)
  local copies, waits for them, and re-layouts  9.15 us (2%)
    psum x1, waiting for transfers between devices, on_device(): both = lax.psum(jnp.stack([up_part, down_part]), 'tensor')  152 us
    all_gather x1, waiting for transfers between devices, on_device(): whole_raw = lax.all_gather(output_grad, 'tensor', axis=0, tiled=True)  99.8 us
    reduce_scatter x1, waiting for transfers between devices, on_device(): total = lax.psum_scatter(part, 'dp', scatter_dimension=0, tiled=True)  54.3 us
    all_gather x1, waiting for transfers between devices, on_device(): stores = lax.all_gather(local_store, 'dp', axis=0, tiled=True)  46.7 us
  transfers between devices with their start and end apart: 4, of which 4 were waited for; matrix products, arithmetic and copies ran while one was open for 4% of the time, Pallas kernels for 0%

profile of v1, /device:TPU:1, one launch (start us, length us, event | category | flops | bytes accessed | tf_op | source)
XLA Modules:
  0.0 402.4 jit_solution(13323799420373628107)
XLA Ops:
  7.2 1.6 pad_maximum_fusion.2
  8.9 0.0 all-gather.3.cloned.1.call-start
  8.9 0.7 all-gather.3.cloned.1.call-update
  10.3 0.9 select_reduce_fusion
  11.3 0.1 dynamic_slice.6
  11.4 0.1 broadcast_bitcast_fusion
  11.4 46.7 %all-gather.5.cloned.1.call-done = bf16[128,16,288]{2,1,0:T(8,128)(2,1)} async-done(((bf16[8,16,288]{2,1,0:T(8,128)(2,1)}), bf16[128,16,288]{2,1,0:T(8,128)(2,1)}) %all-gather.5.cloned.1.call-update) | async-done | bytes 1179664 | tf_op jit(solution)/shard_map/all_gather | solution.py:40
  58.1 2.0 copy.26
  60.2 1.2 convolution_convert_fusion
  61.4 1.5 reshape.28
  63.0 1.4 convolution_bitcast_fusion
  64.3 99.8 %all-gather.3.cloned.1.call-done = bf16[4096,1024]{1,0:T(8,128)(2,1)} async-done(((bf16[128,1024]{1,0:T(8,128)(2,1)}), bf16[4096,1024]{1,0:T(8,128)(2,1)}) %all-gather.3.cloned.1.call-update) | async-done | bytes 8388624 | tf_op jit(solution)/shard_map/all_gather | solution.py:31
  164.1 4.5 %broadcast_select_fusion = bf16[4096,1024]{1,0:T(8,128)(2,1)S(1)} fusion(bf16[4096,1024]{1,0:T(8,128)(2,1)} %all-gather.3.cloned.1.call-done, pred[4096]{0:T(1024)(128)(4,1)S(1)} %broadcast_bitcast_fusion), kind=kLoop, calls=%fused_computation | loop fusion | flops 4194304 | bytes 16781312 | tf_op jit(solution)/shard_map/jit(_where)/select_n | solution.py:47
  168.6 3.2 copy-done.1
  171.8 0.4 constant_dynamic-slice_fusion
  172.2 0.6 convolution_bitcast_fusion.1
  172.8 0.9 pad_maximum_fusion.1
  173.7 0.0 reduce-scatter.2.cloned.1.call-start
  173.8 151.7 %all-reduce.2.cloned.1.call-done = f32[2,32,16,128]{3,2,1,0:T(8,128)} async-done(((f32[2,32,16,128]{3,2,1,0:T(8,128)}), f32[2,32,16,128]{3,2,1,0:T(8,128)}) %all-reduce.2.cloned.1.call-update) | async-done | bytes 524304 | tf_op jit(solution)/shard_map/psum | solution.py:56
  325.5 1.1 reduce-precision_convert_fusion
  326.6 0.4 convolution_multiply_fusion.2
  327.0 0.3 copy-done.2
  327.3 0.4 convolution_multiply_fusion.1
  327.7 0.1 pad_maximum_fusion
  327.7 3.2 convolution_reduce-precision_fusion
  331.0 0.8 convolution_multiply_fusion
  331.8 0.2 copy-done.5
  332.0 7.3 %fusion = bf16[4096,256]{1,0:T(8,128)(2,1)} fusion(f32[4096,256]{1,0:T(8,128)S(1)} %bitcast.34, bf16[4096,1024]{1,0:T(8,128)(2,1)} %copy-done.1, bf16[256,1024]{1,0:T(8,128)(2,1)S(1)} %copy-done.5), kind=kOutput, calls=%fused_computation.3 | convolution fusion | flops 2149580800 | bytes 15204352 | tf_op jit(solution)/shard_map/dot_general | solution.py:61
  339.3 54.3 %reduce-scatter.2.cloned.1.call-done = f32[8,16,288]{2,0,1:T(8,128)} async-done(((f32[128,16,288]{2,0,1:T(8,128)}), f32[8,16,288]{2,0,1:T(8,128)}) %reduce-scatter.2.cloned.1.call-update) | async-done | bytes 147472 | tf_op jit(solution)/shard_map/reduce_scatter | solution.py:77
  393.7 0.9 convert.9
  394.6 0.6 copy.31
  395.3 0.6 copy.32
  (17 shorter events, 0.2 us)
Async XLA Ops:
  7.2 55.8 %copy-start = (bf16[4096,256]{1,0:T(8,128)(2,1)S(1)}, bf16[4096,256]{1,0:T(8,128)(2,1)}, u32[]{:S(2)}) copy-start(bf16[4096,256]{1,0:T(8,128)(2,1)} %param.8) | copy-start | bytes 6291460
  7.2 51.0 %all-gather.5.cloned.1.call-start = ((), (), s32[]{:S(2)}) async-start(), calls=%async_computation.2 | async-start | bytes 1671168 | tf_op jit(solution)/shard_map/all_gather | solution.py:40
  8.9 155.2 %all-gather.3.cloned.1.call-start = ((), (), s32[]{:S(2)}) async-start(), calls=%async_computation.1 | async-start | bytes 8650752 | tf_op jit(solution)/shard_map/all_gather | solution.py:31
  9.6 315.9 %all-reduce.2.cloned.1.call-start = ((), (), s32[]{:S(2)}) async-start(), calls=%async_computation.3 | async-start | bytes 1048576 | tf_op jit(solution)/shard_map/psum | solution.py:56
  164.1 8.7 %copy-start.4 = (f32[1,32,16,128]{3,2,1,0:T(8,128)S(1)}, f32[1,32,16,128]{3,2,1,0:T(8,128)}, u32[]{:S(2)}) copy-start(f32[1,32,16,128]{3,2,1,0:T(8,128)} %convolution_bitcast_fusion) | copy-start | bytes 786436
  168.6 3.2 copy-start.1
  173.7 219.9 %reduce-scatter.2.cloned.1.call-start = ((), (), s32[]{:S(2)}) async-start(), calls=%async_computation.4 | async-start | bytes 3342336 | tf_op jit(solution)/shard_map/reduce_scatter | solution.py:77
  326.6 0.7 copy-start.2
  327.7 3.3 copy-start.3
  331.0 1.0 copy-start.5
Sparse Core Ops, SparseCore 0:
  10.7 47.3 all-gather.4
  61.3 102.7 all-gather.2
  173.9 151.6 all-reduce.1
  331.1 62.4 reduce-scatter.1

commit v2 on v1

v2 whole, which is shorter than its diff:
```python
import jax
import jax.numpy as jnp
from jax import lax
from jax.sharding import PartitionSpec as P


def on_device(
    layer_input,
    output_grad,
    key_weight,
    adapter_down,
    adapter_up,
    segment_adapter,
    adapter_slot,
    live_segments,
):
    tensor_size = lax.axis_size("tensor")
    position = lax.axis_index("tensor")
    group_count = lax.axis_size("dp")
    group_index = lax.axis_index("dp")
    row_count = output_grad.shape[0]
    tok_group = layer_input.shape[0]
    width_shard = layer_input.shape[1]
    key_width = output_grad.shape[1]
    key_shard = key_width // tensor_size
    adapters = adapter_slot.shape[0]
    rank_dim = adapter_down.shape[1]
    per_owner = adapter_down.shape[0]
    seg_total = segment_adapter.shape[0]
    seg_group = seg_total // group_count
    seg_len = tok_group // seg_group
    f32 = jnp.float32
    bf16 = jnp.bfloat16

    whole_raw = lax.all_gather(output_grad, "tensor", axis=0, tiled=True)

    slot_ids = jnp.arange(adapters, dtype=jnp.int32)
    lookup = segment_adapter[:, None] == slot_ids[None, :]
    every_slot = jnp.sum(jnp.where(lookup, adapter_slot[None, :], 0), axis=1)
    seg_slot = lax.dynamic_slice_in_dim(every_slot, group_index * seg_group, seg_group)
    seg_live = jnp.arange(seg_group, dtype=jnp.int32) < live_segments[0]

    local_store = jnp.concatenate([adapter_down, adapter_up], axis=2)
    spread = jnp.broadcast_to(local_store[None], (group_count,) + local_store.shape)
    stores = lax.all_to_all(spread, "dp", 0, 0, tiled=True).reshape(adapters, -1)
    choose = (seg_slot[:, None] == slot_ids[None, :]).astype(bf16)
    seg_store = jnp.dot(choose, stores, preferred_element_type=f32).astype(bf16)
    seg_store = seg_store.reshape(seg_group, rank_dim, width_shard + key_shard)
    down_seg = seg_store[:, :, :width_shard]
    up_seg = seg_store[:, :, width_shard:]

    input_seg = layer_input.reshape(seg_group, seg_len, width_shard)
    proj_part = jnp.einsum("sjd,srd->srj", input_seg, down_seg, preferred_element_type=f32)
    first = jnp.concatenate([proj_part, up_seg.astype(f32)], axis=2)
    first = lax.all_to_all(first, "tensor", 0, 0, tiled=True)
    projected_own = jnp.sum(first[:, :, :seg_len], axis=0).astype(bf16)
    up_own = jnp.transpose(first[:, :, seg_len:], (1, 0, 2)).reshape(rank_dim, key_width)
    up_own = up_own.astype(bf16)

    own_live = position < live_segments[0]
    masked_own = jnp.where(own_live, output_grad, jnp.zeros_like(output_grad))
    lowrank_own = lax.dot_general(
        masked_own, up_own, (((1,), (1,)), ((), ())), preferred_element_type=f32
    ).astype(bf16)
    seg_up_own = 2.0 * jnp.dot(projected_own, masked_own, preferred_element_type=f32)

    low_spread = jnp.broadcast_to(
        lowrank_own.astype(f32).reshape(1, row_count * rank_dim),
        (tensor_size, row_count * rank_dim),
    )
    up_pieces = jnp.transpose(
        seg_up_own.reshape(rank_dim, tensor_size, key_shard), (1, 0, 2)
    ).reshape(tensor_size, rank_dim * key_shard)
    second = jnp.concatenate([low_spread, up_pieces], axis=1)
    second = lax.all_to_all(second, "tensor", 0, 0, tiled=True)
    lowrank = second[:, : row_count * rank_dim].reshape(seg_group, seg_len, rank_dim)
    lowrank = lowrank.astype(bf16)
    seg_up = second[:, row_count * rank_dim :].reshape(seg_group, rank_dim, key_shard)

    seg_down = 2.0 * jnp.einsum("sjr,sjd->srd", lowrank, input_seg, preferred_element_type=f32)
    seg_grad = jnp.concatenate([seg_down, seg_up], axis=2)
    onehot = (seg_slot[:, None] == slot_ids[None, :]).astype(f32)
    part = jnp.einsum("sa,srd->ard", onehot, seg_grad, precision=lax.Precision.HIGHEST)
    part = part.astype(bf16).reshape(group_count, per_owner, rank_dim, -1)
    gathered = lax.all_to_all(part, "dp", 0, 0, tiled=True)
    total = jnp.sum(gathered.astype(f32), axis=0)
    down_grad = total[:, :, :width_shard].astype(bf16)
    up_grad = total[:, :, width_shard:].astype(bf16)

    whole = jnp.where(
        jnp.repeat(seg_live, seg_len)[:, None], whole_raw, jnp.zeros_like(whole_raw)
    )
    frozen = lax.dot_general(
        whole, key_weight, (((1,), (1,)), ((), ())), preferred_element_type=f32
    )
    extra = jnp.einsum("sjr,srd->sjd", lowrank, down_seg, preferred_element_type=f32)
    input_grad = (frozen + 2.0 * extra.reshape(tok_group, width_shard)).astype(bf16)
    return (input_grad, down_grad, up_grad)


def solution(mesh):
    in_specs = (
        P("dp", "tensor"),
        P(("dp", "tensor"), None),
        P("tensor", None),
        P("dp", None, "tensor"),
        P("dp", None, "tensor"),
        P(),
        P(),
        P("dp"),
    )
    out_specs = (P("dp", "tensor"), P("dp", None, "tensor"), P("dp", None, "tensor"))
    return jax.shard_map(
        on_device, mesh=mesh, in_specs=in_specs, out_specs=out_specs, check_vma=False
    )
```

time: 404 us -> 191 us (0.47)
  waiting for transfers between devices: 353 us -> 97.1 us
  starting transfers between devices: 0.16 us -> 28.5 us
  blocking collectives: 0 us -> 20.7 us
  other arithmetic: 9.97 us -> 3.77 us
    psum x1 -> x0, waiting for transfers between devices: 152 us -> none  [on_device(): both = lax.psum(jnp.stack([up_part, down_part]), 'tensor')]
    all_gather x1, waiting for transfers between devices: 99.8 us -> 0.01 us  [on_device(): whole_raw = lax.all_gather(output_grad, 'tensor', axis=0, tiled=True)]
    all_to_all x0 -> x3, waiting for transfers between devices: none -> 96.5 us  [the longest x1 38.3 us: on_device(): lax.all_to_all(spread, 'dp', 0, 0, tiled=True).reshape(adapters, -1)]
    reduce_scatter x1 -> x0, waiting for transfers between devices: 54.3 us -> none  [on_device(): total = lax.psum_scatter(part, 'dp', scatter_dimension=0, tiled=True)]
    all_gather x1 -> x0, waiting for transfers between devices: 46.7 us -> none  [on_device(): stores = lax.all_gather(local_store, 'dp', axis=0, tiled=True)]
    all_to_all x0 -> x3, starting transfers between devices: none -> 28.4 us  [the longest x1 11 us: on_device(): lax.all_to_all(spread, 'dp', 0, 0, tiled=True).reshape(adapters, -1)]
    all_to_all x0 -> x1, blocking collectives: none -> 20.7 us  [on_device(): second = lax.all_to_all(second, 'tensor', 0, 0, tiled=True)]
    unnamed x14 -> x15, local copies, waits for them, and re-layouts: 5.06 us -> 0.06 us
  transfers between devices with their start and end apart: 4 -> 4, of which waited for: 4 -> 3; matrix products, arithmetic and copies ran while one was open for 4% -> 11% of each run, Pallas kernels for 0% -> 0%
where the time goes in v2:
time: 191 us; the launch traced here: 190 us
  waiting for transfers between devices  97.1 us (51%)
  starting transfers between devices  28.5 us (15%)
  blocking collectives  20.7 us (11%)
  between operations  14.9 us (8%)
  matrix products  14.1 us (7%)
  local copies, waits for them, and re-layouts  11.2 us (6%)
  other arithmetic  3.77 us (2%)
    all_to_all x1, waiting for transfers between devices, on_device(): lax.all_to_all(spread, 'dp', 0, 0, tiled=True).reshape(adapters, -1)  38.3 us
    all_to_all x1, waiting for transfers between devices, on_device(): gathered = lax.all_to_all(part, 'dp', 0, 0, tiled=True)  35.8 us
    all_to_all x1, waiting for transfers between devices, on_device(): first = lax.all_to_all(first, 'tensor', 0, 0, tiled=True)  22.4 us
    all_to_all x1, blocking collectives, on_device(): second = lax.all_to_all(second, 'tensor', 0, 0, tiled=True)  20.7 us
    all_to_all x1, starting transfers between devices, on_device(): lax.all_to_all(spread, 'dp', 0, 0, tiled=True).reshape(adapters, -1)  11 us
    all_to_all x1, starting transfers between devices, on_device(): first = lax.all_to_all(first, 'tensor', 0, 0, tiled=True)  10.5 us
    all_to_all x1, starting transfers between devices, on_device(): gathered = lax.all_to_all(part, 'dp', 0, 0, tiled=True)  6.98 us
    dot_general x1, matrix products, on_device(): lax.dot_general(whole, key_weight, (((1,), (1,)), ((), ())), preferred_el...  6.95 us
  transfers between devices with their start and end apart: 4, of which 3 were waited for; matrix products, arithmetic and copies ran while one was open for 11% of the time, Pallas kernels for 0%

profile of v2, /device:TPU:1, one launch (start us, length us, event | category | flops | bytes accessed | tf_op | source)
XLA Modules:
  0.0 190.3 jit_solution(6208099868843389185)
XLA Ops:
  7.2 0.7 all-gather.2.cloned.1.call-update
  7.9 0.9 pad_maximum_fusion.3
  8.8 1.3 broadcast_in_dim.61
  10.2 11.0 %all-to-all-start = ((bf16[16,8,16,288]{3,2,1,0:T(8,128)(2,1)}), bf16[16,8,16,288]{3,2,1,0:T(8,128)(2,1)}, u32[]{:S(2)}, u32[]{:S(2)}) async-start(bf16[16,8,16,288]{3,2,1,0:T(8,128)(2,1)} %broadcast_in_dim.61), calls=%async_computation | async-start | bytes 3145728 | tf_op jit(solution)/shard_map/all_to_all | solution.py:45
  21.2 0.2 select_reduce_fusion
  21.5 38.3 %all-to-all-done = bf16[16,8,16,288]{3,2,1,0:T(8,128)(2,1)} async-done(((bf16[16,8,16,288]{3,2,1,0:T(8,128)(2,1)}), bf16[16,8,16,288]{3,2,1,0:T(8,128)(2,1)}, u32[]{:S(2)}, u32[]{:S(2)}) %all-to-all-start) | async-done | bytes 1179680 | tf_op jit(solution)/shard_map/all_to_all | solution.py:45
  59.8 3.0 %reshape.43 = bf16[128,4608]{1,0:T(8,128)(2,1)S(1)} reshape(bf16[16,8,16,288]{3,2,1,0:T(8,128)(2,1)} %all-to-all-done) | data formatting | bytes 2359296 | tf_op jit(solution)/shard_map/reshape | solution.py:45
  62.7 1.1 convolution_convert_fusion
  63.8 1.5 reshape.44
  65.4 0.6 fusion.13
  66.0 0.9 pad_maximum_fusion.1
  66.9 10.5 %all-to-all-start.1 = ((f32[32,16,160]{2,1,0:T(8,128)}), f32[32,16,160]{2,1,0:T(8,128)S(1)}, u32[]{:S(2)}, u32[]{:S(2)}) async-start(f32[32,16,160]{2,1,0:T(8,128)} %pad_maximum_fusion.1), calls=%async_computation.1 | async-start | bytes 1048576 | tf_op jit(solution)/shard_map/all_to_all | solution.py:55
  78.0 22.4 %all-to-all-done.1 = f32[32,16,160]{2,1,0:T(8,128)S(1)} async-done(((f32[32,16,160]{2,1,0:T(8,128)}), f32[32,16,160]{2,1,0:T(8,128)S(1)}, u32[]{:S(2)}, u32[]{:S(2)}) %all-to-all-start.1) | async-done | bytes 327712 | tf_op jit(solution)/shard_map/all_to_all | solution.py:55
  100.5 0.2 convert_element_type.40
  100.7 0.2 fusion.10
  101.1 0.2 convolution_multiply_fusion.2
  101.3 0.2 copy.40
  101.5 0.1 reshape.47
  101.7 0.2 all_to_all.19
  101.9 20.7 %all_to_all.27 = f32[32,1,2560]{2,1,0:T(1,128)S(1)} all-to-all(f32[32,1,2560]{2,1,0:T(1,128)S(1)} %all_to_all.19), channel_id=1, replica_groups=mesh['dp'=16,'tensor'=32] {'tensor'}, dimensions={0} | all-to-all | bytes 655360 | tf_op jit(solution)/shard_map/all_to_all | solution.py:75
  122.8 0.3 copy.29
  123.1 0.5 copy.30
  123.6 0.4 convolution_multiply_fusion.1
  124.1 2.1 %convolution_convert_fusion.1 = bf16[128,16,288]{0,2,1:T(8,128)(2,1)S(1)} fusion(f32[32,16,288]{2,1,0:T(8,128)S(1)} %pad_maximum_fusion, s32[32]{0:T(128)S(1)} %dynamic_slice.3), kind=kOutput, calls=%fused_computation.8 | convolution fusion | flops 227086336 | bytes 1769600 | tf_op jit(solution)/shard_map/sa,srd->ard/dot_general | solution.py:83
  126.1 1.9 copy.33
  128.0 7.0 %all-to-all-start.3 = ((bf16[16,8,16,288]{3,2,1,0:T(8,128)(2,1)}), bf16[16,8,16,288]{3,2,1,0:T(8,128)(2,1)}, u32[]{:S(2)}, u32[]{:S(2)}) async-start(bf16[16,8,16,288]{3,2,1,0:T(8,128)(2,1)} %bitcast.32), calls=%async_computation.3 | async-start | bytes 3145728 | tf_op jit(solution)/shard_map/all_to_all | solution.py:85
  135.1 2.7 %convolution_multiply_fusion = f32[32,128,256]{2,1,0:T(8,128)} fusion(bf16[32,128,16]{1,2,0:T(8,128)(2,1)S(1)} %copy.30, bf16[32,16,288]{2,1,0:T(8,128)(2,1)S(1)} %copy-done.2), kind=kOutput, calls=%fused_computation.7 | convolution fusion | flops 34603008 | bytes 4587520 | tf_op jit(solution)/shard_map/sjr,srd->sjd/dot_general | solution.py:96
  137.8 35.8 %all-to-all-done.3 = bf16[16,8,16,288]{3,2,1,0:T(8,128)(2,1)} async-done(((bf16[16,8,16,288]{3,2,1,0:T(8,128)(2,1)}), bf16[16,8,16,288]{3,2,1,0:T(8,128)(2,1)}, u32[]{:S(2)}, u32[]{:S(2)}) %all-to-all-start.3) | async-done | bytes 1179680 | tf_op jit(solution)/shard_map/all_to_all | solution.py:85
  173.6 1.7 reduce
  175.3 0.6 slice.43
  175.9 0.6 slice.42
  176.5 7.0 %fusion.6 = bf16[4096,256]{1,0:T(8,128)(2,1)} fusion(f32[4096,256]{1,0:T(8,128)} %bitcast.33, bf16[256,1024]{1,0:T(8,128)(2,1)S(1)} %copy-done.6, bf16[4096,1024]{1,0:T(8,128)(2,1)} %all-gather.2.cloned.1.call-done, pred[4096]{0:T(1024)(128)(4,1)S(1)} %broadcast_bitcast_fusion), kind=kOutput, calls=%fused_computation.5 | convolution fusion | flops 2153775104 | bytes 15208448 | tf_op jit(solution)/shard_map/dot_general | solution.py:93
  (33 shorter events, 0.9 us)
Async XLA Ops:
  7.2 58.2 %copy-start = (bf16[4096,256]{1,0:T(8,128)(2,1)S(1)}, bf16[4096,256]{1,0:T(8,128)(2,1)}, u32[]{:S(2)}) copy-start(bf16[4096,256]{1,0:T(8,128)(2,1)} %param.8) | copy-start | bytes 6291460
  7.2 169.3 %all-gather.2.cloned.1.call-start = ((), (), s32[]{:S(2)}) async-start(), calls=%async_computation.4 | async-start | bytes 8650752 | tf_op jit(solution)/shard_map/all_gather | solution.py:35
  8.8 12.4 %copy-start.4 = (s32[512]{0:T(512)S(1)}, s32[512]{0:T(512)}, u32[]{:S(2)}) copy-start(s32[512]{0:T(512)} %param.13) | copy-start | bytes 6148
  8.8 12.4 %copy-start.5 = (s32[128]{0:T(128)S(1)}, s32[128]{0:T(128)}, u32[]{:S(2)}) copy-start(s32[128]{0:T(128)} %param.14) | copy-start | bytes 1540
  10.2 49.6 %all-to-all-start = ((bf16[16,8,16,288]{3,2,1,0:T(8,128)(2,1)}), bf16[16,8,16,288]{3,2,1,0:T(8,128)(2,1)}, u32[]{:S(2)}, u32[]{:S(2)}) async-start(bf16[16,8,16,288]{3,2,1,0:T(8,128)(2,1)} %broadcast_in_dim.61), calls=%async_computation | async-start | bytes 3145728 | tf_op jit(solution)/shard_map/all_to_all | solution.py:45
  65.3 1.6 copy-start.1
  65.3 35.3 %copy-start.3 = (bf16[128,1024]{1,0:T(8,128)(2,1)S(1)}, bf16[128,1024]{1,0:T(8,128)(2,1)}, u32[]{:S(2)}) copy-start(bf16[128,1024]{1,0:T(8,128)(2,1)} %param.9) | copy-start | bytes 786436
  66.9 33.5 %all-to-all-start.1 = ((f32[32,16,160]{2,1,0:T(8,128)}), f32[32,16,160]{2,1,0:T(8,128)S(1)}, u32[]{:S(2)}, u32[]{:S(2)}) async-start(f32[32,16,160]{2,1,0:T(8,128)} %pad_maximum_fusion.1), calls=%async_computation.1 | async-start | bytes 1048576 | tf_op jit(solution)/shard_map/all_to_all | solution.py:55
  128.0 7.1 %copy-start.2 = (bf16[32,16,288]{2,1,0:T(8,128)(2,1)S(1)}, bf16[32,16,288]{2,1,0:T(8,128)(2,1)}, u32[]{:S(2)}) copy-start(bf16[32,16,288]{2,1,0:T(8,128)(2,1)} %copy-done.1) | copy-start | bytes 884740
  128.0 45.6 %all-to-all-start.3 = ((bf16[16,8,16,288]{3,2,1,0:T(8,128)(2,1)}), bf16[16,8,16,288]{3,2,1,0:T(8,128)(2,1)}, u32[]{:S(2)}, u32[]{:S(2)}) async-start(bf16[16,8,16,288]{3,2,1,0:T(8,128)(2,1)} %bitcast.32), calls=%async_computation.3 | async-start | bytes 3145728 | tf_op jit(solution)/shard_map/all_to_all | solution.py:85
  135.1 41.4 %copy-start.6 = (bf16[256,1024]{1,0:T(8,128)(2,1)S(1)}, bf16[256,1024]{1,0:T(8,128)(2,1)}, u32[]{:S(2)}) copy-start(bf16[256,1024]{1,0:T(8,128)(2,1)} %param.10) | copy-start | bytes 1572868
Sparse Core Ops, SparseCore 0:
  11.2 124.6 all-gather.1

commit v3 on v2

--- a/solution.py
+++ b/solution.py
@@ -42,10 +42,11 @@
 
     local_store = jnp.concatenate([adapter_down, adapter_up], axis=2)
     spread = jnp.broadcast_to(local_store[None], (group_count,) + local_store.shape)
-    stores = lax.all_to_all(spread, "dp", 0, 0, tiled=True).reshape(adapters, -1)
+    stores = lax.all_to_all(spread, "dp", 0, 0, tiled=True)
+    stores = stores.reshape((adapters,) + local_store.shape[1:])
     choose = (seg_slot[:, None] == slot_ids[None, :]).astype(bf16)
-    seg_store = jnp.dot(choose, stores, preferred_element_type=f32).astype(bf16)
-    seg_store = seg_store.reshape(seg_group, rank_dim, width_shard + key_shard)
+    seg_store = jnp.einsum("sa,ark->srk", choose, stores, preferred_element_type=f32)
+    seg_store = seg_store.astype(bf16)
     down_seg = seg_store[:, :, :width_shard]
     up_seg = seg_store[:, :, width_shard:]
 
@@ -65,17 +66,22 @@
     seg_up_own = 2.0 * jnp.dot(projected_own, masked_own, preferred_element_type=f32)
 
     low_spread = jnp.broadcast_to(
-        lowrank_own.astype(f32).reshape(1, row_count * rank_dim),
-        (tensor_size, row_count * rank_dim),
+        lowrank_own.reshape(1, row_count * rank_dim), (tensor_size, row_count * rank_dim)
     )
     up_pieces = jnp.transpose(
         seg_up_own.reshape(rank_dim, tensor_size, key_shard), (1, 0, 2)
     ).reshape(tensor_size, rank_dim * key_shard)
-    second = jnp.concatenate([low_spread, up_pieces], axis=1)
-    second = lax.all_to_all(second, "tensor", 0, 0, tiled=True)
+    up_high = up_pieces.astype(bf16)
+    up_low = (up_pieces - up_high.astype(f32)).astype(bf16)
+    second = jnp.concatenate([low_spread, up_high, up_low], axis=1)
+    second = second.reshape(tensor_size, -1, 128)
+    second = lax.all_to_all(second, "tensor", 0, 0, tiled=True).reshape(tensor_size, -1)
     lowrank = second[:, : row_count * rank_dim].reshape(seg_group, seg_len, rank_dim)
-    lowrank = lowrank.astype(bf16)
-    seg_up = second[:, row_count * rank_dim :].reshape(seg_group, rank_dim, key_shard)
+    piece = rank_dim * key_shard
+    low_end = row_count * rank_dim
+    seg_up = second[:, low_end : low_end + piece].astype(f32)
+    seg_up = seg_up + second[:, low_end + piece :].astype(f32)
+    seg_up = seg_up.reshape(seg_group, rank_dim, key_shard)
 
     seg_down = 2.0 * jnp.einsum("sjr,sjd->srd", lowrank, input_seg, preferred_element_type=f32)
     seg_grad = jnp.concatenate([seg_down, seg_up], axis=2)

time: 191 us -> 184 us (0.963)
  local copies, waits for them, and re-layouts: 11.2 us -> 7 us
  blocking collectives: 20.7 us -> 17.1 us
    reshape x3 -> x2, local copies, waits for them, and re-layouts: 4.59 us -> 0.62 us  [the longest x1 0.51 us: on_device(): second[:, :row_count * rank_dim].reshape(seg_group, seg_len, rank_dim)]
    all_to_all x1, blocking collectives: 20.7 us -> 17.1 us  [on_device(): lax.all_to_all(second, 'tensor', 0, 0, tiled=True).reshape(tensor_size, -1)]
  transfers between devices with their start and end apart: 4 -> 4, of which waited for: 3 -> 3; matrix products, arithmetic and copies ran while one was open for 11% -> 10% of each run, Pallas kernels for 0% -> 0%
where the time goes in v3:
time: 184 us; the launch traced here: 183 us
  waiting for transfers between devices  97.2 us (53%)
  starting transfers between devices  28.2 us (15%)
  blocking collectives  17.1 us (9%)
  matrix products  14.9 us (8%)
  between operations  14.9 us (8%)
  local copies, waits for them, and re-layouts  7 us (4%)
  other arithmetic  3.79 us (2%)
    all_to_all x1, waiting for transfers between devices, on_device(): stores = lax.all_to_all(spread, 'dp', 0, 0, tiled=True)  38.3 us
    all_to_all x1, waiting for transfers between devices, on_device(): gathered = lax.all_to_all(part, 'dp', 0, 0, tiled=True)  35.8 us
    all_to_all x1, waiting for transfers between devices, on_device(): first = lax.all_to_all(first, 'tensor', 0, 0, tiled=True)  22.5 us
    all_to_all x1, blocking collectives, on_device(): lax.all_to_all(second, 'tensor', 0, 0, tiled=True).reshape(tensor_size, -1)  17.1 us
    all_to_all x1, starting transfers between devices, on_device(): stores = lax.all_to_all(spread, 'dp', 0, 0, tiled=True)  11 us
    all_to_all x1, starting transfers between devices, on_device(): first = lax.all_to_all(first, 'tensor', 0, 0, tiled=True)  10.5 us
    dot_general x1, matrix products, on_device(): lax.dot_general(whole, key_weight, (((1,), (1,)), ((), ())), preferred_el...  6.96 us
    all_to_all x1, starting transfers between devices, on_device(): gathered = lax.all_to_all(part, 'dp', 0, 0, tiled=True)  6.66 us
  transfers between devices with their start and end apart: 4, of which 3 were waited for; matrix products, arithmetic and copies ran while one was open for 10% of the time, Pallas kernels for 0%

profile of v3, /device:TPU:1, one launch (start us, length us, event | category | flops | bytes accessed | tf_op | source)
XLA Modules:
  0.0 183.1 jit_solution(9862819210675680933)
XLA Ops:
  7.2 0.7 all-gather.2.cloned.1.call-update
  7.9 0.9 pad_maximum_fusion.2
  8.8 1.3 broadcast_in_dim.58
  10.2 11.0 %all-to-all-start = ((bf16[16,8,16,288]{3,2,1,0:T(8,128)(2,1)}), bf16[16,8,16,288]{3,2,1,0:T(8,128)(2,1)}, u32[]{:S(2)}, u32[]{:S(2)}) async-start(bf16[16,8,16,288]{3,2,1,0:T(8,128)(2,1)} %broadcast_in_dim.58), calls=%async_computation | async-start | bytes 3145728 | tf_op jit(solution)/shard_map/all_to_all | solution.py:45
  21.2 0.2 select_reduce_fusion
  21.5 38.3 %all-to-all-done = bf16[16,8,16,288]{3,2,1,0:T(8,128)(2,1)} async-done(((bf16[16,8,16,288]{3,2,1,0:T(8,128)(2,1)}), bf16[16,8,16,288]{3,2,1,0:T(8,128)(2,1)}, u32[]{:S(2)}, u32[]{:S(2)}) %all-to-all-start) | async-done | bytes 1179680 | tf_op jit(solution)/shard_map/all_to_all | solution.py:45
  59.8 1.8 %fusion.12 = bf16[32,16,288]{2,0,1:T(8,128)(2,1)S(1)} fusion(bf16[128,16,288]{2,1,0:T(8,128)(2,1)} %bitcast.3, s32[32]{0:T(128)S(1)} %dynamic_slice.3), kind=kOutput, calls=%fused_computation.10 | convolution fusion | flops 37900288 | bytes 1474688 | tf_op jit(solution)/shard_map/sa,ark->srk/dot_general | solution.py:48
  61.7 0.2 copy.28
  61.8 0.6 fusion.17
  62.5 0.9 pad_maximum_fusion.1
  63.3 10.5 %all-to-all-start.1 = ((f32[32,16,160]{2,1,0:T(8,128)}), f32[32,16,160]{2,1,0:T(8,128)S(1)}, u32[]{:S(2)}, u32[]{:S(2)}) async-start(f32[32,16,160]{2,1,0:T(8,128)} %pad_maximum_fusion.1), calls=%async_computation.1 | async-start | bytes 1048576 | tf_op jit(solution)/shard_map/all_to_all | solution.py:56
  74.5 22.5 %all-to-all-done.1 = f32[32,16,160]{2,1,0:T(8,128)S(1)} async-done(((f32[32,16,160]{2,1,0:T(8,128)}), f32[32,16,160]{2,1,0:T(8,128)S(1)}, u32[]{:S(2)}, u32[]{:S(2)}) %all-to-all-start.1) | async-done | bytes 327712 | tf_op jit(solution)/shard_map/all_to_all | solution.py:56
  97.0 0.2 convert_element_type.50
  97.2 0.2 convolution_convert_fusion.1
  97.3 0.1 copy.30
  97.6 0.2 convolution_multiply_fusion.2
  97.9 0.2 copy.52
  98.1 0.1 reshape.48
  98.3 17.1 %all_to_all.20 = bf16[32,24,128]{2,1,0:T(8,128)(2,1)S(1)} all-to-all(bf16[32,24,128]{2,1,0:T(8,128)(2,1)S(1)} %bitcast.41), channel_id=1, replica_groups=mesh['dp'=16,'tensor'=32] {'tensor'}, dimensions={0} | all-to-all | bytes 393216 | tf_op jit(solution)/shard_map/all_to_all | solution.py:78
  115.6 0.3 copy.32
  115.9 0.5 copy.33
  116.4 0.4 convolution_multiply_fusion.1
  116.8 0.3 copy-done.1
  117.1 2.1 %convolution_convert_fusion = bf16[128,16,288]{0,2,1:T(8,128)(2,1)S(1)} fusion(f32[32,16,288]{2,1,0:T(8,128)S(1)} %pad_maximum_fusion, s32[32]{0:T(128)S(1)} %dynamic_slice.3), kind=kOutput, calls=%fused_computation.9 | convolution fusion | flops 227086336 | bytes 1769600 | tf_op jit(solution)/shard_map/sa,srd->ard/dot_general | solution.py:89
  119.2 1.9 %copy.37 = bf16[128,16,288]{2,1,0:T(8,128)(2,1)} copy(bf16[128,16,288]{0,2,1:T(8,128)(2,1)S(1)} %convolution_convert_fusion) | data formatting | bytes 2359296 | tf_op jit(solution)/shard_map/convert_element_type | solution.py:90
  121.1 6.7 %all-to-all-start.3 = ((bf16[16,8,16,288]{3,2,1,0:T(8,128)(2,1)}), bf16[16,8,16,288]{3,2,1,0:T(8,128)(2,1)}, u32[]{:S(2)}, u32[]{:S(2)}) async-start(bf16[16,8,16,288]{3,2,1,0:T(8,128)(2,1)} %bitcast.35), calls=%async_computation.3 | async-start | bytes 3145728 | tf_op jit(solution)/shard_map/all_to_all | solution.py:91
  127.8 2.7 %convolution_multiply_fusion = f32[32,128,256]{2,1,0:T(8,128)} fusion(bf16[32,128,16]{1,2,0:T(8,128)(2,1)S(1)} %copy-done.2, bf16[32,16,256]{2,0,1:T(8,128)(2,1)S(1)} %slice.39), kind=kOutput, calls=%fused_computation.6 | convolution fusion | flops 34603008 | bytes 4587520 | tf_op jit(solution)/shard_map/sjr,srd->sjd/dot_general | solution.py:102
  130.6 35.8 %all-to-all-done.3 = bf16[16,8,16,288]{3,2,1,0:T(8,128)(2,1)} async-done(((bf16[16,8,16,288]{3,2,1,0:T(8,128)(2,1)}), bf16[16,8,16,288]{3,2,1,0:T(8,128)(2,1)}, u32[]{:S(2)}, u32[]{:S(2)}) %all-to-all-start.3) | async-done | bytes 1179680 | tf_op jit(solution)/shard_map/all_to_all | solution.py:91
  166.3 1.7 reduce
  168.0 0.6 slice.47
  168.6 0.6 slice.46
  169.3 7.0 %fusion.6 = bf16[4096,256]{1,0:T(8,128)(2,1)} fusion(f32[4096,256]{1,0:T(8,128)} %bitcast.36, bf16[256,1024]{1,0:T(8,128)(2,1)S(1)} %copy-done.6, bf16[4096,1024]{1,0:T(8,128)(2,1)} %all-gather.2.cloned.1.call-done, pred[4096]{0:T(1024)(128)(4,1)S(1)} %broadcast_bitcast_fusion), kind=kOutput, calls=%fused_computation.4 | convolution fusion | flops 2153775104 | bytes 15208448 | tf_op jit(solution)/shard_map/dot_general | solution.py:99
  (34 shorter events, 0.9 us)
Async XLA Ops:
  7.2 54.7 %copy-start = (bf16[4096,256]{1,0:T(8,128)(2,1)S(1)}, bf16[4096,256]{1,0:T(8,128)(2,1)}, u32[]{:S(2)}) copy-start(bf16[4096,256]{1,0:T(8,128)(2,1)} %param.8) | copy-start | bytes 6291460
  7.2 162.1 %all-gather.2.cloned.1.call-start = ((), (), s32[]{:S(2)}) async-start(), calls=%async_computation.4 | async-start | bytes 8650752 | tf_op jit(solution)/shard_map/all_gather | solution.py:35
  8.8 12.4 %copy-start.4 = (s32[512]{0:T(512)S(1)}, s32[512]{0:T(512)}, u32[]{:S(2)}) copy-start(s32[512]{0:T(512)} %param.13) | copy-start | bytes 6148
  8.8 12.4 %copy-start.5 = (s32[128]{0:T(128)S(1)}, s32[128]{0:T(128)}, u32[]{:S(2)}) copy-start(s32[128]{0:T(128)} %param.14) | copy-start | bytes 1540
  10.2 49.6 %all-to-all-start = ((bf16[16,8,16,288]{3,2,1,0:T(8,128)(2,1)}), bf16[16,8,16,288]{3,2,1,0:T(8,128)(2,1)}, u32[]{:S(2)}, u32[]{:S(2)}) async-start(bf16[16,8,16,288]{3,2,1,0:T(8,128)(2,1)} %broadcast_in_dim.58), calls=%async_computation | async-start | bytes 3145728 | tf_op jit(solution)/shard_map/all_to_all | solution.py:45
  61.8 35.3 %copy-start.3 = (bf16[128,1024]{1,0:T(8,128)(2,1)S(1)}, bf16[128,1024]{1,0:T(8,128)(2,1)}, u32[]{:S(2)}) copy-start(bf16[128,1024]{1,0:T(8,128)(2,1)} %param.9) | copy-start | bytes 786436
  63.3 33.6 %all-to-all-start.1 = ((f32[32,16,160]{2,1,0:T(8,128)}), f32[32,16,160]{2,1,0:T(8,128)S(1)}, u32[]{:S(2)}, u32[]{:S(2)}) async-start(f32[32,16,160]{2,1,0:T(8,128)} %pad_maximum_fusion.1), calls=%async_computation.1 | async-start | bytes 1048576 | tf_op jit(solution)/shard_map/all_to_all | solution.py:56
  116.4 0.7 copy-start.1
  121.1 6.7 %copy-start.2 = (bf16[32,128,16]{1,2,0:T(8,128)(2,1)S(1)}, bf16[32,128,16]{1,2,0:T(8,128)(2,1)}, u32[]{:S(2)}) copy-start(bf16[32,128,16]{1,2,0:T(8,128)(2,1)} %copy-done.1) | copy-start | bytes 393220
  121.1 45.2 %all-to-all-start.3 = ((bf16[16,8,16,288]{3,2,1,0:T(8,128)(2,1)}), bf16[16,8,16,288]{3,2,1,0:T(8,128)(2,1)}, u32[]{:S(2)}, u32[]{:S(2)}) async-start(bf16[16,8,16,288]{3,2,1,0:T(8,128)(2,1)} %bitcast.35), calls=%async_computation.3 | async-start | bytes 3145728 | tf_op jit(solution)/shard_map/all_to_all | solution.py:91
  127.8 41.4 %copy-start.6 = (bf16[256,1024]{1,0:T(8,128)(2,1)S(1)}, bf16[256,1024]{1,0:T(8,128)(2,1)}, u32[]{:S(2)}) copy-start(bf16[256,1024]{1,0:T(8,128)(2,1)} %param.10) | copy-start | bytes 1572868
Sparse Core Ops, SparseCore 0:
  11.2 121.9 all-gather.1

commit v4 on v3

--- a/solution.py
+++ b/solution.py
@@ -71,8 +71,9 @@
     up_pieces = jnp.transpose(
         seg_up_own.reshape(rank_dim, tensor_size, key_shard), (1, 0, 2)
     ).reshape(tensor_size, rank_dim * key_shard)
-    up_high = up_pieces.astype(bf16)
-    up_low = (up_pieces - up_high.astype(f32)).astype(bf16)
+    up_round = lax.reduce_precision(up_pieces, exponent_bits=8, mantissa_bits=7)
+    up_high = up_round.astype(bf16)
+    up_low = (up_pieces - up_round).astype(bf16)
     second = jnp.concatenate([low_spread, up_high, up_low], axis=1)
     second = second.reshape(tensor_size, -1, 128)
     second = lax.all_to_all(second, "tensor", 0, 0, tiled=True).reshape(tensor_size, -1)
@@ -89,10 +90,6 @@
     part = jnp.einsum("sa,srd->ard", onehot, seg_grad, precision=lax.Precision.HIGHEST)
     part = part.astype(bf16).reshape(group_count, per_owner, rank_dim, -1)
     gathered = lax.all_to_all(part, "dp", 0, 0, tiled=True)
-    total = jnp.sum(gathered.astype(f32), axis=0)
-    down_grad = total[:, :, :width_shard].astype(bf16)
-    up_grad = total[:, :, width_shard:].astype(bf16)
-
     whole = jnp.where(
         jnp.repeat(seg_live, seg_len)[:, None], whole_raw, jnp.zeros_like(whole_raw)
     )
@@ -101,6 +98,11 @@
     )
     extra = jnp.einsum("sjr,srd->sjd", lowrank, down_seg, preferred_element_type=f32)
     input_grad = (frozen + 2.0 * extra.reshape(tok_group, width_shard)).astype(bf16)
+    gathered, input_grad = lax.optimization_barrier((gathered, input_grad))
+    total = jnp.sum(gathered.astype(f32), axis=0)
+    down_grad = total[:, :, :width_shard].astype(bf16)
+    up_grad = total[:, :, width_shard:].astype(bf16)
+
     return (input_grad, down_grad, up_grad)
 
 

time: 184 us -> 177 us (0.962)
  waiting for transfers between devices: 97.2 us -> 90.2 us
    all_to_all x1, waiting for transfers between devices: 35.8 us -> 27 us  [on_device(): gathered = lax.all_to_all(part, 'dp', 0, 0, tiled=True)]
  transfers between devices with their start and end apart: 4 -> 4, of which waited for: 3 -> 4; matrix products, arithmetic and copies ran while one was open for 10% -> 13% of each run, Pallas kernels for 0% -> 0%
where the time goes in v4:
time: 177 us
  waiting for transfers between devices  90.2 us (51%)
  starting transfers between devices  28.2 us (16%)
  blocking collectives  17 us (10%)
  matrix products  15.9 us (9%)
  between operations  14.9 us (8%)
  local copies, waits for them, and re-layouts  6.88 us (4%)
  other arithmetic  3.78 us (2%)
    all_to_all x1, waiting for transfers between devices, on_device(): stores = lax.all_to_all(spread, 'dp', 0, 0, tiled=True)  38.3 us
    all_to_all x1, waiting for transfers between devices, on_device(): gathered = lax.all_to_all(part, 'dp', 0, 0, tiled=True)  27 us
    all_to_all x1, waiting for transfers between devices, on_device(): first = lax.all_to_all(first, 'tensor', 0, 0, tiled=True)  22.5 us
    all_to_all x1, blocking collectives, on_device(): lax.all_to_all(second, 'tensor', 0, 0, tiled=True).reshape(tensor_size, -1)  17 us
    all_to_all x1, starting transfers between devices, on_device(): stores = lax.all_to_all(spread, 'dp', 0, 0, tiled=True)  11 us
    all_to_all x1, starting transfers between devices, on_device(): first = lax.all_to_all(first, 'tensor', 0, 0, tiled=True)  10.5 us
    dot_general x1, matrix products, on_device(): lax.dot_general(whole, key_weight, (((1,), (1,)), ((), ())), preferred_el...  6.95 us
    all_to_all x1, starting transfers between devices, on_device(): gathered = lax.all_to_all(part, 'dp', 0, 0, tiled=True)  6.67 us
  transfers between devices with their start and end apart: 4, of which 4 were waited for; matrix products, arithmetic and copies ran while one was open for 13% of the time, Pallas kernels for 0%

profile of v4, /device:TPU:1, one launch (start us, length us, event | category | flops | bytes accessed | tf_op | source)
XLA Modules:
  0.0 176.9 jit_solution(16008067518316470989)
XLA Ops:
  7.2 0.7 all-gather.2.cloned.1.call-update
  7.9 0.9 pad_maximum_fusion.2
  8.8 1.3 broadcast_in_dim.54
  10.2 11.0 %all-to-all-start = ((bf16[16,8,16,288]{3,2,1,0:T(8,128)(2,1)}), bf16[16,8,16,288]{3,2,1,0:T(8,128)(2,1)}, u32[]{:S(2)}, u32[]{:S(2)}) async-start(bf16[16,8,16,288]{3,2,1,0:T(8,128)(2,1)} %broadcast_in_dim.54), calls=%async_computation | async-start | bytes 3145728 | tf_op jit(solution)/shard_map/all_to_all | solution.py:45
  21.2 0.2 select_reduce_fusion
  21.5 38.3 %all-to-all-done = bf16[16,8,16,288]{3,2,1,0:T(8,128)(2,1)} async-done(((bf16[16,8,16,288]{3,2,1,0:T(8,128)(2,1)}), bf16[16,8,16,288]{3,2,1,0:T(8,128)(2,1)}, u32[]{:S(2)}, u32[]{:S(2)}) %all-to-all-start) | async-done | bytes 1179680 | tf_op jit(solution)/shard_map/all_to_all | solution.py:45
  59.8 1.8 %fusion.12 = bf16[32,16,288]{2,0,1:T(8,128)(2,1)S(1)} fusion(bf16[128,16,288]{2,1,0:T(8,128)(2,1)} %bitcast.2, s32[32]{0:T(128)S(1)} %dynamic_slice.3), kind=kOutput, calls=%fused_computation.10 | convolution fusion | flops 37900288 | bytes 1474688 | tf_op jit(solution)/shard_map/sa,ark->srk/dot_general | solution.py:48
  61.7 0.2 copy.28
  61.8 0.6 fusion.17
  62.5 0.9 pad_maximum_fusion.1
  63.3 10.5 %all-to-all-start.1 = ((f32[32,16,160]{2,1,0:T(8,128)}), f32[32,16,160]{2,1,0:T(8,128)S(1)}, u32[]{:S(2)}, u32[]{:S(2)}) async-start(f32[32,16,160]{2,1,0:T(8,128)} %pad_maximum_fusion.1), calls=%async_computation.1 | async-start | bytes 1048576 | tf_op jit(solution)/shard_map/all_to_all | solution.py:56
  74.5 22.5 %all-to-all-done.1 = f32[32,16,160]{2,1,0:T(8,128)S(1)} async-done(((f32[32,16,160]{2,1,0:T(8,128)}), f32[32,16,160]{2,1,0:T(8,128)S(1)}, u32[]{:S(2)}, u32[]{:S(2)}) %all-to-all-start.1) | async-done | bytes 327712 | tf_op jit(solution)/shard_map/all_to_all | solution.py:56
  97.0 0.2 convolution_multiply_fusion.2
  97.2 0.2 copy.52
  97.4 0.1 reshape.48
  97.6 0.2 convert_element_type.47
  97.8 1.1 convolution_convert_fusion.1
  98.9 0.1 copy.30
  99.3 17.0 %all_to_all.20 = bf16[32,24,128]{2,1,0:T(8,128)(2,1)S(1)} all-to-all(bf16[32,24,128]{2,1,0:T(8,128)(2,1)S(1)} %bitcast.41), channel_id=1, replica_groups=mesh['dp'=16,'tensor'=32] {'tensor'}, dimensions={0} | all-to-all | bytes 393216 | tf_op jit(solution)/shard_map/all_to_all | solution.py:79
  116.4 0.3 copy.32
  116.6 0.5 copy.33
  117.3 0.4 convolution_multiply_fusion.1
  117.9 2.1 %convolution_convert_fusion = bf16[128,16,288]{0,2,1:T(8,128)(2,1)S(1)} fusion(f32[32,16,288]{2,1,0:T(8,128)S(1)} %pad_maximum_fusion, s32[32]{0:T(128)S(1)} %dynamic_slice.3), kind=kOutput, calls=%fused_computation.9 | convolution fusion | flops 227086336 | bytes 1769600 | tf_op jit(solution)/shard_map/sa,srd->ard/dot_general | solution.py:90
  120.0 1.9 %copy.35 = bf16[128,16,288]{2,1,0:T(8,128)(2,1)} copy(bf16[128,16,288]{0,2,1:T(8,128)(2,1)S(1)} %convolution_convert_fusion) | data formatting | bytes 2359296 | tf_op jit(solution)/shard_map/convert_element_type | solution.py:91
  121.9 6.7 %all-to-all-start.3 = ((bf16[16,8,16,288]{3,2,1,0:T(8,128)(2,1)}), bf16[16,8,16,288]{3,2,1,0:T(8,128)(2,1)}, u32[]{:S(2)}, u32[]{:S(2)}) async-start(bf16[16,8,16,288]{3,2,1,0:T(8,128)(2,1)} %bitcast.35), calls=%async_computation.3 | async-start | bytes 3145728 | tf_op jit(solution)/shard_map/all_to_all | solution.py:92
  128.7 2.7 %convolution_multiply_fusion = f32[32,128,256]{2,1,0:T(8,128)} fusion(bf16[32,128,16]{1,2,0:T(8,128)(2,1)S(1)} %copy-done.2, bf16[32,16,256]{2,0,1:T(8,128)(2,1)S(1)} %slice.39), kind=kOutput, calls=%fused_computation.6 | convolution fusion | flops 34603008 | bytes 4587520 | tf_op jit(solution)/shard_map/sjr,srd->sjd/dot_general | solution.py:99
  131.4 1.8 %all-gather.2.cloned.1.call-done = bf16[4096,1024]{1,0:T(8,128)(2,1)} async-done(((bf16[128,1024]{1,0:T(8,128)(2,1)}), bf16[4096,1024]{1,0:T(8,128)(2,1)}) %all-gather.2.cloned.1.call-update) | async-done | bytes 8388624 | tf_op jit(solution)/shard_map/all_gather | solution.py:35
  133.2 7.0 %fusion.6 = bf16[4096,256]{1,0:T(8,128)(2,1)} fusion(f32[4096,256]{1,0:T(8,128)} %bitcast.36, bf16[256,1024]{1,0:T(8,128)(2,1)S(1)} %copy-done.6, bf16[4096,1024]{1,0:T(8,128)(2,1)} %all-gather.2.cloned.1.call-done, pred[4096]{0:T(1024)(128)(4,1)S(1)} %broadcast_bitcast_fusion), kind=kOutput, calls=%fused_computation.4 | convolution fusion | flops 2153775104 | bytes 15208448 | tf_op jit(solution)/shard_map/dot_general | solution.py:96
  140.1 27.0 %all-to-all-done.3 = bf16[16,8,16,288]{3,2,1,0:T(8,128)(2,1)} async-done(((bf16[16,8,16,288]{3,2,1,0:T(8,128)(2,1)}), bf16[16,8,16,288]{3,2,1,0:T(8,128)(2,1)}, u32[]{:S(2)}, u32[]{:S(2)}) %all-to-all-start.3) | async-done | bytes 1179680 | tf_op jit(solution)/shard_map/all_to_all | solution.py:92
  167.2 1.7 reduce
  168.8 0.6 slice.46
  169.4 0.6 slice.47
  (34 shorter events, 1.0 us)
Async XLA Ops:
  7.2 54.7 %copy-start = (bf16[4096,256]{1,0:T(8,128)(2,1)S(1)}, bf16[4096,256]{1,0:T(8,128)(2,1)}, u32[]{:S(2)}) copy-start(bf16[4096,256]{1,0:T(8,128)(2,1)} %param.8) | copy-start | bytes 6291460
  7.2 126.0 %all-gather.2.cloned.1.call-start = ((), (), s32[]{:S(2)}) async-start(), calls=%async_computation.4 | async-start | bytes 8650752 | tf_op jit(solution)/shard_map/all_gather | solution.py:35
  8.8 12.4 %copy-start.4 = (s32[512]{0:T(512)S(1)}, s32[512]{0:T(512)}, u32[]{:S(2)}) copy-start(s32[512]{0:T(512)} %param.13) | copy-start | bytes 6148
  8.8 12.4 %copy-start.5 = (s32[128]{0:T(128)S(1)}, s32[128]{0:T(128)}, u32[]{:S(2)}) copy-start(s32[128]{0:T(128)} %param.14) | copy-start | bytes 1540
  10.2 49.6 %all-to-all-start = ((bf16[16,8,16,288]{3,2,1,0:T(8,128)(2,1)}), bf16[16,8,16,288]{3,2,1,0:T(8,128)(2,1)}, u32[]{:S(2)}, u32[]{:S(2)}) async-start(bf16[16,8,16,288]{3,2,1,0:T(8,128)(2,1)} %broadcast_in_dim.54), calls=%async_computation | async-start | bytes 3145728 | tf_op jit(solution)/shard_map/all_to_all | solution.py:45
  61.8 35.1 %copy-start.3 = (bf16[128,1024]{1,0:T(8,128)(2,1)S(1)}, bf16[128,1024]{1,0:T(8,128)(2,1)}, u32[]{:S(2)}) copy-start(bf16[128,1024]{1,0:T(8,128)(2,1)} %param.9) | copy-start | bytes 786436
  63.3 33.6 %all-to-all-start.1 = ((f32[32,16,160]{2,1,0:T(8,128)}), f32[32,16,160]{2,1,0:T(8,128)S(1)}, u32[]{:S(2)}, u32[]{:S(2)}) async-start(f32[32,16,160]{2,1,0:T(8,128)} %pad_maximum_fusion.1), calls=%async_computation.1 | async-start | bytes 1048576 | tf_op jit(solution)/shard_map/all_to_all | solution.py:56
  117.2 0.7 copy-start.1
  121.9 6.8 %copy-start.2 = (bf16[32,128,16]{1,2,0:T(8,128)(2,1)S(1)}, bf16[32,128,16]{1,2,0:T(8,128)(2,1)}, u32[]{:S(2)}) copy-start(bf16[32,128,16]{1,2,0:T(8,128)(2,1)} %copy-done.1) | copy-start | bytes 393220
  121.9 45.3 %all-to-all-start.3 = ((bf16[16,8,16,288]{3,2,1,0:T(8,128)(2,1)}), bf16[16,8,16,288]{3,2,1,0:T(8,128)(2,1)}, u32[]{:S(2)}, u32[]{:S(2)}) async-start(bf16[16,8,16,288]{3,2,1,0:T(8,128)(2,1)} %bitcast.35), calls=%async_computation.3 | async-start | bytes 3145728 | tf_op jit(solution)/shard_map/all_to_all | solution.py:92
  128.7 4.5 %copy-start.6 = (bf16[256,1024]{1,0:T(8,128)(2,1)S(1)}, bf16[256,1024]{1,0:T(8,128)(2,1)}, u32[]{:S(2)}) copy-start(bf16[256,1024]{1,0:T(8,128)(2,1)} %param.10) | copy-start | bytes 1572868
Sparse Core Ops, SparseCore 0:
  11.2 121.9 all-gather.1

commit v5 on v4

--- a/solution.py
+++ b/solution.py
@@ -86,8 +86,12 @@
 
     seg_down = 2.0 * jnp.einsum("sjr,sjd->srd", lowrank, input_seg, preferred_element_type=f32)
     seg_grad = jnp.concatenate([seg_down, seg_up], axis=2)
-    onehot = (seg_slot[:, None] == slot_ids[None, :]).astype(f32)
-    part = jnp.einsum("sa,srd->ard", onehot, seg_grad, precision=lax.Precision.HIGHEST)
+    onehot = (slot_ids[:, None] == seg_slot[None, :]).astype(bf16)
+    grad_round = lax.reduce_precision(seg_grad, exponent_bits=8, mantissa_bits=7)
+    grad_high = grad_round.astype(bf16)
+    grad_low = (seg_grad - grad_round).astype(bf16)
+    part = jnp.einsum("as,srd->ard", onehot, grad_high, preferred_element_type=f32)
+    part = part + jnp.einsum("as,srd->ard", onehot, grad_low, preferred_element_type=f32)
     part = part.astype(bf16).reshape(group_count, per_owner, rank_dim, -1)
     gathered = lax.all_to_all(part, "dp", 0, 0, tiled=True)
     whole = jnp.where(
@@ -99,9 +103,8 @@
     extra = jnp.einsum("sjr,srd->sjd", lowrank, down_seg, preferred_element_type=f32)
     input_grad = (frozen + 2.0 * extra.reshape(tok_group, width_shard)).astype(bf16)
     gathered, input_grad = lax.optimization_barrier((gathered, input_grad))
-    total = jnp.sum(gathered.astype(f32), axis=0)
-    down_grad = total[:, :, :width_shard].astype(bf16)
-    up_grad = total[:, :, width_shard:].astype(bf16)
+    down_grad = jnp.sum(gathered[..., :width_shard].astype(f32), axis=0).astype(bf16)
+    up_grad = jnp.sum(gathered[..., width_shard:].astype(f32), axis=0).astype(bf16)
 
     return (input_grad, down_grad, up_grad)
 

time: 177 us -> 177 us (level)
  other arithmetic: 3.78 us -> 5.99 us
    reduce_sum x1 -> x2, other arithmetic: 1.66 us -> 3.79 us  [the longest x1 2.02 us: on_device(): jnp.sum(gathered[..., :width_shard].astype(f32), axis=0).astype(bf16)]
where the time goes in v5:
time: 177 us
  waiting for transfers between devices  90.2 us (51%)
  starting transfers between devices  28.2 us (16%)
  blocking collectives  17.1 us (10%)
  matrix products  15 us (8%)
  between operations  14.9 us (8%)
  other arithmetic  5.99 us (3%)
  local copies, waits for them, and re-layouts  5.49 us (3%)
    all_to_all x1, waiting for transfers between devices, on_device(): stores = lax.all_to_all(spread, 'dp', 0, 0, tiled=True)  38.3 us
    all_to_all x1, waiting for transfers between devices, on_device(): gathered = lax.all_to_all(part, 'dp', 0, 0, tiled=True)  26.1 us
    all_to_all x1, waiting for transfers between devices, on_device(): first = lax.all_to_all(first, 'tensor', 0, 0, tiled=True)  22.5 us
    all_to_all x1, blocking collectives, on_device(): lax.all_to_all(second, 'tensor', 0, 0, tiled=True).reshape(tensor_size, -1)  17.1 us
    all_to_all x1, starting transfers between devices, on_device(): stores = lax.all_to_all(spread, 'dp', 0, 0, tiled=True)  11 us
    all_to_all x1, starting transfers between devices, on_device(): first = lax.all_to_all(first, 'tensor', 0, 0, tiled=True)  10.4 us
    dot_general x1, matrix products, on_device(): lax.dot_general(whole, key_weight, (((1,), (1,)), ((), ())), preferred_el...  6.95 us
    all_to_all x1, starting transfers between devices, on_device(): gathered = lax.all_to_all(part, 'dp', 0, 0, tiled=True)  6.66 us
  transfers between devices with their start and end apart: 4, of which 4 were waited for; matrix products, arithmetic and copies ran while one was open for 13% of the time, Pallas kernels for 0%

profile of v5, /device:TPU:1, one launch (start us, length us, event | category | flops | bytes accessed | tf_op | source)
XLA Modules:
  0.0 176.9 jit_solution(10040351715815421121)
XLA Ops:
  7.2 0.7 all-gather.2.cloned.1.call-update
  7.9 0.9 pad_maximum_fusion.2
  8.8 1.3 broadcast_in_dim.54
  10.2 11.0 %all-to-all-start = ((bf16[16,8,16,288]{3,2,1,0:T(8,128)(2,1)}), bf16[16,8,16,288]{3,2,1,0:T(8,128)(2,1)}, u32[]{:S(2)}, u32[]{:S(2)}) async-start(bf16[16,8,16,288]{3,2,1,0:T(8,128)(2,1)} %broadcast_in_dim.54), calls=%async_computation | async-start | bytes 3145728 | tf_op jit(solution)/shard_map/all_to_all | solution.py:45
  21.2 0.2 select_reduce_fusion
  21.5 38.3 %all-to-all-done = bf16[16,8,16,288]{3,2,1,0:T(8,128)(2,1)} async-done(((bf16[16,8,16,288]{3,2,1,0:T(8,128)(2,1)}), bf16[16,8,16,288]{3,2,1,0:T(8,128)(2,1)}, u32[]{:S(2)}, u32[]{:S(2)}) %all-to-all-start) | async-done | bytes 1179680 | tf_op jit(solution)/shard_map/all_to_all | solution.py:45
  59.8 1.8 %fusion.12 = bf16[32,16,288]{2,0,1:T(8,128)(2,1)S(1)} fusion(bf16[128,16,288]{2,1,0:T(8,128)(2,1)} %bitcast.3, s32[32]{0:T(128)S(1)} %dynamic_slice.3), kind=kOutput, calls=%fused_computation.10 | convolution fusion | flops 37900288 | bytes 1474688 | tf_op jit(solution)/shard_map/sa,ark->srk/dot_general | solution.py:48
  61.7 0.2 copy.47
  61.8 0.6 fusion.20
  62.5 0.9 pad_maximum_fusion.1
  63.3 10.4 %all-to-all-start.1 = ((f32[32,16,160]{2,1,0:T(8,128)}), f32[32,16,160]{2,1,0:T(8,128)S(1)}, u32[]{:S(2)}, u32[]{:S(2)}) async-start(f32[32,16,160]{2,1,0:T(8,128)} %pad_maximum_fusion.1), calls=%async_computation.1 | async-start | bytes 1048576 | tf_op jit(solution)/shard_map/all_to_all | solution.py:56
  74.5 22.5 %all-to-all-done.1 = f32[32,16,160]{2,1,0:T(8,128)S(1)} async-done(((f32[32,16,160]{2,1,0:T(8,128)}), f32[32,16,160]{2,1,0:T(8,128)S(1)}, u32[]{:S(2)}, u32[]{:S(2)}) %all-to-all-start.1) | async-done | bytes 327712 | tf_op jit(solution)/shard_map/all_to_all | solution.py:56
  97.0 0.2 convolution_multiply_fusion.2
  97.2 0.2 copy.75
  97.4 0.1 reshape.49
  97.6 0.2 convert_element_type.52
  97.8 1.1 convolution_convert_fusion
  98.9 0.1 copy.49
  99.3 17.1 %all_to_all.20 = bf16[32,24,128]{2,1,0:T(8,128)(2,1)S(1)} all-to-all(bf16[32,24,128]{2,1,0:T(8,128)(2,1)S(1)} %bitcast.44), channel_id=1, replica_groups=mesh['dp'=16,'tensor'=32] {'tensor'}, dimensions={0} | all-to-all | bytes 393216 | tf_op jit(solution)/shard_map/all_to_all | solution.py:79
  116.4 0.3 copy.58
  116.7 0.5 copy.52
  117.3 0.4 convolution_multiply_fusion.1
  117.9 0.6 fusion.17
  118.5 0.6 add_convert_fusion
  119.1 1.9 %copy.55 = bf16[128,16,288]{2,1,0:T(8,128)(2,1)} copy(bf16[128,16,288]{0,2,1:T(8,128)(2,1)S(1)} %add_convert_fusion) | data formatting | bytes 2359296 | tf_op jit(solution)/shard_map/convert_element_type | solution.py:95
  121.0 6.7 %all-to-all-start.3 = ((bf16[16,8,16,288]{3,2,1,0:T(8,128)(2,1)}), bf16[16,8,16,288]{3,2,1,0:T(8,128)(2,1)}, u32[]{:S(2)}, u32[]{:S(2)}) async-start(bf16[16,8,16,288]{3,2,1,0:T(8,128)(2,1)} %bitcast.38), calls=%async_computation.3 | async-start | bytes 3145728 | tf_op jit(solution)/shard_map/all_to_all | solution.py:96
  127.7 2.7 %convolution_multiply_fusion = f32[32,128,256]{2,1,0:T(8,128)} fusion(bf16[32,128,16]{1,2,0:T(8,128)(2,1)S(1)} %copy-done.2, bf16[32,16,256]{2,0,1:T(8,128)(2,1)S(1)} %slice.37), kind=kOutput, calls=%fused_computation.7 | convolution fusion | flops 34603008 | bytes 4587520 | tf_op jit(solution)/shard_map/sjr,srd->sjd/dot_general | solution.py:103
  130.5 2.7 %all-gather.2.cloned.1.call-done = bf16[4096,1024]{1,0:T(8,128)(2,1)} async-done(((bf16[128,1024]{1,0:T(8,128)(2,1)}), bf16[4096,1024]{1,0:T(8,128)(2,1)}) %all-gather.2.cloned.1.call-update) | async-done | bytes 8388624 | tf_op jit(solution)/shard_map/all_gather | solution.py:35
  133.2 7.0 %fusion.6 = bf16[4096,256]{1,0:T(8,128)(2,1)} fusion(f32[4096,256]{1,0:T(8,128)} %bitcast.39, bf16[256,1024]{1,0:T(8,128)(2,1)S(1)} %copy-done.6, bf16[4096,1024]{1,0:T(8,128)(2,1)} %all-gather.2.cloned.1.call-done, pred[4096]{0:T(1024)(128)(4,1)S(1)} %broadcast_bitcast_fusion), kind=kOutput, calls=%fused_computation.4 | convolution fusion | flops 2153775104 | bytes 15208448 | tf_op jit(solution)/shard_map/dot_general | solution.py:100
  140.1 26.1 %all-to-all-done.3 = bf16[16,8,16,288]{3,2,1,0:T(8,128)(2,1)} async-done(((bf16[16,8,16,288]{3,2,1,0:T(8,128)(2,1)}), bf16[16,8,16,288]{3,2,1,0:T(8,128)(2,1)}, u32[]{:S(2)}, u32[]{:S(2)}) %all-to-all-start.3) | async-done | bytes 1179680 | tf_op jit(solution)/shard_map/all_to_all | solution.py:96
  166.2 2.0 %slice_reduce_fusion = bf16[8,16,256]{2,1,0:T(8,128)(2,1)} fusion(bf16[16,8,16,288]{3,2,1,0:T(8,128)(2,1)} %all-to-all-done.3), kind=kLoop, calls=%fused_computation.16 | loop fusion | flops 491520 | bytes 1114112 | tf_op jit(solution)/shard_map/reduce_sum | solution.py:106
  168.3 1.8 %slice_reduce_fusion.1 = bf16[8,16,32]{2,1,0:T(8,128)(2,1)} fusion(bf16[16,8,16,288]{3,2,1,0:T(8,128)(2,1)} %all-to-all-done.3), kind=kLoop, calls=%fused_computation.20 | loop fusion | flops 61440 | bytes 139264 | tf_op jit(solution)/shard_map/reduce_sum | solution.py:107
  (34 shorter events, 1.0 us)
Async XLA Ops:
  7.2 54.7 %copy-start = (bf16[4096,256]{1,0:T(8,128)(2,1)S(1)}, bf16[4096,256]{1,0:T(8,128)(2,1)}, u32[]{:S(2)}) copy-start(bf16[4096,256]{1,0:T(8,128)(2,1)} %param.8) | copy-start | bytes 6291460
  7.2 126.0 %all-gather.2.cloned.1.call-start = ((), (), s32[]{:S(2)}) async-start(), calls=%async_computation.4 | async-start | bytes 8650752 | tf_op jit(solution)/shard_map/all_gather | solution.py:35
  8.8 12.4 %copy-start.4 = (s32[512]{0:T(512)S(1)}, s32[512]{0:T(512)}, u32[]{:S(2)}) copy-start(s32[512]{0:T(512)} %param.13) | copy-start | bytes 6148
  8.8 12.4 %copy-start.5 = (s32[128]{0:T(128)S(1)}, s32[128]{0:T(128)}, u32[]{:S(2)}) copy-start(s32[128]{0:T(128)} %param.14) | copy-start | bytes 1540
  10.2 49.6 %all-to-all-start = ((bf16[16,8,16,288]{3,2,1,0:T(8,128)(2,1)}), bf16[16,8,16,288]{3,2,1,0:T(8,128)(2,1)}, u32[]{:S(2)}, u32[]{:S(2)}) async-start(bf16[16,8,16,288]{3,2,1,0:T(8,128)(2,1)} %broadcast_in_dim.54), calls=%async_computation | async-start | bytes 3145728 | tf_op jit(solution)/shard_map/all_to_all | solution.py:45
  61.8 35.1 %copy-start.3 = (bf16[128,1024]{1,0:T(8,128)(2,1)S(1)}, bf16[128,1024]{1,0:T(8,128)(2,1)}, u32[]{:S(2)}) copy-start(bf16[128,1024]{1,0:T(8,128)(2,1)} %param.9) | copy-start | bytes 786436
  63.3 33.6 %all-to-all-start.1 = ((f32[32,16,160]{2,1,0:T(8,128)}), f32[32,16,160]{2,1,0:T(8,128)S(1)}, u32[]{:S(2)}, u32[]{:S(2)}) async-start(f32[32,16,160]{2,1,0:T(8,128)} %pad_maximum_fusion.1), calls=%async_computation.1 | async-start | bytes 1048576 | tf_op jit(solution)/shard_map/all_to_all | solution.py:56
  117.2 0.7 copy-start.1
  121.0 6.7 %copy-start.2 = (bf16[32,128,16]{1,2,0:T(8,128)(2,1)S(1)}, bf16[32,128,16]{1,2,0:T(8,128)(2,1)}, u32[]{:S(2)}) copy-start(bf16[32,128,16]{1,2,0:T(8,128)(2,1)} %copy-done.1) | copy-start | bytes 393220
  121.0 45.2 %all-to-all-start.3 = ((bf16[16,8,16,288]{3,2,1,0:T(8,128)(2,1)}), bf16[16,8,16,288]{3,2,1,0:T(8,128)(2,1)}, u32[]{:S(2)}, u32[]{:S(2)}) async-start(bf16[16,8,16,288]{3,2,1,0:T(8,128)(2,1)} %bitcast.38), calls=%async_computation.3 | async-start | bytes 3145728 | tf_op jit(solution)/shard_map/all_to_all | solution.py:96
  127.7 5.4 %copy-start.6 = (bf16[256,1024]{1,0:T(8,128)(2,1)S(1)}, bf16[256,1024]{1,0:T(8,128)(2,1)}, u32[]{:S(2)}) copy-start(bf16[256,1024]{1,0:T(8,128)(2,1)} %param.10) | copy-start | bytes 1572868
Sparse Core Ops, SparseCore 0:
  11.2 121.9 all-gather.1

commit v6 on v5

--- a/solution.py
+++ b/solution.py
@@ -90,9 +90,11 @@
     grad_round = lax.reduce_precision(seg_grad, exponent_bits=8, mantissa_bits=7)
     grad_high = grad_round.astype(bf16)
     grad_low = (seg_grad - grad_round).astype(bf16)
-    part = jnp.einsum("as,srd->ard", onehot, grad_high, preferred_element_type=f32)
-    part = part + jnp.einsum("as,srd->ard", onehot, grad_low, preferred_element_type=f32)
-    part = part.astype(bf16).reshape(group_count, per_owner, rank_dim, -1)
+    flat_high = grad_high.reshape(seg_group, -1)
+    flat_low = grad_low.reshape(seg_group, -1)
+    part = jnp.dot(onehot, flat_high, preferred_element_type=f32)
+    part = part + jnp.dot(onehot, flat_low, preferred_element_type=f32)
+    part = part.astype(bf16).reshape(group_count, per_owner, -1)
     gathered = lax.all_to_all(part, "dp", 0, 0, tiled=True)
     whole = jnp.where(
         jnp.repeat(seg_live, seg_len)[:, None], whole_raw, jnp.zeros_like(whole_raw)
@@ -103,8 +105,9 @@
     extra = jnp.einsum("sjr,srd->sjd", lowrank, down_seg, preferred_element_type=f32)
     input_grad = (frozen + 2.0 * extra.reshape(tok_group, width_shard)).astype(bf16)
     gathered, input_grad = lax.optimization_barrier((gathered, input_grad))
-    down_grad = jnp.sum(gathered[..., :width_shard].astype(f32), axis=0).astype(bf16)
-    up_grad = jnp.sum(gathered[..., width_shard:].astype(f32), axis=0).astype(bf16)
+    total = jnp.sum(gathered.astype(f32), axis=0).reshape(per_owner, rank_dim, -1)
+    down_grad = total[:, :, :width_shard].astype(bf16)
+    up_grad = total[:, :, width_shard:].astype(bf16)
 
     return (input_grad, down_grad, up_grad)
 

time: 177 us -> 166 us (0.938)
  waiting for transfers between devices: 90.2 us -> 80.8 us
  other arithmetic: 5.99 us -> 2.3 us
    all_to_all x1, waiting for transfers between devices: 26.1 us -> 17 us  [on_device(): gathered = lax.all_to_all(part, 'dp', 0, 0, tiled=True)]
    reduce_sum x2 -> x1, other arithmetic: 3.79 us -> 0.16 us  [on_device(): jnp.sum(gathered.astype(f32), axis=0).reshape(per_owner, rank_dim, -1)]
    convert_element_type x1 -> x0, local copies, waits for them, and re-layouts: 1.92 us -> none  [on_device(): part = part.astype(bf16).reshape(group_count, per_owner, rank_dim, -1)]
where the time goes in v6:
time: 166 us
  waiting for transfers between devices  80.8 us (49%)
  starting transfers between devices  28 us (17%)
  blocking collectives  17.4 us (10%)
  matrix products  15.9 us (10%)
  between operations  14.9 us (9%)
  local copies, waits for them, and re-layouts  6.35 us (4%)
  other arithmetic  2.3 us (1%)
    all_to_all x1, waiting for transfers between devices, on_device(): stores = lax.all_to_all(spread, 'dp', 0, 0, tiled=True)  38.3 us
    all_to_all x1, waiting for transfers between devices, on_device(): first = lax.all_to_all(first, 'tensor', 0, 0, tiled=True)  22.1 us
    all_to_all x1, blocking collectives, on_device(): lax.all_to_all(second, 'tensor', 0, 0, tiled=True).reshape(tensor_size, -1)  17.4 us
    all_to_all x1, waiting for transfers between devices, on_device(): gathered = lax.all_to_all(part, 'dp', 0, 0, tiled=True)  17 us
    all_to_all x1, starting transfers between devices, on_device(): stores = lax.all_to_all(spread, 'dp', 0, 0, tiled=True)  11 us
    all_to_all x1, starting transfers between devices, on_device(): first = lax.all_to_all(first, 'tensor', 0, 0, tiled=True)  10.5 us
    dot_general x1, matrix products, on_device(): lax.dot_general(whole, key_weight, (((1,), (1,)), ((), ())), preferred_el...  7.11 us
    all_to_all x1, starting transfers between devices, on_device(): gathered = lax.all_to_all(part, 'dp', 0, 0, tiled=True)  6.46 us
  transfers between devices with their start and end apart: 4, of which 4 were waited for; matrix products, arithmetic and copies ran while one was open for 13% of the time, Pallas kernels for 0%

profile of v6, /device:TPU:1, one launch (start us, length us, event | category | flops | bytes accessed | tf_op | source)
XLA Modules:
  0.0 165.6 jit_solution(7460826680548958170)
XLA Ops:
  7.2 0.7 all-gather.2.cloned.1.call-update
  7.9 0.9 pad_maximum_fusion.2
  8.8 1.3 broadcast_in_dim.54
  10.2 11.0 %all-to-all-start = ((bf16[16,8,16,288]{3,2,1,0:T(8,128)(2,1)}), bf16[16,8,16,288]{3,2,1,0:T(8,128)(2,1)}, u32[]{:S(2)}, u32[]{:S(2)}) async-start(bf16[16,8,16,288]{3,2,1,0:T(8,128)(2,1)} %broadcast_in_dim.54), calls=%async_computation | async-start | bytes 3145728 | tf_op jit(solution)/shard_map/all_to_all | solution.py:45
  21.2 0.2 select_reduce_fusion
  21.5 38.3 %all-to-all-done = bf16[16,8,16,288]{3,2,1,0:T(8,128)(2,1)} async-done(((bf16[16,8,16,288]{3,2,1,0:T(8,128)(2,1)}), bf16[16,8,16,288]{3,2,1,0:T(8,128)(2,1)}, u32[]{:S(2)}, u32[]{:S(2)}) %all-to-all-start) | async-done | bytes 1179680 | tf_op jit(solution)/shard_map/all_to_all | solution.py:45
  59.8 1.8 %fusion.14 = bf16[32,16,288]{2,0,1:T(8,128)(2,1)S(1)} fusion(bf16[128,16,288]{2,1,0:T(8,128)(2,1)} %bitcast.2, s32[32]{0:T(128)S(1)} %dynamic_slice.3), kind=kOutput, calls=%fused_computation.12 | convolution fusion | flops 37900288 | bytes 1474688 | tf_op jit(solution)/shard_map/sa,ark->srk/dot_general | solution.py:48
  61.8 0.5 copy-done.1
  62.4 0.7 fusion.21
  63.0 0.9 pad_maximum_fusion.1
  63.9 10.5 %all-to-all-start.1 = ((f32[32,16,160]{2,1,0:T(8,128)}), f32[32,16,160]{2,1,0:T(8,128)S(1)}, u32[]{:S(2)}, u32[]{:S(2)}) async-start(f32[32,16,160]{2,1,0:T(8,128)} %pad_maximum_fusion.1), calls=%async_computation.1 | async-start | bytes 1048576 | tf_op jit(solution)/shard_map/all_to_all | solution.py:56
  75.0 22.1 %all-to-all-done.1 = f32[32,16,160]{2,1,0:T(8,128)S(1)} async-done(((f32[32,16,160]{2,1,0:T(8,128)}), f32[32,16,160]{2,1,0:T(8,128)S(1)}, u32[]{:S(2)}, u32[]{:S(2)}) %all-to-all-start.1) | async-done | bytes 327712 | tf_op jit(solution)/shard_map/all_to_all | solution.py:56
  97.4 0.2 copy.60
  97.8 0.2 convert_element_type.55
  97.9 0.2 convolution_convert_fusion
  98.5 17.4 %all_to_all.20 = bf16[32,24,128]{2,1,0:T(8,128)(2,1)S(1)} all-to-all(bf16[32,24,128]{2,1,0:T(8,128)(2,1)S(1)} %bitcast.40), channel_id=1, replica_groups=mesh['dp'=16,'tensor'=32] {'tensor'}, dimensions={0} | all-to-all | bytes 393216 | tf_op jit(solution)/shard_map/all_to_all | solution.py:79
  115.9 0.3 copy.47
  116.1 0.5 copy.44
  116.8 0.5 copy-done.3
  117.3 0.4 convolution_multiply_fusion.1
  117.8 0.3 concatenate.18
  118.1 0.4 fusion.19
  118.6 1.5 fusion.4
  120.1 6.5 %all-to-all-start.3 = ((bf16[16,8,4608]{2,1,0:T(8,128)(2,1)}), bf16[16,8,4608]{2,1,0:T(8,128)(2,1)S(1)}, u32[]{:S(2)}, u32[]{:S(2)}) async-start(bf16[16,8,4608]{2,1,0:T(8,128)(2,1)} %fusion.4), calls=%async_computation.3 | async-start | bytes 2359296 | tf_op jit(solution)/shard_map/all_to_all | solution.py:98
  126.7 3.6 %convolution_multiply_fusion = f32[32,128,256]{2,1,0:T(8,128)} fusion(bf16[32,128,16]{1,2,0:T(8,128)(2,1)} %copy-done.3, bf16[32,16,256]{2,0,1:T(8,128)(2,1)S(1)} %copy-done.2), kind=kOutput, calls=%fused_computation.9 | convolution fusion | flops 34603008 | bytes 4587520 | tf_op jit(solution)/shard_map/sjr,srd->sjd/dot_general | solution.py:105
  130.3 2.7 %all-gather.2.cloned.1.call-done = bf16[4096,1024]{1,0:T(8,128)(2,1)} async-done(((bf16[128,1024]{1,0:T(8,128)(2,1)}), bf16[4096,1024]{1,0:T(8,128)(2,1)}) %all-gather.2.cloned.1.call-update) | async-done | bytes 8388624 | tf_op jit(solution)/shard_map/all_gather | solution.py:35
  133.0 7.1 %fusion.8 = bf16[4096,256]{1,0:T(8,128)(2,1)} fusion(f32[4096,256]{1,0:T(8,128)} %bitcast.35, bf16[256,1024]{1,0:T(8,128)(2,1)} %param.10, bf16[4096,1024]{1,0:T(8,128)(2,1)} %all-gather.2.cloned.1.call-done, pred[4096]{0:T(1024)(128)(4,1)S(1)} %broadcast_bitcast_fusion), kind=kOutput, calls=%fused_computation.7 | convolution fusion | flops 2153775104 | bytes 15208448 | tf_op jit(solution)/shard_map/dot_general | solution.py:102
  140.1 17.0 %all-to-all-done.3 = bf16[16,8,4608]{2,1,0:T(8,128)(2,1)S(1)} async-done(((bf16[16,8,4608]{2,1,0:T(8,128)(2,1)}), bf16[16,8,4608]{2,1,0:T(8,128)(2,1)S(1)}, u32[]{:S(2)}, u32[]{:S(2)}) %all-to-all-start.3) | async-done | bytes 1179680 | tf_op jit(solution)/shard_map/all_to_all | solution.py:98
  157.1 0.2 reduce
  157.3 0.2 reshape.63
  157.5 0.6 slice.46
  158.1 0.6 slice.47
  (36 shorter events, 1.5 us)
Async XLA Ops:
  7.2 54.7 %copy-start = (bf16[4096,256]{1,0:T(8,128)(2,1)S(1)}, bf16[4096,256]{1,0:T(8,128)(2,1)}, u32[]{:S(2)}) copy-start(bf16[4096,256]{1,0:T(8,128)(2,1)} %param.8) | copy-start | bytes 6291460
  7.2 125.8 %all-gather.2.cloned.1.call-start = ((), (), s32[]{:S(2)}) async-start(), calls=%async_computation.4 | async-start | bytes 8650752 | tf_op jit(solution)/shard_map/all_gather | solution.py:35
  8.8 12.4 %copy-start.5 = (s32[512]{0:T(512)S(1)}, s32[512]{0:T(512)}, u32[]{:S(2)}) copy-start(s32[512]{0:T(512)} %param.13) | copy-start | bytes 6148
  8.8 12.4 %copy-start.6 = (s32[128]{0:T(128)S(1)}, s32[128]{0:T(128)}, u32[]{:S(2)}) copy-start(s32[128]{0:T(128)} %param.14) | copy-start | bytes 1540
  10.2 49.6 %all-to-all-start = ((bf16[16,8,16,288]{3,2,1,0:T(8,128)(2,1)}), bf16[16,8,16,288]{3,2,1,0:T(8,128)(2,1)}, u32[]{:S(2)}, u32[]{:S(2)}) async-start(bf16[16,8,16,288]{3,2,1,0:T(8,128)(2,1)} %broadcast_in_dim.54), calls=%async_computation | async-start | bytes 3145728 | tf_op jit(solution)/shard_map/all_to_all | solution.py:45
  61.6 0.7 copy-start.1
  62.3 34.8 %copy-start.4 = (bf16[128,1024]{1,0:T(8,128)(2,1)S(1)}, bf16[128,1024]{1,0:T(8,128)(2,1)}, u32[]{:S(2)}) copy-start(bf16[128,1024]{1,0:T(8,128)(2,1)} %param.9) | copy-start | bytes 786436
  63.9 33.2 %all-to-all-start.1 = ((f32[32,16,160]{2,1,0:T(8,128)}), f32[32,16,160]{2,1,0:T(8,128)S(1)}, u32[]{:S(2)}, u32[]{:S(2)}) async-start(f32[32,16,160]{2,1,0:T(8,128)} %pad_maximum_fusion.1), calls=%async_computation.1 | async-start | bytes 1048576 | tf_op jit(solution)/shard_map/all_to_all | solution.py:56
  116.7 0.7 copy-start.3
  118.6 8.1 %copy-start.2 = (bf16[32,16,256]{2,0,1:T(8,128)(2,1)S(1)}, bf16[32,16,256]{2,0,1:T(8,128)(2,1)}, u32[]{:S(2)}) copy-start(bf16[32,16,256]{2,0,1:T(8,128)(2,1)} %copy-done.1) | copy-start | bytes 786436
  120.1 37.0 %all-to-all-start.3 = ((bf16[16,8,4608]{2,1,0:T(8,128)(2,1)}), bf16[16,8,4608]{2,1,0:T(8,128)(2,1)S(1)}, u32[]{:S(2)}, u32[]{:S(2)}) async-start(bf16[16,8,4608]{2,1,0:T(8,128)(2,1)} %fusion.4), calls=%async_computation.3 | async-start | bytes 2359296 | tf_op jit(solution)/shard_map/all_to_all | solution.py:98
Sparse Core Ops, SparseCore 0:
  11.2 121.8 all-gather.1

commit v7 on v6

--- a/solution.py
+++ b/solution.py
@@ -40,20 +40,20 @@
     seg_slot = lax.dynamic_slice_in_dim(every_slot, group_index * seg_group, seg_group)
     seg_live = jnp.arange(seg_group, dtype=jnp.int32) < live_segments[0]
 
-    local_store = jnp.concatenate([adapter_down, adapter_up], axis=2)
+    local_store = jnp.concatenate([adapter_down, adapter_up], axis=2).reshape(per_owner, -1)
     spread = jnp.broadcast_to(local_store[None], (group_count,) + local_store.shape)
-    stores = lax.all_to_all(spread, "dp", 0, 0, tiled=True)
-    stores = stores.reshape((adapters,) + local_store.shape[1:])
+    stores = lax.all_to_all(spread, "dp", 0, 0, tiled=True).reshape(adapters, -1)
     choose = (seg_slot[:, None] == slot_ids[None, :]).astype(bf16)
-    seg_store = jnp.einsum("sa,ark->srk", choose, stores, preferred_element_type=f32)
-    seg_store = seg_store.astype(bf16)
+    seg_store = jnp.dot(choose, stores, preferred_element_type=f32).astype(bf16)
+    seg_store = seg_store.reshape(seg_group, rank_dim, width_shard + key_shard)
     down_seg = seg_store[:, :, :width_shard]
     up_seg = seg_store[:, :, width_shard:]
 
     input_seg = layer_input.reshape(seg_group, seg_len, width_shard)
     proj_part = jnp.einsum("sjd,srd->srj", input_seg, down_seg, preferred_element_type=f32)
-    first = jnp.concatenate([proj_part, up_seg.astype(f32)], axis=2)
+    first = jnp.concatenate([proj_part, up_seg.astype(f32)], axis=2).reshape(seg_group, -1)
     first = lax.all_to_all(first, "tensor", 0, 0, tiled=True)
+    first = first.reshape(tensor_size, rank_dim, seg_len + key_shard)
     projected_own = jnp.sum(first[:, :, :seg_len], axis=0).astype(bf16)
     up_own = jnp.transpose(first[:, :, seg_len:], (1, 0, 2)).reshape(rank_dim, key_width)
     up_own = up_own.astype(bf16)

time: 166 us -> 149 us (0.90)
  waiting for transfers between devices: 80.8 us -> 63.8 us
  local copies, waits for them, and re-layouts: 6.35 us -> 8.73 us
    all_to_all x1, waiting for transfers between devices: 22.1 us -> 13.1 us  [on_device(): first = lax.all_to_all(first, 'tensor', 0, 0, tiled=True)]
    all_gather x1, waiting for transfers between devices: 2.73 us -> 11.5 us  [on_device(): whole_raw = lax.all_gather(output_grad, 'tensor', axis=0, tiled=True)]
    all_to_all x1, waiting for transfers between devices: 17 us -> 8.27 us  [on_device(): gathered = lax.all_to_all(part, 'dp', 0, 0, tiled=True)]
    all_to_all x1, waiting for transfers between devices: 38.3 us -> 30.3 us  [on_device(): lax.all_to_all(spread, 'dp', 0, 0, tiled=True).reshape(adapters, -1)]
    reshape x0 -> x2, local copies, waits for them, and re-layouts: none -> 1.81 us  [the longest x1 1.52 us: on_device(): seg_store = seg_store.reshape(seg_group, rank_dim, width_shard + key_shard)]
  transfers between devices with their start and end apart: 4 -> 4, of which waited for: 4 -> 4; matrix products, arithmetic and copies ran while one was open for 13% -> 15% of each run, Pallas kernels for 0% -> 0%
where the time goes in v7:
time: 149 us
  waiting for transfers between devices  63.8 us (43%)
  starting transfers between devices  26.8 us (18%)
  blocking collectives  16.9 us (11%)
  matrix products  15.2 us (10%)
  between operations  14.9 us (10%)
  local copies, waits for them, and re-layouts  8.73 us (6%)
  other arithmetic  2.27 us (2%)
    all_to_all x1, waiting for transfers between devices, on_device(): lax.all_to_all(spread, 'dp', 0, 0, tiled=True).reshape(adapters, -1)  30.3 us
    all_to_all x1, blocking collectives, on_device(): lax.all_to_all(second, 'tensor', 0, 0, tiled=True).reshape(tensor_size, -1)  16.9 us
    all_to_all x1, waiting for transfers between devices, on_device(): first = lax.all_to_all(first, 'tensor', 0, 0, tiled=True)  13.1 us
    all_gather x1, waiting for transfers between devices, on_device(): whole_raw = lax.all_gather(output_grad, 'tensor', axis=0, tiled=True)  11.5 us
    all_to_all x1, starting transfers between devices, on_device(): first = lax.all_to_all(first, 'tensor', 0, 0, tiled=True)  11.1 us
    all_to_all x1, starting transfers between devices, on_device(): lax.all_to_all(spread, 'dp', 0, 0, tiled=True).reshape(adapters, -1)  10.4 us
    all_to_all x1, waiting for transfers between devices, on_device(): gathered = lax.all_to_all(part, 'dp', 0, 0, tiled=True)  8.27 us
    dot_general x1, matrix products, on_device(): lax.dot_general(whole, key_weight, (((1,), (1,)), ((), ())), preferred_el...  7.11 us
  transfers between devices with their start and end apart: 4, of which 4 were waited for; matrix products, arithmetic and copies ran while one was open for 15% of the time, Pallas kernels for 0%

profile of v7, /device:TPU:1, one launch (start us, length us, event | category | flops | bytes accessed | tf_op | source)
XLA Modules:
  0.0 148.7 jit_solution(4439874792775974399)
XLA Ops:
  7.2 0.7 all-gather.2.cloned.1.call-update
  7.9 0.9 pad_maximum_fusion.2
  9.0 1.1 broadcast_in_dim.56
  10.0 10.4 %all-to-all-start = ((bf16[16,8,4608]{2,1,0:T(8,128)(2,1)}), bf16[16,8,4608]{2,1,0:T(8,128)(2,1)S(1)}, u32[]{:S(2)}, u32[]{:S(2)}) async-start(bf16[16,8,4608]{2,1,0:T(8,128)(2,1)} %broadcast_in_dim.56), calls=%async_computation | async-start | bytes 2359296 | tf_op jit(solution)/shard_map/all_to_all | solution.py:45
  20.4 0.2 select_reduce_fusion
  20.7 30.3 %all-to-all-done = bf16[16,8,4608]{2,1,0:T(8,128)(2,1)S(1)} async-done(((bf16[16,8,4608]{2,1,0:T(8,128)(2,1)}), bf16[16,8,4608]{2,1,0:T(8,128)(2,1)S(1)}, u32[]{:S(2)}, u32[]{:S(2)}) %all-to-all-start) | async-done | bytes 1179680 | tf_op jit(solution)/shard_map/all_to_all | solution.py:45
  51.0 1.1 convolution_convert_fusion
  52.1 1.5 %reshape.65 = bf16[32,16,288]{2,1,0:T(8,128)(2,1)S(1)} reshape(bf16[32,4608]{1,0:T(8,128)(2,1)} %convolution_convert_fusion) | data formatting | bytes 589824 | tf_op jit(solution)/shard_map/reshape | solution.py:48
  53.7 0.6 fusion.17
  54.4 1.4 all_to_all.20
  55.8 11.1 %all-to-all-start.1 = ((f32[32,1,2560]{2,1,0:T(1,128)}), f32[32,1,2560]{2,1,0:T(1,128)S(1)}, u32[]{:S(2)}, u32[]{:S(2)}) async-start(f32[32,1,2560]{2,1,0:T(1,128)} %all_to_all.20), calls=%async_computation.1 | async-start | bytes 655360 | tf_op jit(solution)/shard_map/all_to_all | solution.py:55
  67.5 13.1 %all-to-all-done.1 = f32[32,1,2560]{2,1,0:T(1,128)S(1)} async-done(((f32[32,1,2560]{2,1,0:T(1,128)}), f32[32,1,2560]{2,1,0:T(1,128)S(1)}, u32[]{:S(2)}, u32[]{:S(2)}) %all-to-all-start.1) | async-done | bytes 327712 | tf_op jit(solution)/shard_map/all_to_all | solution.py:55
  80.6 0.8 reduce.1
  81.4 0.3 reshape.67
  82.4 0.2 convert_element_type.55
  82.6 0.2 convolution_convert_fusion.1
  83.1 16.9 %all_to_all.25 = bf16[32,24,128]{2,1,0:T(8,128)(2,1)S(1)} all-to-all(bf16[32,24,128]{2,1,0:T(8,128)(2,1)S(1)} %bitcast.39), channel_id=1, replica_groups=mesh['dp'=16,'tensor'=32] {'tensor'}, dimensions={0} | all-to-all | bytes 393216 | tf_op jit(solution)/shard_map/all_to_all | solution.py:79
  100.1 0.3 copy.40
  100.3 0.5 copy.38
  101.0 0.5 copy-done.2
  101.5 0.4 convolution_multiply_fusion.1
  101.9 0.3 concatenate.18
  102.3 0.4 fusion.15
  102.7 1.6 %fusion.4 = bf16[16,8,4608]{2,1,0:T(8,128)(2,1)} fusion(f32[128,4608]{1,0:T(8,128)S(1)} %fusion.15, f32[32,4608]{1,0:T(8,128)S(1)} %concatenate.18, s32[32]{0:T(128)S(1)} %dynamic_slice.3), kind=kOutput, calls=%fused_computation.5 | convolution fusion | flops 39374848 | bytes 4128896 | tf_op jit(solution)/shard_map/dot_general | solution.py:96
  104.3 5.3 %all-to-all-start.3 = ((bf16[16,8,4608]{2,1,0:T(8,128)(2,1)}), bf16[16,8,4608]{2,1,0:T(8,128)(2,1)S(1)}, u32[]{:S(2)}, u32[]{:S(2)}) async-start(bf16[16,8,4608]{2,1,0:T(8,128)(2,1)} %fusion.4), calls=%async_computation.3 | async-start | bytes 2359296 | tf_op jit(solution)/shard_map/all_to_all | solution.py:98
  109.7 3.7 %convolution_multiply_fusion = f32[32,128,256]{2,1,0:T(8,128)} fusion(bf16[32,128,16]{1,2,0:T(8,128)(2,1)S(1)} %copy-done.3, bf16[32,16,288]{2,1,0:T(8,128)(2,1)} %copy-done.1), kind=kOutput, calls=%fused_computation.10 | convolution fusion | flops 34603008 | bytes 4587520 | tf_op jit(solution)/shard_map/sjr,srd->sjd/dot_general | solution.py:105
  113.4 11.5 %all-gather.2.cloned.1.call-done = bf16[4096,1024]{1,0:T(8,128)(2,1)} async-done(((bf16[128,1024]{1,0:T(8,128)(2,1)}), bf16[4096,1024]{1,0:T(8,128)(2,1)}) %all-gather.2.cloned.1.call-update) | async-done | bytes 8388624 | tf_op jit(solution)/shard_map/all_gather | solution.py:35
  124.8 7.1 %fusion.8 = bf16[4096,256]{1,0:T(8,128)(2,1)} fusion(f32[4096,256]{1,0:T(8,128)} %bitcast.34, bf16[256,1024]{1,0:T(8,128)(2,1)} %param.10, bf16[4096,1024]{1,0:T(8,128)(2,1)} %all-gather.2.cloned.1.call-done, pred[4096]{0:T(1024)(128)(4,1)S(1)} %broadcast_bitcast_fusion), kind=kOutput, calls=%fused_computation.8 | convolution fusion | flops 2153775104 | bytes 15208448 | tf_op jit(solution)/shard_map/dot_general | solution.py:102
  132.0 8.3 %all-to-all-done.3 = bf16[16,8,4608]{2,1,0:T(8,128)(2,1)S(1)} async-done(((bf16[16,8,4608]{2,1,0:T(8,128)(2,1)}), bf16[16,8,4608]{2,1,0:T(8,128)(2,1)S(1)}, u32[]{:S(2)}, u32[]{:S(2)}) %all-to-all-start.3) | async-done | bytes 1179680 | tf_op jit(solution)/shard_map/all_to_all | solution.py:98
  140.4 0.2 reshape.76
  140.6 0.6 slice.46
  141.2 0.6 slice.47
  (39 shorter events, 1.8 us)
Async XLA Ops:
  7.2 46.5 %copy-start = (bf16[4096,256]{1,0:T(8,128)(2,1)S(1)}, bf16[4096,256]{1,0:T(8,128)(2,1)}, u32[]{:S(2)}) copy-start(bf16[4096,256]{1,0:T(8,128)(2,1)} %param.8) | copy-start | bytes 6291460
  7.2 13.2 %copy-start.5 = (s32[512]{0:T(512)S(1)}, s32[512]{0:T(512)}, u32[]{:S(2)}) copy-start(s32[512]{0:T(512)} %param.13) | copy-start | bytes 6148
  7.2 13.2 %copy-start.6 = (s32[128]{0:T(128)S(1)}, s32[128]{0:T(128)}, u32[]{:S(2)}) copy-start(s32[128]{0:T(128)} %param.14) | copy-start | bytes 1540
  7.2 117.6 %all-gather.2.cloned.1.call-start = ((), (), s32[]{:S(2)}) async-start(), calls=%async_computation.4 | async-start | bytes 8650752 | tf_op jit(solution)/shard_map/all_gather | solution.py:35
  10.0 41.0 %all-to-all-start = ((bf16[16,8,4608]{2,1,0:T(8,128)(2,1)}), bf16[16,8,4608]{2,1,0:T(8,128)(2,1)S(1)}, u32[]{:S(2)}, u32[]{:S(2)}) async-start(bf16[16,8,4608]{2,1,0:T(8,128)(2,1)} %broadcast_in_dim.56), calls=%async_computation | async-start | bytes 2359296 | tf_op jit(solution)/shard_map/all_to_all | solution.py:45
  53.6 2.2 %copy-start.1 = (bf16[32,16,288]{2,1,0:T(8,128)(2,1)}, bf16[32,16,288]{2,1,0:T(8,128)(2,1)S(1)}, u32[]{:S(2)}) copy-start(bf16[32,16,288]{2,1,0:T(8,128)(2,1)S(1)} %reshape.65) | copy-start | bytes 884740
  54.3 27.4 %copy-start.4 = (bf16[128,1024]{1,0:T(8,128)(2,1)S(1)}, bf16[128,1024]{1,0:T(8,128)(2,1)}, u32[]{:S(2)}) copy-start(bf16[128,1024]{1,0:T(8,128)(2,1)} %param.9) | copy-start | bytes 786436
  55.8 24.9 %all-to-all-start.1 = ((f32[32,1,2560]{2,1,0:T(1,128)}), f32[32,1,2560]{2,1,0:T(1,128)S(1)}, u32[]{:S(2)}, u32[]{:S(2)}) async-start(f32[32,1,2560]{2,1,0:T(1,128)} %all_to_all.20), calls=%async_computation.1 | async-start | bytes 655360 | tf_op jit(solution)/shard_map/all_to_all | solution.py:55
  100.8 0.6 copy-start.2
  102.7 7.0 %copy-start.3 = (bf16[32,128,16]{1,2,0:T(8,128)(2,1)S(1)}, bf16[32,128,16]{1,2,0:T(8,128)(2,1)}, u32[]{:S(2)}) copy-start(bf16[32,128,16]{1,2,0:T(8,128)(2,1)} %copy-done.2) | copy-start | bytes 393220
  104.3 35.9 %all-to-all-start.3 = ((bf16[16,8,4608]{2,1,0:T(8,128)(2,1)}), bf16[16,8,4608]{2,1,0:T(8,128)(2,1)S(1)}, u32[]{:S(2)}, u32[]{:S(2)}) async-start(bf16[16,8,4608]{2,1,0:T(8,128)(2,1)} %fusion.4), calls=%async_computation.3 | async-start | bytes 2359296 | tf_op jit(solution)/shard_map/all_to_all | solution.py:98
Sparse Core Ops, SparseCore 0:
  11.2 113.5 all-gather.1

commit v8 on v7

--- a/solution.py
+++ b/solution.py
@@ -32,7 +32,9 @@
     f32 = jnp.float32
     bf16 = jnp.bfloat16
 
-    whole_raw = lax.all_gather(output_grad, "tensor", axis=0, tiled=True)
+    half_key = key_width // 2
+    whole_first = lax.all_gather(output_grad[:, :half_key], "tensor", axis=0, tiled=True)
+    whole_second = lax.all_gather(output_grad[:, half_key:], "tensor", axis=0, tiled=True)
 
     slot_ids = jnp.arange(adapters, dtype=jnp.int32)
     lookup = segment_adapter[:, None] == slot_ids[None, :]
@@ -96,12 +98,17 @@
     part = part + jnp.dot(onehot, flat_low, preferred_element_type=f32)
     part = part.astype(bf16).reshape(group_count, per_owner, -1)
     gathered = lax.all_to_all(part, "dp", 0, 0, tiled=True)
-    whole = jnp.where(
-        jnp.repeat(seg_live, seg_len)[:, None], whole_raw, jnp.zeros_like(whole_raw)
-    )
-    frozen = lax.dot_general(
-        whole, key_weight, (((1,), (1,)), ((), ())), preferred_element_type=f32
-    )
+    tok_live = jnp.repeat(seg_live, seg_len)[:, None]
+    frozen = None
+    for rows, weight in (
+        (whole_first, key_weight[:, :half_key]),
+        (whole_second, key_weight[:, half_key:]),
+    ):
+        rows = jnp.where(tok_live, rows, jnp.zeros_like(rows))
+        step = lax.dot_general(
+            rows, weight, (((1,), (1,)), ((), ())), preferred_element_type=f32
+        )
+        frozen = step if frozen is None else frozen + step
     extra = jnp.einsum("sjr,srd->sjd", lowrank, down_seg, preferred_element_type=f32)
     input_grad = (frozen + 2.0 * extra.reshape(tok_group, width_shard)).astype(bf16)
     gathered, input_grad = lax.optimization_barrier((gathered, input_grad))

time: 149 us -> 211 us (1.42); the launches traced: 149 us -> 208 us
  waiting for transfers between devices: 63.8 us -> 118 us
  matrix products: 15.2 us -> 19.1 us
    all_gather x1 -> x2, waiting for transfers between devices: 11.5 us -> 72.3 us  [the longest x1 72.3 us: on_device(): lax.all_gather(output_grad[:, half_key:], 'tensor', axis=0, tiled=True)]
    all_to_all x1, waiting for transfers between devices: 8.27 us -> 0.01 us  [on_device(): gathered = lax.all_to_all(part, 'dp', 0, 0, tiled=True)]
    dot_general x1 -> x2, matrix products: 7.11 us -> 11 us  [on_device(): lax.dot_general(rows, weight, (((1,), (1,)), ((), ())), preferred_element...]
  transfers between devices with their start and end apart: 4 -> 5, of which waited for: 4 -> 3; matrix products, arithmetic and copies ran while one was open for 15% -> 13% of each run, Pallas kernels for 0% -> 0%
where the time goes in v8:
time: 211 us; the launch traced here: 208 us
  waiting for transfers between devices  118 us (56%)
  starting transfers between devices  26.8 us (13%)
  matrix products  19.1 us (9%)
  blocking collectives  17.1 us (8%)
  between operations  14.9 us (7%)
  local copies, waits for them, and re-layouts  10.6 us (5%)
  other arithmetic  2.25 us (1%)
    all_gather x1, waiting for transfers between devices, on_device(): lax.all_gather(output_grad[:, half_key:], 'tensor', axis=0, tiled=True)  72.3 us
    all_to_all x1, waiting for transfers between devices, on_device(): lax.all_to_all(spread, 'dp', 0, 0, tiled=True).reshape(adapters, -1)  30.3 us
    all_to_all x1, blocking collectives, on_device(): lax.all_to_all(second, 'tensor', 0, 0, tiled=True).reshape(tensor_size, -1)  17.1 us
    all_to_all x1, waiting for transfers between devices, on_device(): first = lax.all_to_all(first, 'tensor', 0, 0, tiled=True)  14.3 us
    all_to_all x1, starting transfers between devices, on_device(): first = lax.all_to_all(first, 'tensor', 0, 0, tiled=True)  11.1 us
    dot_general x2, matrix products, on_device(): lax.dot_general(rows, weight, (((1,), (1,)), ((), ())), preferred_element...  11 us
    all_to_all x1, starting transfers between devices, on_device(): lax.all_to_all(spread, 'dp', 0, 0, tiled=True).reshape(adapters, -1)  10.4 us
    all_to_all x1, starting transfers between devices, on_device(): gathered = lax.all_to_all(part, 'dp', 0, 0, tiled=True)  5.24 us
  transfers between devices with their start and end apart: 5, of which 3 were waited for; matrix products, arithmetic and copies ran while one was open for 13% of the time, Pallas kernels for 0%

profile of v8, /device:TPU:1, one launch (start us, length us, event | category | flops | bytes accessed | tf_op | source)
XLA Modules:
  0.0 208.3 jit_solution(13261729175844528475)
XLA Ops:
  7.2 1.8 fusion.32
  9.2 0.7 all-gather.5.cloned.1.call-update
  9.9 0.9 pad_maximum_fusion.2
  10.9 1.1 broadcast_in_dim.56
  12.0 10.4 %all-to-all-start = ((bf16[16,8,4608]{2,1,0:T(8,128)(2,1)}), bf16[16,8,4608]{2,1,0:T(8,128)(2,1)S(1)}, u32[]{:S(2)}, u32[]{:S(2)}) async-start(bf16[16,8,4608]{2,1,0:T(8,128)(2,1)} %broadcast_in_dim.56), calls=%async_computation | async-start | bytes 2359296 | tf_op jit(solution)/shard_map/all_to_all | solution.py:47
  22.4 0.2 select_reduce_fusion
  22.7 30.3 %all-to-all-done = bf16[16,8,4608]{2,1,0:T(8,128)(2,1)S(1)} async-done(((bf16[16,8,4608]{2,1,0:T(8,128)(2,1)}), bf16[16,8,4608]{2,1,0:T(8,128)(2,1)S(1)}, u32[]{:S(2)}, u32[]{:S(2)}) %all-to-all-start) | async-done | bytes 1179680 | tf_op jit(solution)/shard_map/all_to_all | solution.py:47
  52.9 1.1 convolution_convert_fusion
  54.0 1.5 reshape.65
  55.6 0.7 fusion.18
  56.3 1.4 all_to_all.20
  57.7 11.1 %all-to-all-start.1 = ((f32[32,1,2560]{2,1,0:T(1,128)}), f32[32,1,2560]{2,1,0:T(1,128)S(1)}, u32[]{:S(2)}, u32[]{:S(2)}) async-start(f32[32,1,2560]{2,1,0:T(1,128)} %all_to_all.20), calls=%async_computation.1 | async-start | bytes 655360 | tf_op jit(solution)/shard_map/all_to_all | solution.py:57
  69.4 14.3 %all-to-all-done.1 = f32[32,1,2560]{2,1,0:T(1,128)S(1)} async-done(((f32[32,1,2560]{2,1,0:T(1,128)}), f32[32,1,2560]{2,1,0:T(1,128)S(1)}, u32[]{:S(2)}, u32[]{:S(2)}) %all-to-all-start.1) | async-done | bytes 327712 | tf_op jit(solution)/shard_map/all_to_all | solution.py:57
  83.8 0.8 reduce.1
  84.5 0.3 reshape.67
  85.5 0.2 convert_element_type.55
  86.2 17.1 %all_to_all.25 = bf16[32,24,128]{2,1,0:T(8,128)(2,1)S(1)} all-to-all(bf16[32,24,128]{2,1,0:T(8,128)(2,1)S(1)} %bitcast.38), channel_id=1, replica_groups=mesh['dp'=16,'tensor'=32] {'tensor'}, dimensions={0} | all-to-all | bytes 393216 | tf_op jit(solution)/shard_map/all_to_all | solution.py:81
  103.4 0.3 copy.40
  103.7 0.5 copy.38
  104.3 0.5 copy-done.2
  104.8 0.4 convolution_multiply_fusion.1
  105.3 0.3 concatenate.18
  105.6 0.4 fusion.14
  106.1 1.5 fusion.1
  107.6 5.2 %all-to-all-start.3 = ((bf16[16,8,4608]{2,1,0:T(8,128)(2,1)}), bf16[16,8,4608]{2,1,0:T(8,128)(2,1)S(1)}, u32[]{:S(2)}, u32[]{:S(2)}) async-start(bf16[16,8,4608]{2,1,0:T(8,128)(2,1)} %fusion.1), calls=%async_computation.3 | async-start | bytes 2359296 | tf_op jit(solution)/shard_map/all_to_all | solution.py:100
  112.9 3.7 %convolution_multiply_fusion = f32[32,128,256]{2,1,0:T(8,128)} fusion(bf16[32,128,16]{1,2,0:T(8,128)(2,1)S(1)} %copy-done.3, bf16[32,16,288]{2,1,0:T(8,128)(2,1)} %copy-done.1), kind=kOutput, calls=%fused_computation.12 | convolution fusion | flops 34603008 | bytes 4587520 | tf_op jit(solution)/shard_map/sjr,srd->sjd/dot_general | solution.py:112
  116.6 4.5 %fusion.5 = f32[4096,256]{1,0:T(8,128)} fusion(bf16[4096,512]{1,0:T(8,128)(2,1)} %all-gather.3.cloned.1.call-done, pred[4096]{0:T(1024)(128)(4,1)S(1)} %broadcast_bitcast_fusion, bf16[256,1024]{1,0:T(8,128)(2,1)} %param.10), kind=kOutput, calls=%fused_computation.8 | convolution fusion | flops 1075838976 | bytes 8654848 | tf_op jit(solution)/shard_map/dot_general | solution.py:108
  121.0 72.3 %all-gather.5.cloned.1.call-done = bf16[4096,512]{1,0:T(8,128)(2,1)} async-done(((bf16[128,512]{1,0:T(8,128)(2,1)}), bf16[4096,512]{1,0:T(8,128)(2,1)}) %all-gather.5.cloned.1.call-update) | async-done | bytes 4194320 | tf_op jit(solution)/shard_map/all_gather | solution.py:37
  193.3 6.5 %fusion.3 = bf16[4096,256]{1,0:T(8,128)(2,1)} fusion(f32[4096,256]{1,0:T(8,128)} %bitcast.33, f32[4096,256]{1,0:T(8,128)} %fusion.5, bf16[4096,512]{1,0:T(8,128)(2,1)} %all-gather.5.cloned.1.call-done, pred[4096]{0:T(1024)(128)(4,1)S(1)} %broadcast_bitcast_fusion, bf16[256,1024]{1,0:T(8,128)(2,1)} %param.10), kind=kOutput, calls=%fused_computation.6 | convolution fusion | flops 1078984704 | bytes 14946304 | tf_op jit(solution)/shard_map/dot_general | solution.py:108
  200.0 0.2 reshape.76
  200.2 0.6 slice.62
  200.8 0.6 slice.63
  (44 shorter events, 2.0 us)
Async XLA Ops:
  7.2 48.4 %copy-start = (bf16[4096,256]{1,0:T(8,128)(2,1)S(1)}, bf16[4096,256]{1,0:T(8,128)(2,1)}, u32[]{:S(2)}) copy-start(bf16[4096,256]{1,0:T(8,128)(2,1)} %param.8) | copy-start | bytes 6291460
  7.2 15.2 %copy-start.5 = (s32[512]{0:T(512)S(1)}, s32[512]{0:T(512)}, u32[]{:S(2)}) copy-start(s32[512]{0:T(512)} %param.13) | copy-start | bytes 6148
  7.2 15.2 %copy-start.6 = (s32[128]{0:T(128)S(1)}, s32[128]{0:T(128)}, u32[]{:S(2)}) copy-start(s32[128]{0:T(128)} %param.14) | copy-start | bytes 1540
  7.2 109.4 %all-gather.3.cloned.1.call-start = ((), (), s32[]{:S(2)}) async-start(), calls=%async_computation.4 | async-start | bytes 4325376 | tf_op jit(solution)/shard_map/all_gather | solution.py:36
  9.1 184.2 %all-gather.5.cloned.1.call-start = ((), (), s32[]{:S(2)}) async-start(), calls=%async_computation.5 | async-start | bytes 4325376 | tf_op jit(solution)/shard_map/all_gather | solution.py:37
  12.0 41.0 %all-to-all-start = ((bf16[16,8,4608]{2,1,0:T(8,128)(2,1)}), bf16[16,8,4608]{2,1,0:T(8,128)(2,1)S(1)}, u32[]{:S(2)}, u32[]{:S(2)}) async-start(bf16[16,8,4608]{2,1,0:T(8,128)(2,1)} %broadcast_in_dim.56), calls=%async_computation | async-start | bytes 2359296 | tf_op jit(solution)/shard_map/all_to_all | solution.py:47
  55.5 2.2 %copy-start.1 = (bf16[32,16,288]{2,1,0:T(8,128)(2,1)}, bf16[32,16,288]{2,1,0:T(8,128)(2,1)S(1)}, u32[]{:S(2)}) copy-start(bf16[32,16,288]{2,1,0:T(8,128)(2,1)S(1)} %reshape.65) | copy-start | bytes 884740
  56.2 28.6 %copy-start.4 = (bf16[128,1024]{1,0:T(8,128)(2,1)S(1)}, bf16[128,1024]{1,0:T(8,128)(2,1)}, u32[]{:S(2)}) copy-start(bf16[128,1024]{1,0:T(8,128)(2,1)} %param.9) | copy-start | bytes 786436
  57.7 26.1 %all-to-all-start.1 = ((f32[32,1,2560]{2,1,0:T(1,128)}), f32[32,1,2560]{2,1,0:T(1,128)S(1)}, u32[]{:S(2)}, u32[]{:S(2)}) async-start(f32[32,1,2560]{2,1,0:T(1,128)} %all_to_all.20), calls=%async_computation.1 | async-start | bytes 655360 | tf_op jit(solution)/shard_map/all_to_all | solution.py:57
  104.2 0.6 copy-start.2
  106.1 6.8 %copy-start.3 = (bf16[32,128,16]{1,2,0:T(8,128)(2,1)S(1)}, bf16[32,128,16]{1,2,0:T(8,128)(2,1)}, u32[]{:S(2)}) copy-start(bf16[32,128,16]{1,2,0:T(8,128)(2,1)} %copy-done.2) | copy-start | bytes 393220
  107.6 92.3 %all-to-all-start.3 = ((bf16[16,8,4608]{2,1,0:T(8,128)(2,1)}), bf16[16,8,4608]{2,1,0:T(8,128)(2,1)S(1)}, u32[]{:S(2)}, u32[]{:S(2)}) async-start(bf16[16,8,4608]{2,1,0:T(8,128)(2,1)} %fusion.1), calls=%async_computation.3 | async-start | bytes 2359296 | tf_op jit(solution)/shard_map/all_to_all | solution.py:100
Sparse Core Ops, SparseCore 0:
  11.2 96.1 all-gather.2
  110.5 82.7 all-gather.4

commit v9 on v7

--- a/solution.py
+++ b/solution.py
@@ -96,12 +96,10 @@
     part = part + jnp.dot(onehot, flat_low, preferred_element_type=f32)
     part = part.astype(bf16).reshape(group_count, per_owner, -1)
     gathered = lax.all_to_all(part, "dp", 0, 0, tiled=True)
-    whole = jnp.where(
-        jnp.repeat(seg_live, seg_len)[:, None], whole_raw, jnp.zeros_like(whole_raw)
+    frozen = lax.dot_general(
+        whole_raw, key_weight, (((1,), (1,)), ((), ())), preferred_element_type=f32
     )
-    frozen = lax.dot_general(
-        whole, key_weight, (((1,), (1,)), ((), ())), preferred_element_type=f32
-    )
+    frozen = jnp.where(jnp.repeat(seg_live, seg_len)[:, None], frozen, jnp.zeros_like(frozen))
     extra = jnp.einsum("sjr,srd->sjd", lowrank, down_seg, preferred_element_type=f32)
     input_grad = (frozen + 2.0 * extra.reshape(tok_group, width_shard)).astype(bf16)
     gathered, input_grad = lax.optimization_barrier((gathered, input_grad))

time: 149 us -> 149 us (level)
  no operation moved by 1% of the time
where the time goes in v9:
time: 149 us
  waiting for transfers between devices  63.8 us (43%)
  starting transfers between devices  26.8 us (18%)
  blocking collectives  16.9 us (11%)
  matrix products  15.2 us (10%)
  between operations  14.9 us (10%)
  local copies, waits for them, and re-layouts  8.73 us (6%)
  other arithmetic  2.27 us (2%)
    all_to_all x1, waiting for transfers between devices, on_device(): lax.all_to_all(spread, 'dp', 0, 0, tiled=True).reshape(adapters, -1)  30.3 us
    all_to_all x1, blocking collectives, on_device(): lax.all_to_all(second, 'tensor', 0, 0, tiled=True).reshape(tensor_size, -1)  16.9 us
    all_to_all x1, waiting for transfers between devices, on_device(): first = lax.all_to_all(first, 'tensor', 0, 0, tiled=True)  13.1 us
    all_gather x1, waiting for transfers between devices, on_device(): whole_raw = lax.all_gather(output_grad, 'tensor', axis=0, tiled=True)  11.5 us
    all_to_all x1, starting transfers between devices, on_device(): first = lax.all_to_all(first, 'tensor', 0, 0, tiled=True)  11.1 us
    all_to_all x1, starting transfers between devices, on_device(): lax.all_to_all(spread, 'dp', 0, 0, tiled=True).reshape(adapters, -1)  10.4 us
    all_to_all x1, waiting for transfers between devices, on_device(): gathered = lax.all_to_all(part, 'dp', 0, 0, tiled=True)  8.29 us
    dot_general x1, matrix products, on_device(): lax.dot_general(whole_raw, key_weight, (((1,), (1,)), ((), ())), preferre...  7.09 us
  transfers between devices with their start and end apart: 4, of which 4 were waited for; matrix products, arithmetic and copies ran while one was open for 15% of the time, Pallas kernels for 0%

profile of v9, /device:TPU:1, one launch (start us, length us, event | category | flops | bytes accessed | tf_op | source)
XLA Modules:
  0.0 148.7 jit_solution(9746298316534381369)
XLA Ops:
  7.2 0.7 all-gather.2.cloned.1.call-update
  7.9 0.9 pad_maximum_fusion.2
  9.0 1.1 broadcast_in_dim.56
  10.0 10.4 %all-to-all-start = ((bf16[16,8,4608]{2,1,0:T(8,128)(2,1)}), bf16[16,8,4608]{2,1,0:T(8,128)(2,1)S(1)}, u32[]{:S(2)}, u32[]{:S(2)}) async-start(bf16[16,8,4608]{2,1,0:T(8,128)(2,1)} %broadcast_in_dim.56), calls=%async_computation | async-start | bytes 2359296 | tf_op jit(solution)/shard_map/all_to_all | solution.py:45
  20.4 0.2 select_reduce_fusion
  20.7 30.3 %all-to-all-done = bf16[16,8,4608]{2,1,0:T(8,128)(2,1)S(1)} async-done(((bf16[16,8,4608]{2,1,0:T(8,128)(2,1)}), bf16[16,8,4608]{2,1,0:T(8,128)(2,1)S(1)}, u32[]{:S(2)}, u32[]{:S(2)}) %all-to-all-start) | async-done | bytes 1179680 | tf_op jit(solution)/shard_map/all_to_all | solution.py:45
  51.0 1.1 convolution_convert_fusion
  52.1 1.5 %reshape.65 = bf16[32,16,288]{2,1,0:T(8,128)(2,1)S(1)} reshape(bf16[32,4608]{1,0:T(8,128)(2,1)} %convolution_convert_fusion) | data formatting | bytes 589824 | tf_op jit(solution)/shard_map/reshape | solution.py:48
  53.7 0.6 fusion.9
  54.4 1.4 all_to_all.20
  55.8 11.1 %all-to-all-start.1 = ((f32[32,1,2560]{2,1,0:T(1,128)}), f32[32,1,2560]{2,1,0:T(1,128)S(1)}, u32[]{:S(2)}, u32[]{:S(2)}) async-start(f32[32,1,2560]{2,1,0:T(1,128)} %all_to_all.20), calls=%async_computation.1 | async-start | bytes 655360 | tf_op jit(solution)/shard_map/all_to_all | solution.py:55
  67.5 13.1 %all-to-all-done.1 = f32[32,1,2560]{2,1,0:T(1,128)S(1)} async-done(((f32[32,1,2560]{2,1,0:T(1,128)}), f32[32,1,2560]{2,1,0:T(1,128)S(1)}, u32[]{:S(2)}, u32[]{:S(2)}) %all-to-all-start.1) | async-done | bytes 327712 | tf_op jit(solution)/shard_map/all_to_all | solution.py:55
  80.6 0.8 reduce.1
  81.4 0.3 reshape.67
  82.4 0.2 convert_element_type.55
  82.6 0.2 convolution_convert_fusion.1
  83.1 16.9 %all_to_all.25 = bf16[32,24,128]{2,1,0:T(8,128)(2,1)S(1)} all-to-all(bf16[32,24,128]{2,1,0:T(8,128)(2,1)S(1)} %bitcast.40), channel_id=1, replica_groups=mesh['dp'=16,'tensor'=32] {'tensor'}, dimensions={0} | all-to-all | bytes 393216 | tf_op jit(solution)/shard_map/all_to_all | solution.py:79
  100.1 0.3 copy.40
  100.3 0.5 copy.38
  101.0 0.5 copy-done.2
  101.5 0.4 convolution_multiply_fusion.1
  101.9 0.3 concatenate.18
  102.3 0.4 fusion.7
  102.7 1.6 %fusion.1 = bf16[16,8,4608]{2,1,0:T(8,128)(2,1)} fusion(f32[128,4608]{1,0:T(8,128)S(1)} %fusion.7, f32[32,4608]{1,0:T(8,128)S(1)} %concatenate.18, s32[32]{0:T(128)S(1)} %dynamic_slice.3), kind=kOutput, calls=%fused_computation.2 | convolution fusion | flops 39374848 | bytes 4128896 | tf_op jit(solution)/shard_map/dot_general | solution.py:96
  104.3 5.3 %all-to-all-start.3 = ((bf16[16,8,4608]{2,1,0:T(8,128)(2,1)}), bf16[16,8,4608]{2,1,0:T(8,128)(2,1)S(1)}, u32[]{:S(2)}, u32[]{:S(2)}) async-start(bf16[16,8,4608]{2,1,0:T(8,128)(2,1)} %fusion.1), calls=%async_computation.3 | async-start | bytes 2359296 | tf_op jit(solution)/shard_map/all_to_all | solution.py:98
  109.7 3.7 %convolution_multiply_fusion = f32[32,128,256]{2,1,0:T(8,128)} fusion(bf16[32,128,16]{1,2,0:T(8,128)(2,1)S(1)} %copy-done.3, bf16[32,16,288]{2,1,0:T(8,128)(2,1)} %copy-done.1), kind=kOutput, calls=%fused_computation.7 | convolution fusion | flops 34603008 | bytes 4587520 | tf_op jit(solution)/shard_map/sjr,srd->sjd/dot_general | solution.py:103
  113.4 11.5 %all-gather.2.cloned.1.call-done = bf16[4096,1024]{1,0:T(8,128)(2,1)} async-done(((bf16[128,1024]{1,0:T(8,128)(2,1)}), bf16[4096,1024]{1,0:T(8,128)(2,1)}) %all-gather.2.cloned.1.call-update) | async-done | bytes 8388624 | tf_op jit(solution)/shard_map/all_gather | solution.py:35
  124.8 7.1 %fusion.3 = bf16[4096,256]{1,0:T(8,128)(2,1)} fusion(f32[4096,256]{1,0:T(8,128)} %bitcast.35, bf16[4096,1024]{1,0:T(8,128)(2,1)} %all-gather.2.cloned.1.call-done, bf16[256,1024]{1,0:T(8,128)(2,1)} %param.10, pred[4096]{0:T(1024)(128)(4,1)S(1)} %broadcast_bitcast_fusion), kind=kOutput, calls=%fused_computation.6 | convolution fusion | flops 2150629376 | bytes 15208448 | tf_op jit(solution)/shard_map/dot_general | solution.py:99
  131.9 8.3 %all-to-all-done.3 = bf16[16,8,4608]{2,1,0:T(8,128)(2,1)S(1)} async-done(((bf16[16,8,4608]{2,1,0:T(8,128)(2,1)}), bf16[16,8,4608]{2,1,0:T(8,128)(2,1)S(1)}, u32[]{:S(2)}, u32[]{:S(2)}) %all-to-all-start.3) | async-done | bytes 1179680 | tf_op jit(solution)/shard_map/all_to_all | solution.py:98
  140.4 0.2 reshape.76
  140.6 0.6 slice.46
  141.2 0.6 slice.47
  (39 shorter events, 1.8 us)
Async XLA Ops:
  7.2 46.5 %copy-start = (bf16[4096,256]{1,0:T(8,128)(2,1)S(1)}, bf16[4096,256]{1,0:T(8,128)(2,1)}, u32[]{:S(2)}) copy-start(bf16[4096,256]{1,0:T(8,128)(2,1)} %param.8) | copy-start | bytes 6291460
  7.2 13.2 %copy-start.5 = (s32[512]{0:T(512)S(1)}, s32[512]{0:T(512)}, u32[]{:S(2)}) copy-start(s32[512]{0:T(512)} %param.13) | copy-start | bytes 6148
  7.2 13.2 %copy-start.6 = (s32[128]{0:T(128)S(1)}, s32[128]{0:T(128)}, u32[]{:S(2)}) copy-start(s32[128]{0:T(128)} %param.14) | copy-start | bytes 1540
  7.2 117.6 %all-gather.2.cloned.1.call-start = ((), (), s32[]{:S(2)}) async-start(), calls=%async_computation.4 | async-start | bytes 8650752 | tf_op jit(solution)/shard_map/all_gather | solution.py:35
  10.0 41.0 %all-to-all-start = ((bf16[16,8,4608]{2,1,0:T(8,128)(2,1)}), bf16[16,8,4608]{2,1,0:T(8,128)(2,1)S(1)}, u32[]{:S(2)}, u32[]{:S(2)}) async-start(bf16[16,8,4608]{2,1,0:T(8,128)(2,1)} %broadcast_in_dim.56), calls=%async_computation | async-start | bytes 2359296 | tf_op jit(solution)/shard_map/all_to_all | solution.py:45
  53.6 2.2 %copy-start.1 = (bf16[32,16,288]{2,1,0:T(8,128)(2,1)}, bf16[32,16,288]{2,1,0:T(8,128)(2,1)S(1)}, u32[]{:S(2)}) copy-start(bf16[32,16,288]{2,1,0:T(8,128)(2,1)S(1)} %reshape.65) | copy-start | bytes 884740
  54.3 27.4 %copy-start.4 = (bf16[128,1024]{1,0:T(8,128)(2,1)S(1)}, bf16[128,1024]{1,0:T(8,128)(2,1)}, u32[]{:S(2)}) copy-start(bf16[128,1024]{1,0:T(8,128)(2,1)} %param.9) | copy-start | bytes 786436
  55.8 24.9 %all-to-all-start.1 = ((f32[32,1,2560]{2,1,0:T(1,128)}), f32[32,1,2560]{2,1,0:T(1,128)S(1)}, u32[]{:S(2)}, u32[]{:S(2)}) async-start(f32[32,1,2560]{2,1,0:T(1,128)} %all_to_all.20), calls=%async_computation.1 | async-start | bytes 655360 | tf_op jit(solution)/shard_map/all_to_all | solution.py:55
  100.8 0.6 copy-start.2
  102.7 7.0 %copy-start.3 = (bf16[32,128,16]{1,2,0:T(8,128)(2,1)S(1)}, bf16[32,128,16]{1,2,0:T(8,128)(2,1)}, u32[]{:S(2)}) copy-start(bf16[32,128,16]{1,2,0:T(8,128)(2,1)} %copy-done.2) | copy-start | bytes 393220
  104.3 35.9 %all-to-all-start.3 = ((bf16[16,8,4608]{2,1,0:T(8,128)(2,1)}), bf16[16,8,4608]{2,1,0:T(8,128)(2,1)S(1)}, u32[]{:S(2)}, u32[]{:S(2)}) async-start(bf16[16,8,4608]{2,1,0:T(8,128)(2,1)} %fusion.1), calls=%async_computation.3 | async-start | bytes 2359296 | tf_op jit(solution)/shard_map/all_to_all | solution.py:98
Sparse Core Ops, SparseCore 0:
  11.2 113.5 all-gather.1

commit v10 on v9

--- a/solution.py
+++ b/solution.py
@@ -75,7 +75,7 @@
     up_high = up_round.astype(bf16)
     up_low = (up_pieces - up_round).astype(bf16)
     second = jnp.concatenate([low_spread, up_high, up_low], axis=1)
-    second = second.reshape(tensor_size, -1, 128)
+    second = second.reshape(tensor_size, 1, -1)
     second = lax.all_to_all(second, "tensor", 0, 0, tiled=True).reshape(tensor_size, -1)
     lowrank = second[:, : row_count * rank_dim].reshape(seg_group, seg_len, rank_dim)
     piece = rank_dim * key_shard

time: 149 us -> 151 us (1.013)
  transfers between devices with their start and end apart: 4 -> 4, of which waited for: 4 -> 4; matrix products, arithmetic and copies ran while one was open for 15% -> 16% of each run, Pallas kernels for 0% -> 0%
where the time goes in v10:
time: 151 us
  waiting for transfers between devices  63.8 us (42%)
  starting transfers between devices  27.3 us (18%)
  blocking collectives  16.8 us (11%)
  matrix products  15.2 us (10%)
  between operations  14.9 us (10%)
  local copies, waits for them, and re-layouts  9.56 us (6%)
  other arithmetic  2.99 us (2%)
    all_to_all x1, waiting for transfers between devices, on_device(): lax.all_to_all(spread, 'dp', 0, 0, tiled=True).reshape(adapters, -1)  30.3 us
    all_to_all x1, blocking collectives, on_device(): lax.all_to_all(second, 'tensor', 0, 0, tiled=True).reshape(tensor_size, -1)  16.8 us
    all_to_all x1, waiting for transfers between devices, on_device(): first = lax.all_to_all(first, 'tensor', 0, 0, tiled=True)  13.1 us
    all_to_all x1, starting transfers between devices, on_device(): first = lax.all_to_all(first, 'tensor', 0, 0, tiled=True)  11.1 us
    all_to_all x1, starting transfers between devices, on_device(): lax.all_to_all(spread, 'dp', 0, 0, tiled=True).reshape(adapters, -1)  10.4 us
    all_gather x1, waiting for transfers between devices, on_device(): whole_raw = lax.all_gather(output_grad, 'tensor', axis=0, tiled=True)  10.2 us
    all_to_all x1, waiting for transfers between devices, on_device(): gathered = lax.all_to_all(part, 'dp', 0, 0, tiled=True)  9.52 us
    dot_general x1, matrix products, on_device(): lax.dot_general(whole_raw, key_weight, (((1,), (1,)), ((), ())), preferre...  7.09 us
  transfers between devices with their start and end apart: 4, of which 4 were waited for; matrix products, arithmetic and copies ran while one was open for 16% of the time, Pallas kernels for 0%

profile of v10, /device:TPU:1, one launch (start us, length us, event | category | flops | bytes accessed | tf_op | source)
XLA Modules:
  0.0 150.5 jit_solution(14566918782383951759)
XLA Ops:
  7.2 0.7 all-gather.2.cloned.1.call-update
  7.9 0.9 pad_maximum_fusion.2
  9.0 1.1 broadcast_in_dim.56
  10.0 10.4 %all-to-all-start = ((bf16[16,8,4608]{2,1,0:T(8,128)(2,1)}), bf16[16,8,4608]{2,1,0:T(8,128)(2,1)S(1)}, u32[]{:S(2)}, u32[]{:S(2)}) async-start(bf16[16,8,4608]{2,1,0:T(8,128)(2,1)} %broadcast_in_dim.56), calls=%async_computation | async-start | bytes 2359296 | tf_op jit(solution)/shard_map/all_to_all | solution.py:45
  20.4 0.2 select_reduce_fusion
  20.7 30.3 %all-to-all-done = bf16[16,8,4608]{2,1,0:T(8,128)(2,1)S(1)} async-done(((bf16[16,8,4608]{2,1,0:T(8,128)(2,1)}), bf16[16,8,4608]{2,1,0:T(8,128)(2,1)S(1)}, u32[]{:S(2)}, u32[]{:S(2)}) %all-to-all-start) | async-done | bytes 1179680 | tf_op jit(solution)/shard_map/all_to_all | solution.py:45
  51.0 1.1 convolution_convert_fusion
  52.1 1.5 %reshape.65 = bf16[32,16,288]{2,1,0:T(8,128)(2,1)S(1)} reshape(bf16[32,4608]{1,0:T(8,128)(2,1)} %convolution_convert_fusion) | data formatting | bytes 589824 | tf_op jit(solution)/shard_map/reshape | solution.py:48
  53.7 0.6 fusion.9
  54.4 1.4 all_to_all.20
  55.8 11.1 %all-to-all-start.1 = ((f32[32,1,2560]{2,1,0:T(1,128)}), f32[32,1,2560]{2,1,0:T(1,128)S(1)}, u32[]{:S(2)}, u32[]{:S(2)}) async-start(f32[32,1,2560]{2,1,0:T(1,128)} %all_to_all.20), calls=%async_computation.1 | async-start | bytes 655360 | tf_op jit(solution)/shard_map/all_to_all | solution.py:55
  67.5 13.1 %all-to-all-done.1 = f32[32,1,2560]{2,1,0:T(1,128)S(1)} async-done(((f32[32,1,2560]{2,1,0:T(1,128)}), f32[32,1,2560]{2,1,0:T(1,128)S(1)}, u32[]{:S(2)}, u32[]{:S(2)}) %all-to-all-start.1) | async-done | bytes 327712 | tf_op jit(solution)/shard_map/all_to_all | solution.py:55
  80.6 0.8 reduce.1
  81.4 0.3 reshape.67
  82.4 0.2 convert_element_type.55
  83.0 0.5 broadcast.9
  83.5 0.7 reduce.2
  84.4 16.8 %all_to_all.25 = bf16[32,2,1536]{2,1,0:T(2,128)(2,1)S(1)} all-to-all(bf16[32,2,1536]{2,1,0:T(2,128)(2,1)S(1)} %reshape.79), channel_id=1, replica_groups=mesh['dp'=16,'tensor'=32] {'tensor'}, dimensions={0} | all-to-all | bytes 393216 | tf_op jit(solution)/shard_map/all_to_all | solution.py:79
  101.4 0.3 copy.46
  101.7 0.5 copy.47
  102.3 0.5 copy-done.2
  102.9 0.4 convolution_multiply_fusion.1
  103.3 0.3 concatenate.18
  103.7 0.4 fusion.7
  104.1 1.6 %fusion.1 = bf16[16,8,4608]{2,1,0:T(8,128)(2,1)} fusion(f32[128,4608]{1,0:T(8,128)S(1)} %fusion.7, f32[32,4608]{1,0:T(8,128)S(1)} %concatenate.18, s32[32]{0:T(128)S(1)} %dynamic_slice.3), kind=kOutput, calls=%fused_computation.2 | convolution fusion | flops 39374848 | bytes 4128896 | tf_op jit(solution)/shard_map/dot_general | solution.py:96
  105.7 5.8 %all-to-all-start.3 = ((bf16[16,8,4608]{2,1,0:T(8,128)(2,1)}), bf16[16,8,4608]{2,1,0:T(8,128)(2,1)S(1)}, u32[]{:S(2)}, u32[]{:S(2)}) async-start(bf16[16,8,4608]{2,1,0:T(8,128)(2,1)} %fusion.1), calls=%async_computation.3 | async-start | bytes 2359296 | tf_op jit(solution)/shard_map/all_to_all | solution.py:98
  111.5 3.7 %convolution_multiply_fusion = f32[32,128,256]{2,1,0:T(8,128)} fusion(bf16[32,128,16]{1,2,0:T(8,128)(2,1)S(1)} %copy-done.3, bf16[32,16,288]{2,1,0:T(8,128)(2,1)} %copy-done.1), kind=kOutput, calls=%fused_computation.7 | convolution fusion | flops 34603008 | bytes 4587520 | tf_op jit(solution)/shard_map/sjr,srd->sjd/dot_general | solution.py:103
  115.2 10.2 %all-gather.2.cloned.1.call-done = bf16[4096,1024]{1,0:T(8,128)(2,1)} async-done(((bf16[128,1024]{1,0:T(8,128)(2,1)}), bf16[4096,1024]{1,0:T(8,128)(2,1)}) %all-gather.2.cloned.1.call-update) | async-done | bytes 8388624 | tf_op jit(solution)/shard_map/all_gather | solution.py:35
  125.5 7.1 %fusion.3 = bf16[4096,256]{1,0:T(8,128)(2,1)} fusion(f32[4096,256]{1,0:T(8,128)} %bitcast.33, bf16[4096,1024]{1,0:T(8,128)(2,1)} %all-gather.2.cloned.1.call-done, bf16[256,1024]{1,0:T(8,128)(2,1)} %param.10, pred[4096]{0:T(1024)(128)(4,1)S(1)} %broadcast_bitcast_fusion), kind=kOutput, calls=%fused_computation.6 | convolution fusion | flops 2150629376 | bytes 15208448 | tf_op jit(solution)/shard_map/dot_general | solution.py:99
  132.6 9.5 %all-to-all-done.3 = bf16[16,8,4608]{2,1,0:T(8,128)(2,1)S(1)} async-done(((bf16[16,8,4608]{2,1,0:T(8,128)(2,1)}), bf16[16,8,4608]{2,1,0:T(8,128)(2,1)S(1)}, u32[]{:S(2)}, u32[]{:S(2)}) %all-to-all-start.3) | async-done | bytes 1179680 | tf_op jit(solution)/shard_map/all_to_all | solution.py:98
  142.4 0.6 slice.46
  143.0 0.6 slice.47
  (42 shorter events, 2.4 us)
Async XLA Ops:
  7.2 46.5 %copy-start = (bf16[4096,256]{1,0:T(8,128)(2,1)S(1)}, bf16[4096,256]{1,0:T(8,128)(2,1)}, u32[]{:S(2)}) copy-start(bf16[4096,256]{1,0:T(8,128)(2,1)} %param.8) | copy-start | bytes 6291460
  7.2 13.2 %copy-start.5 = (s32[512]{0:T(512)S(1)}, s32[512]{0:T(512)}, u32[]{:S(2)}) copy-start(s32[512]{0:T(512)} %param.13) | copy-start | bytes 6148
  7.2 13.2 %copy-start.6 = (s32[128]{0:T(128)S(1)}, s32[128]{0:T(128)}, u32[]{:S(2)}) copy-start(s32[128]{0:T(128)} %param.14) | copy-start | bytes 1540
  7.2 118.3 %all-gather.2.cloned.1.call-start = ((), (), s32[]{:S(2)}) async-start(), calls=%async_computation.4 | async-start | bytes 8650752 | tf_op jit(solution)/shard_map/all_gather | solution.py:35
  10.0 41.0 %all-to-all-start = ((bf16[16,8,4608]{2,1,0:T(8,128)(2,1)}), bf16[16,8,4608]{2,1,0:T(8,128)(2,1)S(1)}, u32[]{:S(2)}, u32[]{:S(2)}) async-start(bf16[16,8,4608]{2,1,0:T(8,128)(2,1)} %broadcast_in_dim.56), calls=%async_computation | async-start | bytes 2359296 | tf_op jit(solution)/shard_map/all_to_all | solution.py:45
  53.6 2.2 %copy-start.1 = (bf16[32,16,288]{2,1,0:T(8,128)(2,1)}, bf16[32,16,288]{2,1,0:T(8,128)(2,1)S(1)}, u32[]{:S(2)}) copy-start(bf16[32,16,288]{2,1,0:T(8,128)(2,1)S(1)} %reshape.65) | copy-start | bytes 884740
  54.3 27.4 %copy-start.4 = (bf16[128,1024]{1,0:T(8,128)(2,1)S(1)}, bf16[128,1024]{1,0:T(8,128)(2,1)}, u32[]{:S(2)}) copy-start(bf16[128,1024]{1,0:T(8,128)(2,1)} %param.9) | copy-start | bytes 786436
  55.8 24.9 %all-to-all-start.1 = ((f32[32,1,2560]{2,1,0:T(1,128)}), f32[32,1,2560]{2,1,0:T(1,128)S(1)}, u32[]{:S(2)}, u32[]{:S(2)}) async-start(f32[32,1,2560]{2,1,0:T(1,128)} %all_to_all.20), calls=%async_computation.1 | async-start | bytes 655360 | tf_op jit(solution)/shard_map/all_to_all | solution.py:55
  102.2 0.7 copy-start.2
  104.1 7.4 %copy-start.3 = (bf16[32,128,16]{1,2,0:T(8,128)(2,1)S(1)}, bf16[32,128,16]{1,2,0:T(8,128)(2,1)}, u32[]{:S(2)}) copy-start(bf16[32,128,16]{1,2,0:T(8,128)(2,1)} %copy-done.2) | copy-start | bytes 393220
  105.7 36.4 %all-to-all-start.3 = ((bf16[16,8,4608]{2,1,0:T(8,128)(2,1)}), bf16[16,8,4608]{2,1,0:T(8,128)(2,1)S(1)}, u32[]{:S(2)}, u32[]{:S(2)}) async-start(bf16[16,8,4608]{2,1,0:T(8,128)(2,1)} %fusion.1), calls=%async_computation.3 | async-start | bytes 2359296 | tf_op jit(solution)/shard_map/all_to_all | solution.py:98
Sparse Core Ops, SparseCore 0:
  11.2 114.2 all-gather.1

commit v11 on v9

--- a/solution.py
+++ b/solution.py
@@ -51,12 +51,11 @@
 
     input_seg = layer_input.reshape(seg_group, seg_len, width_shard)
     proj_part = jnp.einsum("sjd,srd->srj", input_seg, down_seg, preferred_element_type=f32)
-    first = jnp.concatenate([proj_part, up_seg.astype(f32)], axis=2).reshape(seg_group, -1)
+    first = jnp.concatenate([proj_part.astype(bf16), up_seg], axis=2).reshape(seg_group, -1)
     first = lax.all_to_all(first, "tensor", 0, 0, tiled=True)
     first = first.reshape(tensor_size, rank_dim, seg_len + key_shard)
-    projected_own = jnp.sum(first[:, :, :seg_len], axis=0).astype(bf16)
+    projected_own = jnp.sum(first[:, :, :seg_len].astype(f32), axis=0).astype(bf16)
     up_own = jnp.transpose(first[:, :, seg_len:], (1, 0, 2)).reshape(rank_dim, key_width)
-    up_own = up_own.astype(bf16)
 
     own_live = position < live_segments[0]
     masked_own = jnp.where(own_live, output_grad, jnp.zeros_like(output_grad))

time: 149 us -> 148 us (level)
  waiting for transfers between devices: 63.8 us -> 61.1 us
  blocking collectives: 16.9 us -> 14.9 us
  other arithmetic: 2.27 us -> 4.02 us
  starting transfers between devices: 26.8 us -> 28.3 us
    all_to_all x1, waiting for transfers between devices: 13.1 us -> 10.4 us  [on_device(): first = lax.all_to_all(first, 'tensor', 0, 0, tiled=True)]
    all_to_all x1, blocking collectives: 16.9 us -> 14.9 us  [on_device(): lax.all_to_all(second, 'tensor', 0, 0, tiled=True).reshape(tensor_size, -1)]
    all_to_all x1 -> x2, other arithmetic: 0.77 us -> 2.53 us  [on_device(): first = lax.all_to_all(first, 'tensor', 0, 0, tiled=True)]
    all_to_all x1, starting transfers between devices: 5.31 us -> 6.81 us  [on_device(): gathered = lax.all_to_all(part, 'dp', 0, 0, tiled=True)]
  transfers between devices with their start and end apart: 4 -> 4, of which waited for: 4 -> 4; matrix products, arithmetic and copies ran while one was open for 15% -> 17% of each run, Pallas kernels for 0% -> 0%
where the time goes in v11:
time: 148 us
  waiting for transfers between devices  61.1 us (41%)
  starting transfers between devices  28.3 us (19%)
  matrix products  15.1 us (10%)
  between operations  15 us (10%)
  blocking collectives  14.9 us (10%)
  local copies, waits for them, and re-layouts  9.19 us (6%)
  other arithmetic  4.02 us (3%)
    all_to_all x1, waiting for transfers between devices, on_device(): lax.all_to_all(spread, 'dp', 0, 0, tiled=True).reshape(adapters, -1)  30.3 us
    all_to_all x1, blocking collectives, on_device(): lax.all_to_all(second, 'tensor', 0, 0, tiled=True).reshape(tensor_size, -1)  14.9 us
    all_gather x1, waiting for transfers between devices, on_device(): whole_raw = lax.all_gather(output_grad, 'tensor', axis=0, tiled=True)  11.3 us
    all_to_all x1, starting transfers between devices, on_device(): first = lax.all_to_all(first, 'tensor', 0, 0, tiled=True)  11.1 us
    all_to_all x1, waiting for transfers between devices, on_device(): first = lax.all_to_all(first, 'tensor', 0, 0, tiled=True)  10.4 us
    all_to_all x1, starting transfers between devices, on_device(): lax.all_to_all(spread, 'dp', 0, 0, tiled=True).reshape(adapters, -1)  10.4 us
    all_to_all x1, waiting for transfers between devices, on_device(): gathered = lax.all_to_all(part, 'dp', 0, 0, tiled=True)  8.48 us
    dot_general x1, matrix products, on_device(): lax.dot_general(whole_raw, key_weight, (((1,), (1,)), ((), ())), preferre...  7.09 us
  transfers between devices with their start and end apart: 4, of which 4 were waited for; matrix products, arithmetic and copies ran while one was open for 17% of the time, Pallas kernels for 0%

profile of v11, /device:TPU:1, one launch (start us, length us, event | category | flops | bytes accessed | tf_op | source)
XLA Modules:
  0.0 147.6 jit_solution(10030317875333943278)
XLA Ops:
  7.2 0.7 all-gather.2.cloned.1.call-update
  7.9 0.9 pad_maximum_fusion.2
  9.0 1.1 broadcast_in_dim.56
  10.0 10.4 %all-to-all-start = ((bf16[16,8,4608]{2,1,0:T(8,128)(2,1)}), bf16[16,8,4608]{2,1,0:T(8,128)(2,1)S(1)}, u32[]{:S(2)}, u32[]{:S(2)}) async-start(bf16[16,8,4608]{2,1,0:T(8,128)(2,1)} %broadcast_in_dim.56), calls=%async_computation | async-start | bytes 2359296 | tf_op jit(solution)/shard_map/all_to_all | solution.py:45
  20.4 0.2 select_reduce_fusion
  20.7 30.3 %all-to-all-done = bf16[16,8,4608]{2,1,0:T(8,128)(2,1)S(1)} async-done(((bf16[16,8,4608]{2,1,0:T(8,128)(2,1)}), bf16[16,8,4608]{2,1,0:T(8,128)(2,1)S(1)}, u32[]{:S(2)}, u32[]{:S(2)}) %all-to-all-start) | async-done | bytes 1179680 | tf_op jit(solution)/shard_map/all_to_all | solution.py:45
  51.0 1.1 convolution_convert_fusion
  52.1 1.5 %reshape.66 = bf16[32,16,288]{2,1,0:T(8,128)(2,1)S(1)} reshape(bf16[32,4608]{1,0:T(8,128)(2,1)} %convolution_convert_fusion) | data formatting | bytes 589824 | tf_op jit(solution)/shard_map/reshape | solution.py:48
  53.7 0.6 convolution_convert_fusion.1
  54.4 0.4 all_to_all.20
  54.8 0.5 broadcast.9
  55.3 1.6 %reduce.3 = bf16[32,2560]{1,0:T(8,128)(2,1)S(1)} reduce(bf16[32,1,2560]{2,1,0:T(2,128)(2,1)S(1)} %all_to_all.20, bf16[]{:T(256)} %broadcast.9), dimensions={1}, to_apply=%all_to_all.20.reduce_sub_computation | reduce | bytes 327682 | tf_op jit(solution)/shard_map/all_to_all | solution.py:55
  56.9 0.7 reshape.81
  57.6 11.1 %all-to-all-start.1 = ((bf16[32,2,1280]{2,1,0:T(2,128)(2,1)}), bf16[32,2,1280]{2,1,0:T(2,128)(2,1)S(1)}, u32[]{:S(2)}, u32[]{:S(2)}) async-start(bf16[32,2,1280]{2,1,0:T(2,128)(2,1)} %reshape.81), calls=%async_computation.1 | async-start | bytes 327680 | tf_op jit(solution)/shard_map/all_to_all | solution.py:55
  69.4 10.4 %all-to-all-done.1 = bf16[32,2,1280]{2,1,0:T(2,128)(2,1)S(1)} async-done(((bf16[32,2,1280]{2,1,0:T(2,128)(2,1)}), bf16[32,2,1280]{2,1,0:T(2,128)(2,1)S(1)}, u32[]{:S(2)}, u32[]{:S(2)}) %all-to-all-start.1) | async-done | bytes 163872 | tf_op jit(solution)/shard_map/all_to_all | solution.py:55
  79.9 0.9 reduce.2
  80.9 0.3 reshape.68
  82.6 14.9 %all_to_all.25 = bf16[32,24,128]{2,1,0:T(8,128)(2,1)S(1)} all-to-all(bf16[32,24,128]{2,1,0:T(8,128)(2,1)S(1)} %bitcast.40), channel_id=1, replica_groups=mesh['dp'=16,'tensor'=32] {'tensor'}, dimensions={0} | all-to-all | bytes 393216 | tf_op jit(solution)/shard_map/all_to_all | solution.py:78
  97.5 0.3 copy.40
  97.8 0.5 copy.38
  98.5 0.5 copy-done.2
  99.0 0.4 convolution_multiply_fusion.1
  99.4 0.3 concatenate.18
  99.8 0.4 fusion.7
  100.2 1.6 %fusion.1 = bf16[16,8,4608]{2,1,0:T(8,128)(2,1)} fusion(f32[128,4608]{1,0:T(8,128)S(1)} %fusion.7, f32[32,4608]{1,0:T(8,128)S(1)} %concatenate.18, s32[32]{0:T(128)S(1)} %dynamic_slice.3), kind=kOutput, calls=%fused_computation.2 | convolution fusion | flops 39374848 | bytes 4128896 | tf_op jit(solution)/shard_map/dot_general | solution.py:95
  101.8 6.8 %all-to-all-start.3 = ((bf16[16,8,4608]{2,1,0:T(8,128)(2,1)}), bf16[16,8,4608]{2,1,0:T(8,128)(2,1)S(1)}, u32[]{:S(2)}, u32[]{:S(2)}) async-start(bf16[16,8,4608]{2,1,0:T(8,128)(2,1)} %fusion.1), calls=%async_computation.3 | async-start | bytes 2359296 | tf_op jit(solution)/shard_map/all_to_all | solution.py:97
  108.7 3.7 %convolution_multiply_fusion = f32[32,128,256]{2,1,0:T(8,128)} fusion(bf16[32,128,16]{1,2,0:T(8,128)(2,1)S(1)} %copy-done.3, bf16[32,16,288]{2,1,0:T(8,128)(2,1)} %copy-done.1), kind=kOutput, calls=%fused_computation.7 | convolution fusion | flops 34603008 | bytes 4587520 | tf_op jit(solution)/shard_map/sjr,srd->sjd/dot_general | solution.py:102
  112.3 11.3 %all-gather.2.cloned.1.call-done = bf16[4096,1024]{1,0:T(8,128)(2,1)} async-done(((bf16[128,1024]{1,0:T(8,128)(2,1)}), bf16[4096,1024]{1,0:T(8,128)(2,1)}) %all-gather.2.cloned.1.call-update) | async-done | bytes 8388624 | tf_op jit(solution)/shard_map/all_gather | solution.py:35
  123.6 7.1 %fusion.3 = bf16[4096,256]{1,0:T(8,128)(2,1)} fusion(f32[4096,256]{1,0:T(8,128)} %bitcast.35, bf16[4096,1024]{1,0:T(8,128)(2,1)} %all-gather.2.cloned.1.call-done, bf16[256,1024]{1,0:T(8,128)(2,1)} %param.10, pred[4096]{0:T(1024)(128)(4,1)S(1)} %broadcast_bitcast_fusion), kind=kOutput, calls=%fused_computation.6 | convolution fusion | flops 2150629376 | bytes 15208448 | tf_op jit(solution)/shard_map/dot_general | solution.py:98
  130.7 8.5 %all-to-all-done.3 = bf16[16,8,4608]{2,1,0:T(8,128)(2,1)S(1)} async-done(((bf16[16,8,4608]{2,1,0:T(8,128)(2,1)}), bf16[16,8,4608]{2,1,0:T(8,128)(2,1)S(1)}, u32[]{:S(2)}, u32[]{:S(2)}) %all-to-all-start.3) | async-done | bytes 1179680 | tf_op jit(solution)/shard_map/all_to_all | solution.py:97
  139.5 0.6 slice.45
  140.1 0.6 slice.46
  (43 shorter events, 2.5 us)
Async XLA Ops:
  7.2 46.5 %copy-start = (bf16[4096,256]{1,0:T(8,128)(2,1)S(1)}, bf16[4096,256]{1,0:T(8,128)(2,1)}, u32[]{:S(2)}) copy-start(bf16[4096,256]{1,0:T(8,128)(2,1)} %param.8) | copy-start | bytes 6291460
  7.2 13.2 %copy-start.5 = (s32[512]{0:T(512)S(1)}, s32[512]{0:T(512)}, u32[]{:S(2)}) copy-start(s32[512]{0:T(512)} %param.13) | copy-start | bytes 6148
  7.2 13.2 %copy-start.6 = (s32[128]{0:T(128)S(1)}, s32[128]{0:T(128)}, u32[]{:S(2)}) copy-start(s32[128]{0:T(128)} %param.14) | copy-start | bytes 1540
  7.2 116.4 %all-gather.2.cloned.1.call-start = ((), (), s32[]{:S(2)}) async-start(), calls=%async_computation.4 | async-start | bytes 8650752 | tf_op jit(solution)/shard_map/all_gather | solution.py:35
  10.0 41.0 %all-to-all-start = ((bf16[16,8,4608]{2,1,0:T(8,128)(2,1)}), bf16[16,8,4608]{2,1,0:T(8,128)(2,1)S(1)}, u32[]{:S(2)}, u32[]{:S(2)}) async-start(bf16[16,8,4608]{2,1,0:T(8,128)(2,1)} %broadcast_in_dim.56), calls=%async_computation | async-start | bytes 2359296 | tf_op jit(solution)/shard_map/all_to_all | solution.py:45
  53.6 4.0 %copy-start.1 = (bf16[32,16,288]{2,1,0:T(8,128)(2,1)}, bf16[32,16,288]{2,1,0:T(8,128)(2,1)S(1)}, u32[]{:S(2)}) copy-start(bf16[32,16,288]{2,1,0:T(8,128)(2,1)S(1)} %reshape.66) | copy-start | bytes 884740
  54.3 26.9 %copy-start.4 = (bf16[128,1024]{1,0:T(8,128)(2,1)S(1)}, bf16[128,1024]{1,0:T(8,128)(2,1)}, u32[]{:S(2)}) copy-start(bf16[128,1024]{1,0:T(8,128)(2,1)} %param.9) | copy-start | bytes 786436
  57.6 22.2 %all-to-all-start.1 = ((bf16[32,2,1280]{2,1,0:T(2,128)(2,1)}), bf16[32,2,1280]{2,1,0:T(2,128)(2,1)S(1)}, u32[]{:S(2)}, u32[]{:S(2)}) async-start(bf16[32,2,1280]{2,1,0:T(2,128)(2,1)} %reshape.81), calls=%async_computation.1 | async-start | bytes 327680 | tf_op jit(solution)/shard_map/all_to_all | solution.py:55
  98.3 0.7 copy-start.2
  100.2 8.5 %copy-start.3 = (bf16[32,128,16]{1,2,0:T(8,128)(2,1)S(1)}, bf16[32,128,16]{1,2,0:T(8,128)(2,1)}, u32[]{:S(2)}) copy-start(bf16[32,128,16]{1,2,0:T(8,128)(2,1)} %copy-done.2) | copy-start | bytes 393220
  101.8 37.4 %all-to-all-start.3 = ((bf16[16,8,4608]{2,1,0:T(8,128)(2,1)}), bf16[16,8,4608]{2,1,0:T(8,128)(2,1)S(1)}, u32[]{:S(2)}, u32[]{:S(2)}) async-start(bf16[16,8,4608]{2,1,0:T(8,128)(2,1)} %fusion.1), calls=%async_computation.3 | async-start | bytes 2359296 | tf_op jit(solution)/shard_map/all_to_all | solution.py:97
Sparse Core Ops, SparseCore 0:
  11.2 112.3 all-gather.1

commit v12 on v9

--- a/solution.py
+++ b/solution.py
@@ -51,7 +51,7 @@
 
     input_seg = layer_input.reshape(seg_group, seg_len, width_shard)
     proj_part = jnp.einsum("sjd,srd->srj", input_seg, down_seg, preferred_element_type=f32)
-    first = jnp.concatenate([proj_part, up_seg.astype(f32)], axis=2).reshape(seg_group, -1)
+    first = jnp.concatenate([proj_part, up_seg.astype(f32)], axis=2).reshape(seg_group, -1, 128)
     first = lax.all_to_all(first, "tensor", 0, 0, tiled=True)
     first = first.reshape(tensor_size, rank_dim, seg_len + key_shard)
     projected_own = jnp.sum(first[:, :, :seg_len], axis=0).astype(bf16)

time: 149 us -> 150 us (level)
  no operation moved by 1% of the time
where the time goes in v12:
time: 150 us
  waiting for transfers between devices  64.9 us (43%)
  starting transfers between devices  27 us (18%)
  blocking collectives  17.7 us (12%)
  matrix products  15.1 us (10%)
  between operations  14.9 us (10%)
  local copies, waits for them, and re-layouts  8.44 us (6%)
  other arithmetic  1.5 us (1%)
    all_to_all x1, waiting for transfers between devices, on_device(): lax.all_to_all(spread, 'dp', 0, 0, tiled=True).reshape(adapters, -1)  30.3 us
    all_to_all x1, blocking collectives, on_device(): lax.all_to_all(second, 'tensor', 0, 0, tiled=True).reshape(tensor_size, -1)  17.7 us
    all_to_all x1, waiting for transfers between devices, on_device(): first = lax.all_to_all(first, 'tensor', 0, 0, tiled=True)  14.2 us
    all_to_all x1, starting transfers between devices, on_device(): first = lax.all_to_all(first, 'tensor', 0, 0, tiled=True)  11.1 us
    all_gather x1, waiting for transfers between devices, on_device(): whole_raw = lax.all_gather(output_grad, 'tensor', axis=0, tiled=True)  11 us
    all_to_all x1, starting transfers between devices, on_device(): lax.all_to_all(spread, 'dp', 0, 0, tiled=True).reshape(adapters, -1)  10.4 us
    all_to_all x1, waiting for transfers between devices, on_device(): gathered = lax.all_to_all(part, 'dp', 0, 0, tiled=True)  8.81 us
    dot_general x1, matrix products, on_device(): lax.dot_general(whole_raw, key_weight, (((1,), (1,)), ((), ())), preferre...  7.09 us
  transfers between devices with their start and end apart: 4, of which 4 were waited for; matrix products, arithmetic and copies ran while one was open for 15% of the time, Pallas kernels for 0%

profile of v12, /device:TPU:1, one launch (start us, length us, event | category | flops | bytes accessed | tf_op | source)
XLA Modules:
  0.0 149.6 jit_solution(2290763522144610270)
XLA Ops:
  7.2 0.7 all-gather.2.cloned.1.call-update
  7.9 0.9 pad_maximum_fusion.2
  9.0 1.1 broadcast_in_dim.56
  10.0 10.4 %all-to-all-start = ((bf16[16,8,4608]{2,1,0:T(8,128)(2,1)}), bf16[16,8,4608]{2,1,0:T(8,128)(2,1)S(1)}, u32[]{:S(2)}, u32[]{:S(2)}) async-start(bf16[16,8,4608]{2,1,0:T(8,128)(2,1)} %broadcast_in_dim.56), calls=%async_computation | async-start | bytes 2359296 | tf_op jit(solution)/shard_map/all_to_all | solution.py:45
  20.4 0.2 select_reduce_fusion
  20.7 30.3 %all-to-all-done = bf16[16,8,4608]{2,1,0:T(8,128)(2,1)S(1)} async-done(((bf16[16,8,4608]{2,1,0:T(8,128)(2,1)}), bf16[16,8,4608]{2,1,0:T(8,128)(2,1)S(1)}, u32[]{:S(2)}, u32[]{:S(2)}) %all-to-all-start) | async-done | bytes 1179680 | tf_op jit(solution)/shard_map/all_to_all | solution.py:45
  51.0 1.1 convolution_convert_fusion
  52.1 1.5 %reshape.63 = bf16[32,16,288]{2,1,0:T(8,128)(2,1)S(1)} reshape(bf16[32,4608]{1,0:T(8,128)(2,1)} %convolution_convert_fusion) | data formatting | bytes 589824 | tf_op jit(solution)/shard_map/reshape | solution.py:48
  53.6 0.6 fusion.9
  54.4 1.1 reshape.65
  55.5 11.1 %all-to-all-start.1 = ((f32[32,20,128]{2,1,0:T(8,128)}), f32[32,20,128]{2,1,0:T(8,128)S(1)}, u32[]{:S(2)}, u32[]{:S(2)}) async-start(f32[32,20,128]{2,1,0:T(8,128)} %reshape.65), calls=%async_computation.1 | async-start | bytes 786432 | tf_op jit(solution)/shard_map/all_to_all | solution.py:55
  67.2 14.2 %all-to-all-done.1 = f32[32,20,128]{2,1,0:T(8,128)S(1)} async-done(((f32[32,20,128]{2,1,0:T(8,128)}), f32[32,20,128]{2,1,0:T(8,128)S(1)}, u32[]{:S(2)}, u32[]{:S(2)}) %all-to-all-start.1) | async-done | bytes 327712 | tf_op jit(solution)/shard_map/all_to_all | solution.py:55
  81.5 0.3 reshape.66
  82.4 0.2 convert_element_type.55
  82.6 0.2 convolution_convert_fusion.1
  83.1 17.7 %all_to_all.20 = bf16[32,24,128]{2,1,0:T(8,128)(2,1)S(1)} all-to-all(bf16[32,24,128]{2,1,0:T(8,128)(2,1)S(1)} %bitcast.40), channel_id=1, replica_groups=mesh['dp'=16,'tensor'=32] {'tensor'}, dimensions={0} | all-to-all | bytes 393216 | tf_op jit(solution)/shard_map/all_to_all | solution.py:79
  100.8 0.3 copy.31
  101.1 0.5 copy.29
  101.8 0.5 copy-done.2
  102.3 0.4 convolution_multiply_fusion.1
  102.7 0.3 concatenate.18
  103.1 0.4 fusion.7
  103.5 1.5 %fusion.1 = bf16[16,8,4608]{2,1,0:T(8,128)(2,1)} fusion(f32[128,4608]{1,0:T(8,128)S(1)} %fusion.7, f32[32,4608]{1,0:T(8,128)S(1)} %concatenate.18, s32[32]{0:T(128)S(1)} %dynamic_slice.3), kind=kOutput, calls=%fused_computation.2 | convolution fusion | flops 39374848 | bytes 4128896 | tf_op jit(solution)/shard_map/dot_general | solution.py:96
  105.1 5.5 %all-to-all-start.3 = ((bf16[16,8,4608]{2,1,0:T(8,128)(2,1)}), bf16[16,8,4608]{2,1,0:T(8,128)(2,1)S(1)}, u32[]{:S(2)}, u32[]{:S(2)}) async-start(bf16[16,8,4608]{2,1,0:T(8,128)(2,1)} %fusion.1), calls=%async_computation.3 | async-start | bytes 2359296 | tf_op jit(solution)/shard_map/all_to_all | solution.py:98
  110.7 3.7 %convolution_multiply_fusion = f32[32,128,256]{2,1,0:T(8,128)} fusion(bf16[32,128,16]{1,2,0:T(8,128)(2,1)S(1)} %copy-done.3, bf16[32,16,288]{2,1,0:T(8,128)(2,1)} %copy-done.1), kind=kOutput, calls=%fused_computation.7 | convolution fusion | flops 34603008 | bytes 4587520 | tf_op jit(solution)/shard_map/sjr,srd->sjd/dot_general | solution.py:103
  114.3 11.0 %all-gather.2.cloned.1.call-done = bf16[4096,1024]{1,0:T(8,128)(2,1)} async-done(((bf16[128,1024]{1,0:T(8,128)(2,1)}), bf16[4096,1024]{1,0:T(8,128)(2,1)}) %all-gather.2.cloned.1.call-update) | async-done | bytes 8388624 | tf_op jit(solution)/shard_map/all_gather | solution.py:35
  125.3 7.1 %fusion.3 = bf16[4096,256]{1,0:T(8,128)(2,1)} fusion(f32[4096,256]{1,0:T(8,128)} %bitcast.35, bf16[4096,1024]{1,0:T(8,128)(2,1)} %all-gather.2.cloned.1.call-done, bf16[256,1024]{1,0:T(8,128)(2,1)} %param.10, pred[4096]{0:T(1024)(128)(4,1)S(1)} %broadcast_bitcast_fusion), kind=kOutput, calls=%fused_computation.6 | convolution fusion | flops 2150629376 | bytes 15208448 | tf_op jit(solution)/shard_map/dot_general | solution.py:99
  132.4 8.8 %all-to-all-done.3 = bf16[16,8,4608]{2,1,0:T(8,128)(2,1)S(1)} async-done(((bf16[16,8,4608]{2,1,0:T(8,128)(2,1)}), bf16[16,8,4608]{2,1,0:T(8,128)(2,1)S(1)}, u32[]{:S(2)}, u32[]{:S(2)}) %all-to-all-start.3) | async-done | bytes 1179680 | tf_op jit(solution)/shard_map/all_to_all | solution.py:98
  141.2 0.2 reduce
  141.3 0.2 reshape.75
  141.5 0.6 slice.46
  142.2 0.6 slice.47
  (38 shorter events, 1.7 us)
Async XLA Ops:
  7.2 46.5 %copy-start = (bf16[4096,256]{1,0:T(8,128)(2,1)S(1)}, bf16[4096,256]{1,0:T(8,128)(2,1)}, u32[]{:S(2)}) copy-start(bf16[4096,256]{1,0:T(8,128)(2,1)} %param.8) | copy-start | bytes 6291460
  7.2 13.2 %copy-start.5 = (s32[512]{0:T(512)S(1)}, s32[512]{0:T(512)}, u32[]{:S(2)}) copy-start(s32[512]{0:T(512)} %param.13) | copy-start | bytes 6148
  7.2 13.2 %copy-start.6 = (s32[128]{0:T(128)S(1)}, s32[128]{0:T(128)}, u32[]{:S(2)}) copy-start(s32[128]{0:T(128)} %param.14) | copy-start | bytes 1540
  7.2 118.1 %all-gather.2.cloned.1.call-start = ((), (), s32[]{:S(2)}) async-start(), calls=%async_computation.4 | async-start | bytes 8650752 | tf_op jit(solution)/shard_map/all_gather | solution.py:35
  10.0 41.0 %all-to-all-start = ((bf16[16,8,4608]{2,1,0:T(8,128)(2,1)}), bf16[16,8,4608]{2,1,0:T(8,128)(2,1)S(1)}, u32[]{:S(2)}, u32[]{:S(2)}) async-start(bf16[16,8,4608]{2,1,0:T(8,128)(2,1)} %broadcast_in_dim.56), calls=%async_computation | async-start | bytes 2359296 | tf_op jit(solution)/shard_map/all_to_all | solution.py:45
  53.6 1.9 %copy-start.1 = (bf16[32,16,288]{2,1,0:T(8,128)(2,1)}, bf16[32,16,288]{2,1,0:T(8,128)(2,1)S(1)}, u32[]{:S(2)}) copy-start(bf16[32,16,288]{2,1,0:T(8,128)(2,1)S(1)} %reshape.63) | copy-start | bytes 884740
  54.3 27.5 %copy-start.4 = (bf16[128,1024]{1,0:T(8,128)(2,1)S(1)}, bf16[128,1024]{1,0:T(8,128)(2,1)}, u32[]{:S(2)}) copy-start(bf16[128,1024]{1,0:T(8,128)(2,1)} %param.9) | copy-start | bytes 786436
  55.5 26.0 %all-to-all-start.1 = ((f32[32,20,128]{2,1,0:T(8,128)}), f32[32,20,128]{2,1,0:T(8,128)S(1)}, u32[]{:S(2)}, u32[]{:S(2)}) async-start(f32[32,20,128]{2,1,0:T(8,128)} %reshape.65), calls=%async_computation.1 | async-start | bytes 786432 | tf_op jit(solution)/shard_map/all_to_all | solution.py:55
  101.6 0.7 copy-start.2
  103.5 7.1 %copy-start.3 = (bf16[32,128,16]{1,2,0:T(8,128)(2,1)S(1)}, bf16[32,128,16]{1,2,0:T(8,128)(2,1)}, u32[]{:S(2)}) copy-start(bf16[32,128,16]{1,2,0:T(8,128)(2,1)} %copy-done.2) | copy-start | bytes 393220
  105.1 36.1 %all-to-all-start.3 = ((bf16[16,8,4608]{2,1,0:T(8,128)(2,1)}), bf16[16,8,4608]{2,1,0:T(8,128)(2,1)S(1)}, u32[]{:S(2)}, u32[]{:S(2)}) async-start(bf16[16,8,4608]{2,1,0:T(8,128)(2,1)} %fusion.1), calls=%async_computation.3 | async-start | bytes 2359296 | tf_op jit(solution)/shard_map/all_to_all | solution.py:98
Sparse Core Ops, SparseCore 0:
  11.2 114.0 all-gather.1

commit v13 on v9

--- a/solution.py
+++ b/solution.py
@@ -61,7 +61,7 @@
     own_live = position < live_segments[0]
     masked_own = jnp.where(own_live, output_grad, jnp.zeros_like(output_grad))
     lowrank_own = lax.dot_general(
-        masked_own, up_own, (((1,), (1,)), ((), ())), preferred_element_type=f32
+        up_own, masked_own, (((1,), (1,)), ((), ())), preferred_element_type=f32
     ).astype(bf16)
     seg_up_own = 2.0 * jnp.dot(projected_own, masked_own, preferred_element_type=f32)
 
@@ -77,14 +77,14 @@
     second = jnp.concatenate([low_spread, up_high, up_low], axis=1)
     second = second.reshape(tensor_size, -1, 128)
     second = lax.all_to_all(second, "tensor", 0, 0, tiled=True).reshape(tensor_size, -1)
-    lowrank = second[:, : row_count * rank_dim].reshape(seg_group, seg_len, rank_dim)
+    lowrank = second[:, : row_count * rank_dim].reshape(seg_group, rank_dim, seg_len)
     piece = rank_dim * key_shard
     low_end = row_count * rank_dim
     seg_up = second[:, low_end : low_end + piece].astype(f32)
     seg_up = seg_up + second[:, low_end + piece :].astype(f32)
     seg_up = seg_up.reshape(seg_group, rank_dim, key_shard)
 
-    seg_down = 2.0 * jnp.einsum("sjr,sjd->srd", lowrank, input_seg, preferred_element_type=f32)
+    seg_down = 2.0 * jnp.einsum("srj,sjd->srd", lowrank, input_seg, preferred_element_type=f32)
     seg_grad = jnp.concatenate([seg_down, seg_up], axis=2)
     onehot = (slot_ids[:, None] == seg_slot[None, :]).astype(bf16)
     grad_round = lax.reduce_precision(seg_grad, exponent_bits=8, mantissa_bits=7)
@@ -100,7 +100,7 @@
         whole_raw, key_weight, (((1,), (1,)), ((), ())), preferred_element_type=f32
     )
     frozen = jnp.where(jnp.repeat(seg_live, seg_len)[:, None], frozen, jnp.zeros_like(frozen))
-    extra = jnp.einsum("sjr,srd->sjd", lowrank, down_seg, preferred_element_type=f32)
+    extra = jnp.einsum("srj,srd->sjd", lowrank, down_seg, preferred_element_type=f32)
     input_grad = (frozen + 2.0 * extra.reshape(tok_group, width_shard)).astype(bf16)
     gathered, input_grad = lax.optimization_barrier((gathered, input_grad))
     total = jnp.sum(gathered.astype(f32), axis=0).reshape(per_owner, rank_dim, -1)

time: 149 us -> 148 us (level)
    all_gather x1, waiting for transfers between devices: 11.5 us -> 13 us  [on_device(): whole_raw = lax.all_gather(output_grad, 'tensor', axis=0, tiled=True)]
    all_to_all x1, waiting for transfers between devices: 8.29 us -> 6.74 us  [on_device(): gathered = lax.all_to_all(part, 'dp', 0, 0, tiled=True)]
where the time goes in v13:
time: 148 us; the launch traced here: 147 us
  waiting for transfers between devices  63.8 us (43%)
  starting transfers between devices  27 us (18%)
  blocking collectives  16.6 us (11%)
  matrix products  15.2 us (10%)
  between operations  14.9 us (10%)
  local copies, waits for them, and re-layouts  7.34 us (5%)
  other arithmetic  2.28 us (2%)
    all_to_all x1, waiting for transfers between devices, on_device(): lax.all_to_all(spread, 'dp', 0, 0, tiled=True).reshape(adapters, -1)  30.3 us
    all_to_all x1, blocking collectives, on_device(): lax.all_to_all(second, 'tensor', 0, 0, tiled=True).reshape(tensor_size, -1)  16.6 us
    all_to_all x1, waiting for transfers between devices, on_device(): first = lax.all_to_all(first, 'tensor', 0, 0, tiled=True)  13.1 us
    all_gather x1, waiting for transfers between devices, on_device(): whole_raw = lax.all_gather(output_grad, 'tensor', axis=0, tiled=True)  13 us
    all_to_all x1, starting transfers between devices, on_device(): first = lax.all_to_all(first, 'tensor', 0, 0, tiled=True)  11.1 us
    all_to_all x1, starting transfers between devices, on_device(): lax.all_to_all(spread, 'dp', 0, 0, tiled=True).reshape(adapters, -1)  10.4 us
    dot_general x1, matrix products, on_device(): lax.dot_general(whole_raw, key_weight, (((1,), (1,)), ((), ())), preferre...  7.09 us
    all_to_all x1, waiting for transfers between devices, on_device(): gathered = lax.all_to_all(part, 'dp', 0, 0, tiled=True)  6.74 us
  transfers between devices with their start and end apart: 4, of which 4 were waited for; matrix products, arithmetic and copies ran while one was open for 15% of the time, Pallas kernels for 0%

profile of v13, /device:TPU:1, one launch (start us, length us, event | category | flops | bytes accessed | tf_op | source)
XLA Modules:
  0.0 147.1 jit_solution(13841824733136216324)
XLA Ops:
  7.2 0.7 all-gather.2.cloned.1.call-update
  7.9 0.9 pad_maximum_fusion.2
  9.0 1.1 broadcast_in_dim.55
  10.0 10.4 %all-to-all-start = ((bf16[16,8,4608]{2,1,0:T(8,128)(2,1)}), bf16[16,8,4608]{2,1,0:T(8,128)(2,1)S(1)}, u32[]{:S(2)}, u32[]{:S(2)}) async-start(bf16[16,8,4608]{2,1,0:T(8,128)(2,1)} %broadcast_in_dim.55), calls=%async_computation | async-start | bytes 2359296 | tf_op jit(solution)/shard_map/all_to_all | solution.py:45
  20.4 0.2 select_reduce_fusion
  20.7 30.3 %all-to-all-done = bf16[16,8,4608]{2,1,0:T(8,128)(2,1)S(1)} async-done(((bf16[16,8,4608]{2,1,0:T(8,128)(2,1)}), bf16[16,8,4608]{2,1,0:T(8,128)(2,1)S(1)}, u32[]{:S(2)}, u32[]{:S(2)}) %all-to-all-start) | async-done | bytes 1179680 | tf_op jit(solution)/shard_map/all_to_all | solution.py:45
  51.0 1.1 convolution_convert_fusion
  52.1 1.5 %reshape.65 = bf16[32,16,288]{2,1,0:T(8,128)(2,1)S(1)} reshape(bf16[32,4608]{1,0:T(8,128)(2,1)} %convolution_convert_fusion) | data formatting | bytes 589824 | tf_op jit(solution)/shard_map/reshape | solution.py:48
  53.7 0.6 fusion.10
  54.4 1.4 all_to_all.20
  55.8 11.1 %all-to-all-start.1 = ((f32[32,1,2560]{2,1,0:T(1,128)}), f32[32,1,2560]{2,1,0:T(1,128)S(1)}, u32[]{:S(2)}, u32[]{:S(2)}) async-start(f32[32,1,2560]{2,1,0:T(1,128)} %all_to_all.20), calls=%async_computation.1 | async-start | bytes 655360 | tf_op jit(solution)/shard_map/all_to_all | solution.py:55
  67.5 13.1 %all-to-all-done.1 = f32[32,1,2560]{2,1,0:T(1,128)S(1)} async-done(((f32[32,1,2560]{2,1,0:T(1,128)}), f32[32,1,2560]{2,1,0:T(1,128)S(1)}, u32[]{:S(2)}, u32[]{:S(2)}) %all-to-all-start.1) | async-done | bytes 327712 | tf_op jit(solution)/shard_map/all_to_all | solution.py:55
  80.6 0.8 reduce.1
  81.4 0.3 reshape.67
  81.7 0.2 convolution_multiply_fusion.2
  82.0 0.2 copy.25
  82.4 0.2 convert_element_type.55
  82.6 0.2 fusion.5
  82.8 16.6 %all_to_all.25 = bf16[32,24,128]{2,1,0:T(8,128)(2,1)S(1)} all-to-all(bf16[32,24,128]{2,1,0:T(8,128)(2,1)S(1)} %bitcast.45), channel_id=1, replica_groups=mesh['dp'=16,'tensor'=32] {'tensor'}, dimensions={0} | all-to-all | bytes 393216 | tf_op jit(solution)/shard_map/all_to_all | solution.py:79
  99.7 0.4 convolution_multiply_fusion.1
  100.2 0.3 concatenate.18
  100.6 0.4 fusion.8
  101.0 1.6 %fusion.1 = bf16[16,8,4608]{2,1,0:T(8,128)(2,1)} fusion(f32[128,4608]{1,0:T(8,128)S(1)} %fusion.8, f32[32,4608]{1,0:T(8,128)S(1)} %concatenate.18, s32[32]{0:T(128)S(1)} %dynamic_slice.3), kind=kOutput, calls=%fused_computation.2 | convolution fusion | flops 39374848 | bytes 4128896 | tf_op jit(solution)/shard_map/dot_general | solution.py:96
  102.6 5.5 %all-to-all-start.3 = ((bf16[16,8,4608]{2,1,0:T(8,128)(2,1)}), bf16[16,8,4608]{2,1,0:T(8,128)(2,1)S(1)}, u32[]{:S(2)}, u32[]{:S(2)}) async-start(bf16[16,8,4608]{2,1,0:T(8,128)(2,1)} %fusion.1), calls=%async_computation.3 | async-start | bytes 2359296 | tf_op jit(solution)/shard_map/all_to_all | solution.py:98
  108.2 3.7 %convolution_multiply_fusion = f32[32,128,256]{2,1,0:T(8,128)} fusion(bf16[32,16,128]{2,1,0:T(8,128)(2,1)S(1)} %bitcast.41, bf16[32,16,288]{2,1,0:T(8,128)(2,1)} %copy-done.1), kind=kOutput, calls=%fused_computation.7 | convolution fusion | flops 34603008 | bytes 4587520 | tf_op jit(solution)/shard_map/srj,srd->sjd/dot_general | solution.py:103
  111.8 13.0 %all-gather.2.cloned.1.call-done = bf16[4096,1024]{1,0:T(8,128)(2,1)} async-done(((bf16[128,1024]{1,0:T(8,128)(2,1)}), bf16[4096,1024]{1,0:T(8,128)(2,1)}) %all-gather.2.cloned.1.call-update) | async-done | bytes 8388624 | tf_op jit(solution)/shard_map/all_gather | solution.py:35
  124.9 7.1 %fusion.3 = bf16[4096,256]{1,0:T(8,128)(2,1)} fusion(f32[4096,256]{1,0:T(8,128)} %bitcast.39, bf16[4096,1024]{1,0:T(8,128)(2,1)} %all-gather.2.cloned.1.call-done, bf16[256,1024]{1,0:T(8,128)(2,1)} %param.10, pred[4096]{0:T(1024)(128)(4,1)S(1)} %broadcast_bitcast_fusion), kind=kOutput, calls=%fused_computation.6 | convolution fusion | flops 2150629376 | bytes 15208448 | tf_op jit(solution)/shard_map/dot_general | solution.py:99
  131.9 6.7 %all-to-all-done.3 = bf16[16,8,4608]{2,1,0:T(8,128)(2,1)S(1)} async-done(((bf16[16,8,4608]{2,1,0:T(8,128)(2,1)}), bf16[16,8,4608]{2,1,0:T(8,128)(2,1)S(1)}, u32[]{:S(2)}, u32[]{:S(2)}) %all-to-all-start.3) | async-done | bytes 1179680 | tf_op jit(solution)/shard_map/all_to_all | solution.py:98
  138.7 0.2 reduce
  138.8 0.2 reshape.76
  139.0 0.6 slice.46
  139.7 0.6 slice.47
  (36 shorter events, 1.2 us)
Async XLA Ops:
  7.2 46.5 %copy-start = (bf16[4096,256]{1,0:T(8,128)(2,1)S(1)}, bf16[4096,256]{1,0:T(8,128)(2,1)}, u32[]{:S(2)}) copy-start(bf16[4096,256]{1,0:T(8,128)(2,1)} %param.8) | copy-start | bytes 6291460
  7.2 13.2 %copy-start.5 = (s32[512]{0:T(512)S(1)}, s32[512]{0:T(512)}, u32[]{:S(2)}) copy-start(s32[512]{0:T(512)} %param.13) | copy-start | bytes 6148
  7.2 13.2 %copy-start.6 = (s32[128]{0:T(128)S(1)}, s32[128]{0:T(128)}, u32[]{:S(2)}) copy-start(s32[128]{0:T(128)} %param.14) | copy-start | bytes 1540
  7.2 117.7 %all-gather.2.cloned.1.call-start = ((), (), s32[]{:S(2)}) async-start(), calls=%async_computation.4 | async-start | bytes 8650752 | tf_op jit(solution)/shard_map/all_gather | solution.py:35
  10.0 41.0 %all-to-all-start = ((bf16[16,8,4608]{2,1,0:T(8,128)(2,1)}), bf16[16,8,4608]{2,1,0:T(8,128)(2,1)S(1)}, u32[]{:S(2)}, u32[]{:S(2)}) async-start(bf16[16,8,4608]{2,1,0:T(8,128)(2,1)} %broadcast_in_dim.55), calls=%async_computation | async-start | bytes 2359296 | tf_op jit(solution)/shard_map/all_to_all | solution.py:45
  53.6 2.2 %copy-start.1 = (bf16[32,16,288]{2,1,0:T(8,128)(2,1)}, bf16[32,16,288]{2,1,0:T(8,128)(2,1)S(1)}, u32[]{:S(2)}) copy-start(bf16[32,16,288]{2,1,0:T(8,128)(2,1)S(1)} %reshape.65) | copy-start | bytes 884740
  54.3 27.4 %copy-start.4 = (bf16[128,1024]{1,0:T(8,128)(2,1)S(1)}, bf16[128,1024]{1,0:T(8,128)(2,1)}, u32[]{:S(2)}) copy-start(bf16[128,1024]{1,0:T(8,128)(2,1)} %param.9) | copy-start | bytes 786436
  55.8 24.9 %all-to-all-start.1 = ((f32[32,1,2560]{2,1,0:T(1,128)}), f32[32,1,2560]{2,1,0:T(1,128)S(1)}, u32[]{:S(2)}, u32[]{:S(2)}) async-start(f32[32,1,2560]{2,1,0:T(1,128)} %all_to_all.20), calls=%async_computation.1 | async-start | bytes 655360 | tf_op jit(solution)/shard_map/all_to_all | solution.py:55
  99.5 0.6 copy-start.2
  101.0 7.1 %copy-start.3 = (bf16[4,8,16,128]{3,2,1,0:T(8,128)(2,1)S(1)}, bf16[4,8,16,128]{3,2,1,0:T(8,128)(2,1)}, u32[]{:S(2)}) copy-start(bf16[4,8,16,128]{3,2,1,0:T(8,128)(2,1)} %copy-done.2) | copy-start | bytes 393220
  102.6 36.1 %all-to-all-start.3 = ((bf16[16,8,4608]{2,1,0:T(8,128)(2,1)}), bf16[16,8,4608]{2,1,0:T(8,128)(2,1)S(1)}, u32[]{:S(2)}, u32[]{:S(2)}) async-start(bf16[16,8,4608]{2,1,0:T(8,128)(2,1)} %fusion.1), calls=%async_computation.3 | async-start | bytes 2359296 | tf_op jit(solution)/shard_map/all_to_all | solution.py:98
Sparse Core Ops, SparseCore 0:
  11.2 113.6 all-gather.1
